TPU v7x, 256 devices: a whole 4x4x8 slice. The times are simulated.
256 devices in a mesh: space: 128 (over z, y, x), rep: 2 (over core).
Axes of the slice: x: 4, y: 4, z: 8, core: 2. Of those that a mesh axis runs over, the one named last changes fastest.
Arguments:
- features: bfloat16 [2, 256, 512, 128], P('rep', 'space'), may hold values from -6 to 6
- voxel_mask: int32 [2, 256, 512], P('rep', 'space'), may hold values from 0 to 1, as said below
- neighbours: int32 [2, 256, 27], P('rep', 'space'), may hold values from 0 to 34, as said below
- send_slots: int32 [2, 2048], P('rep', 'space'), may hold values from 0 to 2, as said below
- w_sub: bfloat16 [27, 128, 128], replicated, may hold values from -0.109375 to 0.109375
- w_down: bfloat16 [8, 128, 256], replicated, may hold values from -0.1875 to 0.1875
- cotangent: bfloat16 [2, 256, 64, 256], P('rep', 'space'), may hold values from -6 to 6
Outputs:
- coarse: bfloat16 [2, 256, 64, 256], P('rep', 'space')
- grad_feats: bfloat16 [2, 256, 512, 128], P('rep', 'space')
- grad_sub: float32 [27, 128, 128], replicated
- grad_down: float32 [8, 128, 256], replicated
Inputs may be any that keep to these rules, and one draw needn't show every extreme that they name: `voxel_mask`: 0 or 1. Each slab of a scan has 1 or 2 live slots, and these are the lowest-numbered ones; some slab of each scan has 2 live slots; all voxels of slots that are not live are 0. `neighbours`: each live slot holds one brick position (p1, p2) of its slab s, p = 4 p1 + p2, one brick per position; its brick neighbour at offset (a, b, c) lies at slab s + a, position (p1 + b, p2 + c). Entry: its slot if a = 0 and that position is live, 2 + p' if a = -1, 18 + p' if a = 1, where p' is the neighbour's position; 34 where the neighbour lies outside the map or is empty on the own slab, and for every offset of a slot that is not live. `send_slots`: entry p of slab s is the slot holding position p, or 2 where no live slot holds it.
All inputs are finite; a program needn't handle non-finite values.
Results may differ from a plain program's by a relative error of at most 0.015.
Values may be sent and summed in bfloat16 or wider, within the bound.
No kernel may reach another device: no remote copies, remote signals or barrier semaphores. Data moves between devices by JAX's collectives and lax.ppermute only.
A program may use at most 128 MiB of HBM per device.

v0:
```python
import jax
import numpy as np
import jax.numpy as jnp
from jax import lax
from jax.sharding import PartitionSpec as P


def from_behind(value, axis, steps):
    count = lax.axis_size(axis)
    leading, last = (max(0, -steps), min(count, count - steps))
    return lax.ppermute(value, axis, [(source, source + steps) for source in range(leading, last)])


HALVE = (None, (1, 4), (4, 16), (16, 1))
SPREAD = ((2, 8), (8, 32), (32, 64), (64, 2))


def joint_pairs(space_count, rep_count, masks):
    pairs = []
    for space in range(space_count):
        for rep in range(rep_count):
            if masks is None:
                target = space * rep_count + (rep ^ 1)
            else:
                target = (space ^ masks[rep]) * rep_count + rep
            pairs.append((space * rep_count + rep, target))
    return pairs


def step_bit(masks):
    rep = lax.axis_index("rep")
    if masks is None:
        return rep
    mask = jnp.where(rep == 0, masks[0], masks[1])
    return ((lax.axis_index("space") & mask) > 0).astype(jnp.int32)


def joint_psum(buf):
    axes = ("space", "rep")
    counts = (lax.axis_size("space"), lax.axis_size("rep"))
    for masks in HALVE:
        me = step_bit(masks)
        halves = buf.reshape(2, buf.shape[0] // 2, buf.shape[1])
        keep = lax.dynamic_index_in_dim(halves, me, 0, keepdims=False)
        send = lax.dynamic_index_in_dim(halves, 1 - me, 0, keepdims=False)
        buf = keep + lax.ppermute(send, axes, joint_pairs(*counts, masks))
    for masks in SPREAD:
        buf = buf + lax.ppermute(buf, axes, joint_pairs(*counts, masks))
    for masks in reversed(HALVE):
        me = step_bit(masks)
        other = lax.ppermute(buf, axes, joint_pairs(*counts, masks))
        buf = jnp.where(me == 0, jnp.concatenate([buf, other]), jnp.concatenate([other, buf]))
    return buf


def padding_maps():
    side = np.array([0] + [1] * 8 + [2])
    inner = (np.arange(10) - 1) % 8
    column = side[:, None, None] * 9 + side[None, :, None] * 3 + side[None, None, :]
    voxel = inner[:, None, None] * 64 + inner[None, :, None] * 8 + inner[None, None, :]
    return column, voxel


def halo_table(values, send_list):
    bricks, voxels, channels = values.shape
    cells = send_list.shape[0]
    slot_row = jnp.zeros((1, channels), values.dtype).at[0, :cells].set(send_list.astype(values.dtype))
    payload = jnp.concatenate([values.reshape(bricks * voxels, channels), slot_row], axis=0)
    from_lower = from_behind(payload, "space", 1)
    from_upper = from_behind(payload, "space", -1)
    table = jnp.concatenate(
        [
            values.reshape(bricks * voxels, channels),
            from_lower[: bricks * voxels],
            from_upper[: bricks * voxels],
            jnp.zeros((voxels, channels), values.dtype),
        ],
        axis=0,
    )
    lower_slots = from_lower[bricks * voxels, :cells].astype(jnp.int32)
    upper_slots = from_upper[bricks * voxels, :cells].astype(jnp.int32)
    return table, lower_slots, upper_slots


def brick_rows(link_rows, lower_slots, upper_slots, bricks):
    cells = lower_slots.shape[0]
    empty = 3 * bricks
    lower = jnp.take(lower_slots, jnp.clip(link_rows - bricks, 0, cells - 1), mode="clip")
    upper = jnp.take(upper_slots, jnp.clip(link_rows - bricks - cells, 0, cells - 1), mode="clip")
    lower = jnp.where(lower < bricks, bricks + lower, empty)
    upper = jnp.where(upper < bricks, 2 * bricks + upper, empty)
    from_upper = jnp.where(link_rows < bricks + 2 * cells, upper, empty)
    from_side = jnp.where(link_rows < bricks + cells, lower, from_upper)
    return jnp.where(link_rows < bricks, link_rows, from_side)


def pad_bricks(table, rows, voxels):
    column, voxel = padding_maps()
    index = jnp.take(rows, jnp.asarray(column.reshape(-1)), axis=1, mode="clip") * voxels
    index = index + jnp.asarray(voxel.reshape(1, -1))
    padded = jnp.take(table, index.reshape(-1), axis=0, mode="clip")
    return padded.reshape(rows.shape[0], 10, 10, 10, table.shape[-1])


DIMS = ("NDHWC", "DHWIO", "NDHWC")


def conv_forward(padded, w_sub):
    channels = w_sub.shape[1]
    kernel = w_sub.reshape(3, 3, 3, channels, w_sub.shape[2])
    out = lax.conv_general_dilated(
        padded, kernel, (1, 1, 1), "VALID", dimension_numbers=DIMS,
        preferred_element_type=jnp.float32,
    )
    return out.reshape(-1, w_sub.shape[2])


def conv_transpose(padded, w_sub):
    kernel = w_sub.reshape(3, 3, 3, w_sub.shape[1], w_sub.shape[2])[::-1, ::-1, ::-1]
    kernel = kernel.transpose(0, 1, 2, 4, 3)
    out = lax.conv_general_dilated(
        padded, kernel, (1, 1, 1), "VALID", dimension_numbers=DIMS,
        preferred_element_type=jnp.float32,
    )
    return out.reshape(-1, w_sub.shape[1])


def weight_grad(padded, grad_rows):
    bricks = padded.shape[0]
    channels = padded.shape[-1]
    grads = grad_rows.reshape(bricks, 8, 8, 8, grad_rows.shape[-1])
    numbers = lax.ConvDimensionNumbers(
        lhs_spec=(4, 0, 1, 2, 3), rhs_spec=(4, 0, 1, 2, 3), out_spec=(3, 4, 0, 1, 2)
    )
    out = lax.conv_general_dilated(
        padded, grads, (1, 1, 1), "VALID", dimension_numbers=numbers,
        preferred_element_type=jnp.float32,
    )
    return out.reshape(27, channels, grad_rows.shape[-1])


def to_columns(values):
    bricks = values.shape[0]
    channels = values.shape[-1]
    cube = values.reshape(bricks, 4, 2, 4, 2, 4, 2, channels)
    return cube.transpose(0, 1, 3, 5, 2, 4, 6, 7).reshape(bricks * 64, 8 * channels)


def from_columns(columns, bricks, channels):
    cube = columns.reshape(bricks, 4, 4, 4, 2, 2, 2, channels)
    return cube.transpose(0, 1, 4, 2, 5, 3, 6, 7).reshape(bricks, 512, channels)


def silu_slope(values):
    sigmoid_value = jax.nn.sigmoid(values)
    return sigmoid_value * (1.0 + values * (1.0 - sigmoid_value))


def body(features, voxel_mask, neighbours, send_slots, w_sub, w_down, cotangent):
    values = features[0]
    bricks, voxels, channels = values.shape
    out_channels = w_down.shape[2]
    link_rows = neighbours[0]
    send_list = send_slots[0]
    occupancy = voxel_mask[0].reshape(-1).astype(jnp.float32)
    masked = values * voxel_mask[0][..., None].astype(jnp.bfloat16)
    table_x, lower_slots, upper_slots = halo_table(masked, send_list)
    rows = brick_rows(link_rows, lower_slots, upper_slots, bricks)
    padded_x = pad_bricks(table_x, rows, voxels)
    pre_act = conv_forward(padded_x, w_sub) * occupancy[:, None]
    hidden = jax.nn.silu(pre_act).astype(jnp.bfloat16)
    columns = to_columns(hidden.reshape(bricks, voxels, channels))
    down_flat = w_down.reshape(-1, out_channels)
    coarse_mask = jnp.max(to_columns(occupancy.reshape(bricks, voxels, 1)), axis=1)
    coarse = (
        jnp.dot(columns, down_flat, preferred_element_type=jnp.float32) * coarse_mask[:, None]
    ).astype(jnp.bfloat16)
    grad_coarse = cotangent[0].reshape(-1, out_channels) * coarse_mask[:, None].astype(jnp.bfloat16)
    grad_cols = jnp.dot(grad_coarse, down_flat.T, preferred_element_type=jnp.float32).astype(
        jnp.bfloat16
    )
    grad_hidden = from_columns(grad_cols, bricks, channels).reshape(-1, channels)
    down_grad = lax.dot_general(
        columns, grad_coarse, (((0,), (0,)), ((), ())), preferred_element_type=jnp.float32
    )
    grad_pre = (grad_hidden.astype(jnp.float32) * silu_slope(pre_act) * occupancy[:, None]).astype(
        jnp.bfloat16
    )
    table_g, _, _ = halo_table(grad_pre.reshape(bricks, voxels, channels), send_list)
    sub_grad, table_g = lax.optimization_barrier((weight_grad(padded_x, grad_pre), table_g))
    padded_g = pad_bricks(table_g, rows, voxels)
    grad_in = (conv_transpose(padded_g, w_sub) * occupancy[:, None]).astype(jnp.bfloat16)
    inverse_count = 1.0 / (lax.axis_size("space") * lax.axis_size("rep"))
    lanes = 128
    flat = jnp.concatenate([sub_grad.reshape(-1, lanes), down_grad.reshape(-1, lanes)])
    flat = joint_psum(flat)
    split = sub_grad.size // lanes
    sub_total = flat[:split].reshape(sub_grad.shape)
    down_total = flat[split:].reshape(down_grad.shape)
    return (
        coarse.reshape(1, bricks, voxels // 8, out_channels),
        grad_in.reshape(1, bricks, voxels, channels),
        sub_total * inverse_count,
        (down_total * inverse_count).reshape(w_down.shape),
    )


def solution(mesh):
    in_specs = (
        P("rep", "space", None, None),
        P("rep", "space", None),
        P("rep", "space", None),
        P("rep", "space"),
        P(),
        P(),
        P("rep", "space", None, None),
    )
    out_specs = (P("rep", "space", None, None), P("rep", "space", None, None), P(), P())
    return jax.shard_map(body, mesh=mesh, in_specs=in_specs, out_specs=out_specs, check_vma=False)
```

profile of v0, /device:TPU:1, one launch (start us, length us, event | category | flops | bytes accessed | tf_op | source)
XLA Modules:
  0.0 200.3 jit_solution(11042373480520457492)
XLA Ops:
  5.9 5.3 %collective-permute-start = (bf16[1025,128]{1,0:T(8,128)(2,1)S(1)}, bf16[1025,128]{1,0:T(8,128)(2,1)}, u32[]{:S(2)}, u32[]{:S(2)}) collective-permute-start(bf16[1025,128]{1,0:T(8,128)(2,1)S(1)} %fusion.7), channel_id=1, source_target_pairs={{0,2},{2,4},{4,6},{6,8},{8,10},{10,12},{12,14},{14,16},{16,18},{18... | collective-permute-start | bytes 787208 | tf_op jit(solution)/shard_map/ppermute | solution.py:11
  19.6 2.9 %gather_fusion.2 = s32[1000,2]{1,0:T(8,128)S(1)} fusion(s32[2,27]{0,1:T(8,128)S(1)} %compare_select_fusion, s32[1024]{0:T(1024)S(1)} %pad_clamp_fusion.1), kind=kCustom, calls=%fused_computation.2 | custom fusion | bytes 20000 | tf_op jit(solution)/shard_map/jit(_take)/gather | solution.py:99
  25.0 5.7 %maximum_maximum_fusion = bf16[3584,128]{1,0:T(8,128)(2,1)S(1)} fusion(bf16[1024,128]{1,0:T(8,128)(2,1)S(1)} %slice.69, bf16[1024,128]{1,0:T(8,128)(2,1)S(1)} %slice.68, bf16[1024,128]{1,0:T(8,128)(2,1)S(1)} %bitcast_multiply_fusion.1, bf16[3584]{0:T(1024)(128)(2,1)S(1)} %pad.34.clone), kind=kLoop, calls=%fused_computation.16 | loop fusion | flops 3670016 | bytes 1711104 | tf_op jit(solution)/shard_map/concatenate | solution.py:71
  30.8 6.3 %gather_fusion.3 = bf16[2000,128]{1,0:T(8,128)(2,1)S(1)} fusion(bf16[3584,128]{1,0:T(8,128)(2,1)S(1)} %maximum_maximum_fusion, s32[2048]{0:T(1024)S(1)} %pad_clamp_fusion), kind=kCustom, calls=%fused_computation.3 | custom fusion | bytes 1032000 | tf_op jit(solution)/shard_map/jit(_take)/gather | solution.py:101
  37.3 3.1 %fusion.13 = f32[2,8,8,8,128]{4,0,3,2,1:T(2,128)S(1)} fusion(bf16[3,3,3,128,128]{4,3,2,1,0:T(8,128)(2,1)S(1)} %bitcast.71, bf16[2,10,10,10,128]{4,3,2,1,0:T(8,128)(2,1)S(1)} %reshape.312), kind=kOutput, calls=%fused_computation.46 | convolution fusion | flops 905969664 | bytes 1921024 | tf_op jit(solution)/shard_map/conv_general_dilated | solution.py:111
  43.1 4.7 %collective-permute-start.2 = (bf16[1025,128]{1,0:T(8,128)(2,1)}, bf16[1025,128]{1,0:T(8,128)(2,1)}, u32[]{:S(2)}, u32[]{:S(2)}) collective-permute-start(bf16[1025,128]{1,0:T(8,128)(2,1)} %fusion.8), channel_id=1, source_target_pairs={{0,2},{2,4},{4,6},{6,8},{8,10},{10,12},{12,14},{14,16},{16,18},{18... | collective-permute-start | bytes 787208 | tf_op jit(solution)/shard_map/ppermute | solution.py:11
  47.8 5.7 %fusion.9 = f32[3,3,3,128,128]{4,3,2,1,0:T(8,128)} fusion(bf16[2,8,8,8,128]{4,3,2,1,0:T(8,128)(2,1)S(1)} %get-tuple-element.29, bf16[2,10,10,10,128]{4,3,2,1,0:T(8,128)(2,1)S(1)} %reshape.312), kind=kOutput, calls=%fused_computation.40 | convolution fusion | flops 905969664 | bytes 2543616 | tf_op jit(solution)/shard_map/conv_general_dilated | solution.py:135
  56.8 5.7 %maximum_maximum_fusion.1 = bf16[3584,128]{1,0:T(8,128)(2,1)S(1)} fusion(bf16[1024,128]{1,0:T(8,128)(2,1)S(1)} %slice.73, bf16[1024,128]{1,0:T(8,128)(2,1)S(1)} %slice.72, bf16[1024,128]{1,0:T(8,128)(2,1)S(1)} %multiply_convert_fusion, bf16[3584]{0:T(1024)(128)(2,1)S(1)} %pad.34.clone), kind=kLoop, calls=%fused_computation.17 | loop fusion | flops 3670016 | bytes 1711104 | tf_op jit(solution)/shard_map/concatenate | solution.py:71
  64.4 3.8 %collective-permute-start.4 = (f32[2752,128]{1,0:T(8,128)S(1)}, f32[2752,128]{1,0:T(8,128)}, u32[]{:S(2)}, u32[]{:S(2)}) collective-permute-start(f32[2752,128]{1,0:T(8,128)S(1)} %dynamic-slice_bitcast_fusion), channel_id=1, source_target_pairs={{0,1},{1,0},{2,3},{3,2},{4,5},{5,4},{6,7},{7,6},{8,9},{9,8},{10,11... | collective-permute-start | bytes 4227080 | tf_op jit(solution)/shard_map/ppermute | solution.py:46
  68.2 2.9 %collective-permute-done.4 = f32[2752,128]{1,0:T(8,128)} collective-permute-done((f32[2752,128]{1,0:T(8,128)S(1)}, f32[2752,128]{1,0:T(8,128)}, u32[]{:S(2)}, u32[]{:S(2)}) %collective-permute-start.4) | collective-permute-done | bytes 1409056 | tf_op jit(solution)/shard_map/ppermute | solution.py:46
  71.1 1.9 bitcast_add_fusion
  74.0 3.8 %collective-permute-start.5 = (f32[1376,128]{1,0:T(8,128)}, f32[1376,128]{1,0:T(8,128)}, u32[]{:S(2)}, u32[]{:S(2)}) collective-permute-start(f32[1376,128]{1,0:T(8,128)} %dynamic-slice_bitcast_fusion.1), channel_id=1, source_target_pairs={{0,2},{1,9},{2,0},{3,11},{4,6},{5,13},{6,4},{7,15},{8,10},{9,1},{1... | collective-permute-start | bytes 2113544 | tf_op jit(solution)/shard_map/ppermute | solution.py:46
  77.8 8.8 %collective-permute-done.5 = f32[1376,128]{1,0:T(8,128)} collective-permute-done((f32[1376,128]{1,0:T(8,128)}, f32[1376,128]{1,0:T(8,128)}, u32[]{:S(2)}, u32[]{:S(2)}) %collective-permute-start.5) | collective-permute-done | bytes 704544 | tf_op jit(solution)/shard_map/ppermute | solution.py:46
  86.6 2.0 %bitcast_add_fusion.1 = f32[1376,128]{1,0:T(8,128)} fusion(f32[1376,128]{1,0:T(8,128)} %collective-permute-done.5, f32[2,1376,128]{2,1,0:T(8,128)S(1)} %bitcast.76, s32[]{:T(128)S(6)} %select_n.104), kind=kLoop, calls=%fused_computation.19 | loop fusion | flops 176128 | bytes 2113540 | tf_op jit(solution)/shard_map/add | solution.py:46
  89.6 7.6 %collective-permute-start.6 = (f32[688,128]{1,0:T(8,128)S(1)}, f32[688,128]{1,0:T(8,128)S(1)}, u32[]{:S(2)}, u32[]{:S(2)}) collective-permute-start(f32[688,128]{1,0:T(8,128)S(1)} %dynamic-slice_bitcast_fusion.2), channel_id=1, source_target_pairs={{0,8},{1,33},{2,10},{3,35},{4,12},{5,37},{6,14},{7,39},{8,0},{9,41... | collective-permute-start | bytes 1056776 | tf_op jit(solution)/shard_map/ppermute | solution.py:46
  97.3 4.7 %collective-permute-done.6 = f32[688,128]{1,0:T(8,128)S(1)} collective-permute-done((f32[688,128]{1,0:T(8,128)S(1)}, f32[688,128]{1,0:T(8,128)S(1)}, u32[]{:S(2)}, u32[]{:S(2)}) %collective-permute-start.6) | collective-permute-done | bytes 352288 | tf_op jit(solution)/shard_map/ppermute | solution.py:46
  103.2 4.3 %collective-permute-done.7 = f32[344,128]{1,0:T(8,128)S(1)} collective-permute-done((f32[344,128]{1,0:T(8,128)S(1)}, f32[344,128]{1,0:T(8,128)S(1)}, u32[]{:S(2)}, u32[]{:S(2)}) %collective-permute-start.7) | collective-permute-done | bytes 176160 | tf_op jit(solution)/shard_map/ppermute | solution.py:46
  107.6 5.8 %collective-permute-done.8 = f32[344,128]{1,0:T(8,128)S(1)} collective-permute-done((f32[344,128]{1,0:T(8,128)S(1)}, f32[344,128]{1,0:T(8,128)S(1)}, u32[]{:S(2)}, u32[]{:S(2)}) %collective-permute-start.8) | collective-permute-done | bytes 176160 | tf_op jit(solution)/shard_map/ppermute | solution.py:48
  113.4 3.6 %collective-permute-start.9 = (f32[344,128]{1,0:T(8,128)S(1)}, f32[344,128]{1,0:T(8,128)S(1)}, u32[]{:S(2)}, u32[]{:S(2)}) collective-permute-start(f32[344,128]{1,0:T(8,128)S(1)} %add.176), channel_id=1, source_target_pairs={{0,16},{1,65},{2,18},{3,67},{4,20},{5,69},{6,22},{7,71},{8,24},{9,... | collective-permute-start | bytes 528392 | tf_op jit(solution)/shard_map/ppermute | solution.py:48
  117.0 4.7 %collective-permute-done.9 = f32[344,128]{1,0:T(8,128)S(1)} collective-permute-done((f32[344,128]{1,0:T(8,128)S(1)}, f32[344,128]{1,0:T(8,128)S(1)}, u32[]{:S(2)}, u32[]{:S(2)}) %collective-permute-start.9) | collective-permute-done | bytes 176160 | tf_op jit(solution)/shard_map/ppermute | solution.py:48
  121.7 8.4 %collective-permute-start.10 = (f32[344,128]{1,0:T(8,128)S(1)}, f32[344,128]{1,0:T(8,128)S(1)}, u32[]{:S(2)}, u32[]{:S(2)}) collective-permute-start(f32[344,128]{1,0:T(8,128)S(1)} %add.177), channel_id=1, source_target_pairs={{0,64},{1,129},{2,66},{3,131},{4,68},{5,133},{6,70},{7,135},{8,72}... | collective-permute-start | bytes 528392 | tf_op jit(solution)/shard_map/ppermute | solution.py:48
  130.1 3.4 %collective-permute-done.10 = f32[344,128]{1,0:T(8,128)S(1)} collective-permute-done((f32[344,128]{1,0:T(8,128)S(1)}, f32[344,128]{1,0:T(8,128)S(1)}, u32[]{:S(2)}, u32[]{:S(2)}) %collective-permute-start.10) | collective-permute-done | bytes 176160 | tf_op jit(solution)/shard_map/ppermute | solution.py:48
  134.1 5.3 %collective-permute-done.11 = f32[344,128]{1,0:T(8,128)S(1)} collective-permute-done((f32[344,128]{1,0:T(8,128)S(1)}, f32[344,128]{1,0:T(8,128)S(1)}, u32[]{:S(2)}, u32[]{:S(2)}) %collective-permute-start.11) | collective-permute-done | bytes 176160 | tf_op jit(solution)/shard_map/ppermute | solution.py:48
  139.5 4.3 %collective-permute-done.12 = f32[344,128]{1,0:T(8,128)S(1)} collective-permute-done((f32[344,128]{1,0:T(8,128)S(1)}, f32[344,128]{1,0:T(8,128)S(1)}, u32[]{:S(2)}, u32[]{:S(2)}) %collective-permute-start.12) | collective-permute-done | bytes 176160 | tf_op jit(solution)/shard_map/ppermute | solution.py:51
  144.6 6.4 %collective-permute-done.13 = f32[688,128]{1,0:T(8,128)S(1)} collective-permute-done((f32[688,128]{1,0:T(8,128)S(1)}, f32[688,128]{1,0:T(8,128)S(1)}, u32[]{:S(2)}, u32[]{:S(2)}) %collective-permute-start.13) | collective-permute-done | bytes 352288 | tf_op jit(solution)/shard_map/ppermute | solution.py:51
  152.0 14.1 %collective-permute-done.14 = f32[1376,128]{1,0:T(8,128)} collective-permute-done((f32[1376,128]{1,0:T(8,128)}, f32[1376,128]{1,0:T(8,128)}, u32[]{:S(2)}, u32[]{:S(2)}) %collective-permute-start.14) | collective-permute-done | bytes 704544 | tf_op jit(solution)/shard_map/ppermute | solution.py:51
  166.0 1.9 maximum_select_fusion.1
  167.9 12.2 %collective-permute-start.15 = (f32[2752,128]{1,0:T(8,128)S(1)}, f32[2752,128]{1,0:T(8,128)}, u32[]{:S(2)}, u32[]{:S(2)}) collective-permute-start(f32[2752,128]{1,0:T(8,128)S(1)} %maximum_select_fusion.1), channel_id=1, source_target_pairs={{0,1},{1,0},{2,3},{3,2},{4,5},{5,4},{6,7},{7,6},{8,9},{9,8},{10,11... | collective-permute-start | bytes 4227080 | tf_op jit(solution)/shard_map/ppermute | solution.py:51
  180.2 1.9 fusion.1
  182.1 8.0 %gather_fusion.4 = bf16[2000,128]{1,0:T(8,128)(2,1)} fusion(bf16[3584,128]{1,0:T(8,128)(2,1)S(1)} %maximum_maximum_fusion.1, s32[2048]{0:T(1024)S(1)} %pad_clamp_fusion), kind=kCustom, calls=%fused_computation.4 | custom fusion | bytes 1032000 | tf_op jit(solution)/shard_map/jit(_take)/gather | solution.py:101
  191.4 3.1 %fusion.5 = f32[2,8,8,8,128]{4,0,3,2,1:T(2,128)S(1)} fusion(bf16[3,3,3,128,128]{4,3,2,1,0:T(8,128)(2,1)S(1)} %bitcast.72, bf16[2,10,10,10,128]{4,3,2,1,0:T(8,128)(2,1)S(1)} %reshape.320), kind=kOutput, calls=%fused_computation.32 | convolution fusion | flops 905969664 | bytes 1921024 | tf_op jit(solution)/shard_map/conv_general_dilated | solution.py:121
  195.4 2.2 %maximum_select_fusion = f32[5504,128]{1,0:T(8,128)S(1)} fusion(f32[2752,128]{1,0:T(8,128)} %collective-permute-done.15, f32[2752,128]{1,0:T(8,128)S(1)} %maximum_select_fusion.1, pred[]{:T(512)S(6)} %eq.8), kind=kLoop, calls=%fused_computation.6 | loop fusion | flops 2113536 | bytes 5636097 | tf_op jit(solution)/shard_map/jit(_where)/select_n | solution.py:52
  (102 shorter events, 34.3 us)
Async XLA Ops:
  0.6 36.6 %copy-start = (bf16[27,128,128]{2,1,0:T(8,128)(2,1)S(1)}, bf16[27,128,128]{2,1,0:T(8,128)(2,1)}, u32[]{:S(2)}) copy-start(bf16[27,128,128]{2,1,0:T(8,128)(2,1)} %param.19) | copy-start | bytes 2654212
  0.6 14.7 %copy-start.6 = (s32[1,2,27]{2,1,0:T(2,128)S(1)}, s32[1,2,27]{2,1,0:T(2,128)}, u32[]{:S(2)}) copy-start(s32[1,2,27]{2,1,0:T(2,128)} %param.17) | copy-start | bytes 652
  0.7 12.8 %copy-start.2 = (bf16[8,128,256]{2,1,0:T(8,128)(2,1)S(1)}, bf16[8,128,256]{2,1,0:T(8,128)(2,1)}, u32[]{:S(2)}) copy-start(bf16[8,128,256]{2,1,0:T(8,128)(2,1)} %param.20) | copy-start | bytes 1572868
  4.6 13.4 %collective-permute-start.1 = (bf16[1025,128]{1,0:T(8,128)(2,1)S(1)}, bf16[1025,128]{1,0:T(8,128)(2,1)}, u32[]{:S(2)}, u32[]{:S(2)}) collective-permute-start(bf16[1025,128]{1,0:T(8,128)(2,1)S(1)} %fusion.7), channel_id=1, source_target_pairs={{2,0},{4,2},{6,4},{8,6},{10,8},{12,10},{14,12},{16,14},{18,16},{20... | collective-permute-start | bytes 787208 | tf_op jit(solution)/shard_map/ppermute | solution.py:11
  5.9 10.5 %collective-permute-start = (bf16[1025,128]{1,0:T(8,128)(2,1)S(1)}, bf16[1025,128]{1,0:T(8,128)(2,1)}, u32[]{:S(2)}, u32[]{:S(2)}) collective-permute-start(bf16[1025,128]{1,0:T(8,128)(2,1)S(1)} %fusion.7), channel_id=1, source_target_pairs={{0,2},{2,4},{4,6},{6,8},{8,10},{10,12},{12,14},{14,16},{16,18},{18... | collective-permute-start | bytes 787208 | tf_op jit(solution)/shard_map/ppermute | solution.py:11
  13.4 2.9 %copy-start.7 = (s32[1000]{0:T(1024)S(1)}, s32[1000]{0:T(1024)}, u32[]{:S(2)}) copy-start(s32[1000]{0:T(1024)} %constant.133) | copy-start | bytes 12004
  16.0 6.5 %copy-start.5 = (s32[1000]{0:T(1024)S(1)}, s32[1000]{0:T(1024)}, u32[]{:S(2)}) copy-start(s32[1000]{0:T(1024)} %constant.132) | copy-start | bytes 12004
  41.8 12.9 %collective-permute-start.3 = (bf16[1025,128]{1,0:T(8,128)(2,1)}, bf16[1025,128]{1,0:T(8,128)(2,1)}, u32[]{:S(2)}, u32[]{:S(2)}) collective-permute-start(bf16[1025,128]{1,0:T(8,128)(2,1)} %fusion.8), channel_id=1, source_target_pairs={{2,0},{4,2},{6,4},{8,6},{10,8},{12,10},{14,12},{16,14},{18,16},{20... | collective-permute-start | bytes 787208 | tf_op jit(solution)/shard_map/ppermute | solution.py:11
  43.1 12.7 %collective-permute-start.2 = (bf16[1025,128]{1,0:T(8,128)(2,1)}, bf16[1025,128]{1,0:T(8,128)(2,1)}, u32[]{:S(2)}, u32[]{:S(2)}) collective-permute-start(bf16[1025,128]{1,0:T(8,128)(2,1)} %fusion.8), channel_id=1, source_target_pairs={{0,2},{2,4},{4,6},{6,8},{8,10},{10,12},{12,14},{14,16},{16,18},{18... | collective-permute-start | bytes 787208 | tf_op jit(solution)/shard_map/ppermute | solution.py:11
  47.8 5.7 %copy-start.4 = (f32[2,4,2,4,2,4,2]{5,6,4,3,2,1,0:T(2,128)S(1)}, f32[2,4,2,4,2,4,2]{5,6,4,3,2,1,0:T(2,128)}, u32[]{:S(2)}) copy-start(f32[2,4,2,4,2,4,2]{5,6,4,3,2,1,0:T(2,128)} %copy.72) | copy-start | bytes 12292
  54.7 7.9 %copy-start.3 = (f32[3,3,3,128,128]{4,3,2,1,0:T(8,128)S(1)}, f32[3,3,3,128,128]{4,3,2,1,0:T(8,128)}, u32[]{:S(2)}) copy-start(f32[3,3,3,128,128]{4,3,2,1,0:T(8,128)} %fusion.9) | copy-start | bytes 5308420
  62.7 1.6 copy-start.1
  64.4 6.8 %collective-permute-start.4 = (f32[2752,128]{1,0:T(8,128)S(1)}, f32[2752,128]{1,0:T(8,128)}, u32[]{:S(2)}, u32[]{:S(2)}) collective-permute-start(f32[2752,128]{1,0:T(8,128)S(1)} %dynamic-slice_bitcast_fusion), channel_id=1, source_target_pairs={{0,1},{1,0},{2,3},{3,2},{4,5},{5,4},{6,7},{7,6},{8,9},{9,8},{10,11... | collective-permute-start | bytes 4227080 | tf_op jit(solution)/shard_map/ppermute | solution.py:46
  74.0 12.6 %collective-permute-start.5 = (f32[1376,128]{1,0:T(8,128)}, f32[1376,128]{1,0:T(8,128)}, u32[]{:S(2)}, u32[]{:S(2)}) collective-permute-start(f32[1376,128]{1,0:T(8,128)} %dynamic-slice_bitcast_fusion.1), channel_id=1, source_target_pairs={{0,2},{1,9},{2,0},{3,11},{4,6},{5,13},{6,4},{7,15},{8,10},{9,1},{1... | collective-permute-start | bytes 2113544 | tf_op jit(solution)/shard_map/ppermute | solution.py:46
  89.6 12.4 %collective-permute-start.6 = (f32[688,128]{1,0:T(8,128)S(1)}, f32[688,128]{1,0:T(8,128)S(1)}, u32[]{:S(2)}, u32[]{:S(2)}) collective-permute-start(f32[688,128]{1,0:T(8,128)S(1)} %dynamic-slice_bitcast_fusion.2), channel_id=1, source_target_pairs={{0,8},{1,33},{2,10},{3,35},{4,12},{5,37},{6,14},{7,39},{8,0},{9,41... | collective-permute-start | bytes 1056776 | tf_op jit(solution)/shard_map/ppermute | solution.py:46
  103.1 4.4 %collective-permute-start.7 = (f32[344,128]{1,0:T(8,128)S(1)}, f32[344,128]{1,0:T(8,128)S(1)}, u32[]{:S(2)}, u32[]{:S(2)}) collective-permute-start(f32[344,128]{1,0:T(8,128)S(1)} %dynamic-slice_bitcast_fusion.3), channel_id=1, source_target_pairs={{0,32},{1,3},{2,34},{3,1},{4,36},{5,7},{6,38},{7,5},{8,40},{9,11},... | collective-permute-start | bytes 528392 | tf_op jit(solution)/shard_map/ppermute | solution.py:46
  107.5 5.9 %collective-permute-start.8 = (f32[344,128]{1,0:T(8,128)S(1)}, f32[344,128]{1,0:T(8,128)S(1)}, u32[]{:S(2)}, u32[]{:S(2)}) collective-permute-start(f32[344,128]{1,0:T(8,128)S(1)} %bitcast_add_fusion.3), channel_id=1, source_target_pairs={{0,4},{1,17},{2,6},{3,19},{4,0},{5,21},{6,2},{7,23},{8,12},{9,25},... | collective-permute-start | bytes 528392 | tf_op jit(solution)/shard_map/ppermute | solution.py:48
  113.4 8.3 %collective-permute-start.9 = (f32[344,128]{1,0:T(8,128)S(1)}, f32[344,128]{1,0:T(8,128)S(1)}, u32[]{:S(2)}, u32[]{:S(2)}) collective-permute-start(f32[344,128]{1,0:T(8,128)S(1)} %add.176), channel_id=1, source_target_pairs={{0,16},{1,65},{2,18},{3,67},{4,20},{5,69},{6,22},{7,71},{8,24},{9,... | collective-permute-start | bytes 528392 | tf_op jit(solution)/shard_map/ppermute | solution.py:48
  121.7 11.7 %collective-permute-start.10 = (f32[344,128]{1,0:T(8,128)S(1)}, f32[344,128]{1,0:T(8,128)S(1)}, u32[]{:S(2)}, u32[]{:S(2)}) collective-permute-start(f32[344,128]{1,0:T(8,128)S(1)} %add.177), channel_id=1, source_target_pairs={{0,64},{1,129},{2,66},{3,131},{4,68},{5,133},{6,70},{7,135},{8,72}... | collective-permute-start | bytes 528392 | tf_op jit(solution)/shard_map/ppermute | solution.py:48
  133.5 5.9 %collective-permute-start.11 = (f32[344,128]{1,0:T(8,128)S(1)}, f32[344,128]{1,0:T(8,128)S(1)}, u32[]{:S(2)}, u32[]{:S(2)}) collective-permute-start(f32[344,128]{1,0:T(8,128)S(1)} %add.178), channel_id=1, source_target_pairs={{0,128},{1,5},{2,130},{3,7},{4,132},{5,1},{6,134},{7,3},{8,136},{9... | collective-permute-start | bytes 528392 | tf_op jit(solution)/shard_map/ppermute | solution.py:48
  139.4 4.4 %collective-permute-start.12 = (f32[344,128]{1,0:T(8,128)S(1)}, f32[344,128]{1,0:T(8,128)S(1)}, u32[]{:S(2)}, u32[]{:S(2)}) collective-permute-start(f32[344,128]{1,0:T(8,128)S(1)} %add.179), channel_id=1, source_target_pairs={{0,32},{1,3},{2,34},{3,1},{4,36},{5,7},{6,38},{7,5},{8,40},{9,11},... | collective-permute-start | bytes 528392 | tf_op jit(solution)/shard_map/ppermute | solution.py:51
  143.8 7.2 %collective-permute-start.13 = (f32[688,128]{1,0:T(8,128)S(1)}, f32[688,128]{1,0:T(8,128)S(1)}, u32[]{:S(2)}, u32[]{:S(2)}) collective-permute-start(f32[688,128]{1,0:T(8,128)S(1)} %maximum_select_fusion.3), channel_id=1, source_target_pairs={{0,8},{1,33},{2,10},{3,35},{4,12},{5,37},{6,14},{7,39},{8,0},{9,41... | collective-permute-start | bytes 1056776 | tf_op jit(solution)/shard_map/ppermute | solution.py:51
  152.0 14.1 %collective-permute-start.14 = (f32[1376,128]{1,0:T(8,128)}, f32[1376,128]{1,0:T(8,128)}, u32[]{:S(2)}, u32[]{:S(2)}) collective-permute-start(f32[1376,128]{1,0:T(8,128)} %maximum_select_fusion.2), channel_id=1, source_target_pairs={{0,2},{1,9},{2,0},{3,11},{4,6},{5,13},{6,4},{7,15},{8,10},{9,1},{1... | collective-permute-start | bytes 2113544 | tf_op jit(solution)/shard_map/ppermute | solution.py:51
  167.9 27.5 %collective-permute-start.15 = (f32[2752,128]{1,0:T(8,128)S(1)}, f32[2752,128]{1,0:T(8,128)}, u32[]{:S(2)}, u32[]{:S(2)}) collective-permute-start(f32[2752,128]{1,0:T(8,128)S(1)} %maximum_select_fusion.1), channel_id=1, source_target_pairs={{0,1},{1,0},{2,3},{3,2},{4,5},{5,4},{6,7},{7,6},{8,9},{9,8},{10,11... | collective-permute-start | bytes 4227080 | tf_op jit(solution)/shard_map/ppermute | solution.py:51
where the time goes:
time: 201 us; the launch traced here: 200 us
  waiting for transfers between devices  64.7 us (32%)
  starting transfers between devices  53.6 us (27%)
  local copies, waits for them, and re-layouts  33.2 us (17%)
  other arithmetic  33 us (16%)
  matrix products  14.5 us (7%)
    ppermute x4, waiting for transfers between devices, joint_psum(): other = lax.ppermute(buf, axes, joint_pairs(*counts, masks))  24.8 us
    ppermute x4, waiting for transfers between devices, joint_psum(): buf = keep + lax.ppermute(send, axes, joint_pairs(*counts, masks))  20.8 us
    ppermute x4, waiting for transfers between devices, joint_psum(): buf = buf + lax.ppermute(buf, axes, joint_pairs(*counts, masks))  19.2 us
    ppermute x4, starting transfers between devices, joint_psum(): buf = keep + lax.ppermute(send, axes, joint_pairs(*counts, masks))  15.4 us
    gather x2, local copies, waits for them, and re-layouts, pad_bricks(): padded = jnp.take(table, index.reshape(-1), axis=0, mode='clip')  14.4 us
    ppermute x4, starting transfers between devices, joint_psum(): other = lax.ppermute(buf, axes, joint_pairs(*counts, masks))  13 us
    ppermute x4, starting transfers between devices, joint_psum(): buf = buf + lax.ppermute(buf, axes, joint_pairs(*counts, masks))  12.7 us
    ppermute x4, starting transfers between devices, from_behind(): lax.ppermute(value, axis, [(source, source + steps) for source in range(l...  12.5 us
  transfers between devices with their start and end apart: 16, of which 11 were waited for; matrix products, arithmetic and copies ran while one was open for 15% of the time, Pallas kernels for 0%

commit v1 on v0

--- a/solution.py
+++ b/solution.py
@@ -38,19 +38,23 @@
 def joint_psum(buf):
     axes = ("space", "rep")
     counts = (lax.axis_size("space"), lax.axis_size("rep"))
+    wide = buf.dtype
     for masks in HALVE:
         me = step_bit(masks)
         halves = buf.reshape(2, buf.shape[0] // 2, buf.shape[1])
         keep = lax.dynamic_index_in_dim(halves, me, 0, keepdims=False)
-        send = lax.dynamic_index_in_dim(halves, 1 - me, 0, keepdims=False)
-        buf = keep + lax.ppermute(send, axes, joint_pairs(*counts, masks))
+        send = lax.dynamic_index_in_dim(halves, 1 - me, 0, keepdims=False).astype(jnp.bfloat16)
+        buf = keep + lax.ppermute(send, axes, joint_pairs(*counts, masks)).astype(wide)
     for masks in SPREAD:
-        buf = buf + lax.ppermute(buf, axes, joint_pairs(*counts, masks))
+        narrow = buf.astype(jnp.bfloat16)
+        other = lax.ppermute(narrow, axes, joint_pairs(*counts, masks))
+        buf = narrow.astype(wide) + other.astype(wide)
+    buf = buf.astype(jnp.bfloat16)
     for masks in reversed(HALVE):
         me = step_bit(masks)
         other = lax.ppermute(buf, axes, joint_pairs(*counts, masks))
         buf = jnp.where(me == 0, jnp.concatenate([buf, other]), jnp.concatenate([other, buf]))
-    return buf
+    return buf.astype(wide)
 
 
 def padding_maps():

time: 201 us -> 160 us (0.80)
  waiting for transfers between devices: 64.7 us -> 35.4 us
  other arithmetic: 33 us -> 28.3 us
  starting transfers between devices: 53.6 us -> 50.4 us
  local copies, waits for them, and re-layouts: 33.2 us -> 30.3 us
    ppermute x4, waiting for transfers between devices: 24.8 us -> 8.69 us  [joint_psum(): other = lax.ppermute(buf, axes, joint_pairs(*counts, masks))]
    ppermute x8, waiting for transfers between devices: 39.9 us -> 26.7 us  [the longest x4 13.6 us: joint_psum(): other = lax.ppermute(narrow, axes, joint_pairs(*counts, masks))]
    select_n x4 -> x3, other arithmetic: 5.01 us -> 0.34 us  [joint_psum(): jnp.where(me == 0, jnp.concatenate([buf, other]), jnp.concatenate([other,...]
    ppermute x4, starting transfers between devices: 13 us -> 9.48 us  [joint_psum(): other = lax.ppermute(buf, axes, joint_pairs(*counts, masks))]
    squeeze x4 -> x0, local copies, waits for them, and re-layouts: 2.03 us -> none  [joint_psum(): send = lax.dynamic_index_in_dim(halves, 1 - me, 0, keepdims=False)]
    add x8 -> x3, other arithmetic: 5.09 us -> 4.6 us  [joint_psum(): keep + lax.ppermute(send, axes, joint_pairs(*counts, masks)).astype(wide)]
  transfers between devices with their start and end apart: 16 -> 16, of which waited for: 11 -> 10; matrix products, arithmetic and copies ran while one was open for 15% -> 16% of each run, Pallas kernels for 0% -> 0%
where the time goes in v1:
time: 160 us; the launch traced here: 159 us
  starting transfers between devices  50.4 us (32%)
  waiting for transfers between devices  35.4 us (22%)
  local copies, waits for them, and re-layouts  30.3 us (19%)
  other arithmetic  28.3 us (18%)
  matrix products  13.5 us (8%)
    ppermute x4, starting transfers between devices, joint_psum(): lax.ppermute(send, axes, joint_pairs(*counts, masks)).astype(wide)  15.4 us
    ppermute x4, waiting for transfers between devices, joint_psum(): other = lax.ppermute(narrow, axes, joint_pairs(*counts, masks))  13.6 us
    ppermute x4, waiting for transfers between devices, joint_psum(): lax.ppermute(send, axes, joint_pairs(*counts, masks)).astype(wide)  13.2 us
    ppermute x4, starting transfers between devices, joint_psum(): other = lax.ppermute(narrow, axes, joint_pairs(*counts, masks))  13.1 us
    gather x2, local copies, waits for them, and re-layouts, pad_bricks(): padded = jnp.take(table, index.reshape(-1), axis=0, mode='clip')  12.7 us
    ppermute x4, starting transfers between devices, from_behind(): lax.ppermute(value, axis, [(source, source + steps) for source in range(l...  12.5 us
    concatenate x2, other arithmetic, halo_table(): jnp.concatenate([values.reshape(bricks * voxels, channels), from_lower[:b...  11.5 us
    ppermute x4, starting transfers between devices, joint_psum(): other = lax.ppermute(buf, axes, joint_pairs(*counts, masks))  9.48 us
  transfers between devices with their start and end apart: 16, of which 10 were waited for; matrix products, arithmetic and copies ran while one was open for 16% of the time, Pallas kernels for 0%

profile of v1, /device:TPU:1, one launch (start us, length us, event | category | flops | bytes accessed | tf_op | source)
XLA Modules:
  0.0 159.2 jit_solution(13052409370751134144)
XLA Ops:
  2.1 1.3 broadcast_select_fusion
  5.9 5.3 %collective-permute-start = (bf16[1025,128]{1,0:T(8,128)(2,1)S(1)}, bf16[1025,128]{1,0:T(8,128)(2,1)}, u32[]{:S(2)}, u32[]{:S(2)}) collective-permute-start(bf16[1025,128]{1,0:T(8,128)(2,1)S(1)} %fusion.10), channel_id=1, source_target_pairs={{0,2},{2,4},{4,6},{6,8},{8,10},{10,12},{12,14},{14,16},{16,18},{18... | collective-permute-start | bytes 787208 | tf_op jit(solution)/shard_map/ppermute | solution.py:11
  13.8 1.5 copy.72
  19.6 2.9 %gather_fusion.2 = s32[1000,2]{1,0:T(8,128)S(1)} fusion(s32[2,27]{0,1:T(8,128)S(1)} %compare_select_fusion, s32[1024]{0:T(1024)S(1)} %pad_clamp_fusion.1), kind=kCustom, calls=%fused_computation.2 | custom fusion | bytes 20000 | tf_op jit(solution)/shard_map/jit(_take)/gather | solution.py:103
  25.0 5.7 %maximum_maximum_fusion = bf16[3584,128]{1,0:T(8,128)(2,1)S(1)} fusion(bf16[1024,128]{1,0:T(8,128)(2,1)S(1)} %slice.69, bf16[1024,128]{1,0:T(8,128)(2,1)S(1)} %slice.68, bf16[1024,128]{1,0:T(8,128)(2,1)S(1)} %bitcast_multiply_fusion.1, bf16[3584]{0:T(1024)(128)(2,1)S(1)} %pad.34.clone), kind=kLoop, calls=%fused_computation.16 | loop fusion | flops 3670016 | bytes 1711104 | tf_op jit(solution)/shard_map/concatenate | solution.py:75
  30.8 6.3 %gather_fusion.3 = bf16[2000,128]{1,0:T(8,128)(2,1)S(1)} fusion(bf16[3584,128]{1,0:T(8,128)(2,1)S(1)} %maximum_maximum_fusion, s32[2048]{0:T(1024)S(1)} %pad_clamp_fusion), kind=kCustom, calls=%fused_computation.3 | custom fusion | bytes 1032000 | tf_op jit(solution)/shard_map/jit(_take)/gather | solution.py:105
  37.3 3.1 %fusion.18 = f32[2,8,8,8,128]{4,0,3,2,1:T(2,128)S(1)} fusion(bf16[3,3,3,128,128]{4,3,2,1,0:T(8,128)(2,1)S(1)} %bitcast.73, bf16[2,10,10,10,128]{4,3,2,1,0:T(8,128)(2,1)S(1)} %reshape.316), kind=kOutput, calls=%fused_computation.55 | convolution fusion | flops 905969664 | bytes 1921024 | tf_op jit(solution)/shard_map/conv_general_dilated | solution.py:115
  43.1 4.7 %collective-permute-start.2 = (bf16[1025,128]{1,0:T(8,128)(2,1)}, bf16[1025,128]{1,0:T(8,128)(2,1)}, u32[]{:S(2)}, u32[]{:S(2)}) collective-permute-start(bf16[1025,128]{1,0:T(8,128)(2,1)} %fusion.11), channel_id=1, source_target_pairs={{0,2},{2,4},{4,6},{6,8},{8,10},{10,12},{12,14},{14,16},{16,18},{18... | collective-permute-start | bytes 787208 | tf_op jit(solution)/shard_map/ppermute | solution.py:11
  47.8 5.7 %fusion.12 = f32[3,3,3,128,128]{4,3,2,1,0:T(8,128)} fusion(bf16[2,8,8,8,128]{4,3,2,1,0:T(8,128)(2,1)S(1)} %get-tuple-element.29, bf16[2,10,10,10,128]{4,3,2,1,0:T(8,128)(2,1)S(1)} %reshape.316), kind=kOutput, calls=%fused_computation.42 | convolution fusion | flops 905969664 | bytes 2543616 | tf_op jit(solution)/shard_map/conv_general_dilated | solution.py:139
  56.8 5.7 %maximum_maximum_fusion.1 = bf16[3584,128]{1,0:T(8,128)(2,1)S(1)} fusion(bf16[1024,128]{1,0:T(8,128)(2,1)S(1)} %slice.73, bf16[1024,128]{1,0:T(8,128)(2,1)S(1)} %slice.72, bf16[1024,128]{1,0:T(8,128)(2,1)S(1)} %multiply_convert_fusion, bf16[3584]{0:T(1024)(128)(2,1)S(1)} %pad.34.clone), kind=kLoop, calls=%fused_computation.17 | loop fusion | flops 3670016 | bytes 1711104 | tf_op jit(solution)/shard_map/concatenate | solution.py:75
  62.7 1.5 copy-done.1
  64.4 3.8 %collective-permute-start.4 = (bf16[2752,128]{1,0:T(8,128)(2,1)S(1)}, bf16[2752,128]{1,0:T(8,128)(2,1)}, u32[]{:S(2)}, u32[]{:S(2)}) collective-permute-start(bf16[2752,128]{1,0:T(8,128)(2,1)S(1)} %fusion.3), channel_id=1, source_target_pairs={{0,1},{1,0},{2,3},{3,2},{4,5},{5,4},{6,7},{7,6},{8,9},{9,8},{10,11... | collective-permute-start | bytes 2113544 | tf_op jit(solution)/shard_map/ppermute | solution.py:47
  68.2 1.9 %collective-permute-done.4 = bf16[2752,128]{1,0:T(8,128)(2,1)} collective-permute-done((bf16[2752,128]{1,0:T(8,128)(2,1)S(1)}, bf16[2752,128]{1,0:T(8,128)(2,1)}, u32[]{:S(2)}, u32[]{:S(2)}) %collective-permute-start.4) | collective-permute-done | bytes 704544 | tf_op jit(solution)/shard_map/ppermute | solution.py:47
  70.1 1.7 %bitcast_add_fusion = f32[2752,128]{1,0:T(8,128)S(1)} fusion(bf16[2752,128]{1,0:T(8,128)(2,1)} %collective-permute-done.4, f32[2,2752,128]{2,1,0:T(8,128)} %bitcast.76, s32[]{:T(128)S(6)} %select_n.102), kind=kLoop, calls=%fused_computation.9 | loop fusion | flops 704512 | bytes 3522564 | tf_op jit(solution)/shard_map/add | solution.py:47
  72.6 3.8 %collective-permute-start.5 = (bf16[1376,128]{1,0:T(8,128)(2,1)}, bf16[1376,128]{1,0:T(8,128)(2,1)}, u32[]{:S(2)}, u32[]{:S(2)}) collective-permute-start(bf16[1376,128]{1,0:T(8,128)(2,1)} %fusion.9), channel_id=1, source_target_pairs={{0,2},{1,9},{2,0},{3,11},{4,6},{5,13},{6,4},{7,15},{8,10},{9,1},{1... | collective-permute-start | bytes 1056776 | tf_op jit(solution)/shard_map/ppermute | solution.py:47
  76.4 5.0 %collective-permute-done.5 = bf16[1376,128]{1,0:T(8,128)(2,1)} collective-permute-done((bf16[1376,128]{1,0:T(8,128)(2,1)}, bf16[1376,128]{1,0:T(8,128)(2,1)}, u32[]{:S(2)}, u32[]{:S(2)}) %collective-permute-start.5) | collective-permute-done | bytes 352288 | tf_op jit(solution)/shard_map/ppermute | solution.py:47
  81.4 1.9 %bitcast_add_fusion.1 = f32[1376,128]{1,0:T(8,128)} fusion(bf16[1376,128]{1,0:T(8,128)(2,1)} %collective-permute-done.5, f32[2,1376,128]{2,1,0:T(8,128)S(1)} %bitcast.80, s32[]{:T(128)S(6)} %select_n.104), kind=kLoop, calls=%fused_computation.20 | loop fusion | flops 352256 | bytes 1761284 | tf_op jit(solution)/shard_map/add | solution.py:47
  84.4 7.6 %collective-permute-start.6 = (bf16[688,128]{1,0:T(8,128)(2,1)S(1)}, bf16[688,128]{1,0:T(8,128)(2,1)S(1)}, u32[]{:S(2)}, u32[]{:S(2)}) collective-permute-start(bf16[688,128]{1,0:T(8,128)(2,1)S(1)} %fusion.15), channel_id=1, source_target_pairs={{0,8},{1,33},{2,10},{3,35},{4,12},{5,37},{6,14},{7,39},{8,0},{9,41... | collective-permute-start | bytes 528392 | tf_op jit(solution)/shard_map/ppermute | solution.py:47
  92.0 2.8 %collective-permute-done.6 = bf16[688,128]{1,0:T(8,128)(2,1)S(1)} collective-permute-done((bf16[688,128]{1,0:T(8,128)(2,1)S(1)}, bf16[688,128]{1,0:T(8,128)(2,1)S(1)}, u32[]{:S(2)}, u32[]{:S(2)}) %collective-permute-start.6) | collective-permute-done | bytes 176160 | tf_op jit(solution)/shard_map/ppermute | solution.py:47
  96.0 3.3 %collective-permute-done.7 = bf16[344,128]{1,0:T(8,128)(2,1)S(1)} collective-permute-done((bf16[344,128]{1,0:T(8,128)(2,1)S(1)}, bf16[344,128]{1,0:T(8,128)(2,1)S(1)}, u32[]{:S(2)}, u32[]{:S(2)}) %collective-permute-start.7) | collective-permute-done | bytes 88096 | tf_op jit(solution)/shard_map/ppermute | solution.py:47
  99.4 4.8 %collective-permute-done.8 = bf16[344,128]{1,0:T(8,128)(2,1)S(1)} collective-permute-done((bf16[344,128]{1,0:T(8,128)(2,1)S(1)}, bf16[344,128]{1,0:T(8,128)(2,1)S(1)}, u32[]{:S(2)}, u32[]{:S(2)}) %collective-permute-start.8) | collective-permute-done | bytes 88096 | tf_op jit(solution)/shard_map/ppermute | solution.py:50
  104.3 3.6 %collective-permute-start.9 = (bf16[344,128]{1,0:T(8,128)(2,1)S(1)}, bf16[344,128]{1,0:T(8,128)(2,1)S(1)}, u32[]{:S(2)}, u32[]{:S(2)}) collective-permute-start(bf16[344,128]{1,0:T(8,128)(2,1)S(1)} %add_convert_fusion.3), channel_id=1, source_target_pairs={{0,16},{1,65},{2,18},{3,67},{4,20},{5,69},{6,22},{7,71},{8,24},{9,... | collective-permute-start | bytes 264200 | tf_op jit(solution)/shard_map/ppermute | solution.py:50
  107.9 1.9 %collective-permute-done.9 = bf16[344,128]{1,0:T(8,128)(2,1)S(1)} collective-permute-done((bf16[344,128]{1,0:T(8,128)(2,1)S(1)}, bf16[344,128]{1,0:T(8,128)(2,1)S(1)}, u32[]{:S(2)}, u32[]{:S(2)}) %collective-permute-start.9) | collective-permute-done | bytes 88096 | tf_op jit(solution)/shard_map/ppermute | solution.py:50
  109.8 9.3 %collective-permute-start.10 = (bf16[344,128]{1,0:T(8,128)(2,1)S(1)}, bf16[344,128]{1,0:T(8,128)(2,1)S(1)}, u32[]{:S(2)}, u32[]{:S(2)}) collective-permute-start(bf16[344,128]{1,0:T(8,128)(2,1)S(1)} %add_convert_fusion.2), channel_id=1, source_target_pairs={{0,64},{1,129},{2,66},{3,131},{4,68},{5,133},{6,70},{7,135},{8,72}... | collective-permute-start | bytes 264200 | tf_op jit(solution)/shard_map/ppermute | solution.py:50
  119.1 2.0 %collective-permute-done.10 = bf16[344,128]{1,0:T(8,128)(2,1)S(1)} collective-permute-done((bf16[344,128]{1,0:T(8,128)(2,1)S(1)}, bf16[344,128]{1,0:T(8,128)(2,1)S(1)}, u32[]{:S(2)}, u32[]{:S(2)}) %collective-permute-start.10) | collective-permute-done | bytes 88096 | tf_op jit(solution)/shard_map/ppermute | solution.py:50
  121.2 4.8 %collective-permute-done.11 = bf16[344,128]{1,0:T(8,128)(2,1)S(1)} collective-permute-done((bf16[344,128]{1,0:T(8,128)(2,1)S(1)}, bf16[344,128]{1,0:T(8,128)(2,1)S(1)}, u32[]{:S(2)}, u32[]{:S(2)}) %collective-permute-start.11) | collective-permute-done | bytes 88096 | tf_op jit(solution)/shard_map/ppermute | solution.py:50
  126.2 3.3 %collective-permute-done.12 = bf16[344,128]{1,0:T(8,128)(2,1)S(1)} collective-permute-done((bf16[344,128]{1,0:T(8,128)(2,1)S(1)}, bf16[344,128]{1,0:T(8,128)(2,1)S(1)}, u32[]{:S(2)}, u32[]{:S(2)}) %collective-permute-start.12) | collective-permute-done | bytes 88096 | tf_op jit(solution)/shard_map/ppermute | solution.py:55
  129.7 5.3 %collective-permute-done.13 = bf16[688,128]{1,0:T(8,128)(2,1)S(1)} collective-permute-done((bf16[688,128]{1,0:T(8,128)(2,1)S(1)}, bf16[688,128]{1,0:T(8,128)(2,1)S(1)}, u32[]{:S(2)}, u32[]{:S(2)}) %collective-permute-start.13) | collective-permute-done | bytes 176160 | tf_op jit(solution)/shard_map/ppermute | solution.py:55
  136.3 6.3 %gather_fusion.4 = bf16[2000,128]{1,0:T(8,128)(2,1)S(1)} fusion(bf16[3584,128]{1,0:T(8,128)(2,1)S(1)} %maximum_maximum_fusion.1, s32[2048]{0:T(1024)S(1)} %pad_clamp_fusion), kind=kCustom, calls=%fused_computation.4 | custom fusion | bytes 1032000 | tf_op jit(solution)/shard_map/jit(_take)/gather | solution.py:105
  143.0 9.2 %collective-permute-start.15 = (bf16[2752,128]{1,0:T(8,128)(2,1)S(1)}, bf16[2752,128]{1,0:T(8,128)(2,1)S(1)}, u32[]{:S(2)}, u32[]{:S(2)}) collective-permute-start(bf16[2752,128]{1,0:T(8,128)(2,1)S(1)} %maximum_select_fusion.1), channel_id=1, source_target_pairs={{0,1},{1,0},{2,3},{3,2},{4,5},{5,4},{6,7},{7,6},{8,9},{9,8},{10,11... | collective-permute-start | bytes 2113544 | tf_op jit(solution)/shard_map/ppermute | solution.py:55
  152.2 3.1 %fusion.7 = f32[2,8,8,8,128]{4,0,3,2,1:T(2,128)S(1)} fusion(bf16[3,3,3,128,128]{4,3,2,1,0:T(8,128)(2,1)S(1)} %bitcast.74, bf16[2,10,10,10,128]{4,3,2,1,0:T(8,128)(2,1)S(1)} %reshape.324), kind=kOutput, calls=%fused_computation.33 | convolution fusion | flops 905969664 | bytes 1921024 | tf_op jit(solution)/shard_map/conv_general_dilated | solution.py:125
  156.5 1.3 slice_multiply_fusion
  (104 shorter events, 26.9 us)
Async XLA Ops:
  0.6 36.6 %copy-start = (bf16[27,128,128]{2,1,0:T(8,128)(2,1)S(1)}, bf16[27,128,128]{2,1,0:T(8,128)(2,1)}, u32[]{:S(2)}) copy-start(bf16[27,128,128]{2,1,0:T(8,128)(2,1)} %param.19) | copy-start | bytes 2654212
  0.6 14.7 %copy-start.7 = (s32[1,2,27]{2,1,0:T(2,128)S(1)}, s32[1,2,27]{2,1,0:T(2,128)}, u32[]{:S(2)}) copy-start(s32[1,2,27]{2,1,0:T(2,128)} %param.17) | copy-start | bytes 652
  0.7 12.8 %copy-start.2 = (bf16[8,128,256]{2,1,0:T(8,128)(2,1)S(1)}, bf16[8,128,256]{2,1,0:T(8,128)(2,1)}, u32[]{:S(2)}) copy-start(bf16[8,128,256]{2,1,0:T(8,128)(2,1)} %param.20) | copy-start | bytes 1572868
  4.6 13.4 %collective-permute-start.1 = (bf16[1025,128]{1,0:T(8,128)(2,1)S(1)}, bf16[1025,128]{1,0:T(8,128)(2,1)}, u32[]{:S(2)}, u32[]{:S(2)}) collective-permute-start(bf16[1025,128]{1,0:T(8,128)(2,1)S(1)} %fusion.10), channel_id=1, source_target_pairs={{2,0},{4,2},{6,4},{8,6},{10,8},{12,10},{14,12},{16,14},{18,16},{20... | collective-permute-start | bytes 787208 | tf_op jit(solution)/shard_map/ppermute | solution.py:11
  5.9 10.5 %collective-permute-start = (bf16[1025,128]{1,0:T(8,128)(2,1)S(1)}, bf16[1025,128]{1,0:T(8,128)(2,1)}, u32[]{:S(2)}, u32[]{:S(2)}) collective-permute-start(bf16[1025,128]{1,0:T(8,128)(2,1)S(1)} %fusion.10), channel_id=1, source_target_pairs={{0,2},{2,4},{4,6},{6,8},{8,10},{10,12},{12,14},{14,16},{16,18},{18... | collective-permute-start | bytes 787208 | tf_op jit(solution)/shard_map/ppermute | solution.py:11
  13.4 2.9 %copy-start.8 = (s32[1000]{0:T(1024)S(1)}, s32[1000]{0:T(1024)}, u32[]{:S(2)}) copy-start(s32[1000]{0:T(1024)} %constant.133) | copy-start | bytes 12004
  16.0 6.6 %copy-start.6 = (s32[1000]{0:T(1024)S(1)}, s32[1000]{0:T(1024)}, u32[]{:S(2)}) copy-start(s32[1000]{0:T(1024)} %constant.132) | copy-start | bytes 12004
  41.8 12.9 %collective-permute-start.3 = (bf16[1025,128]{1,0:T(8,128)(2,1)}, bf16[1025,128]{1,0:T(8,128)(2,1)}, u32[]{:S(2)}, u32[]{:S(2)}) collective-permute-start(bf16[1025,128]{1,0:T(8,128)(2,1)} %fusion.11), channel_id=1, source_target_pairs={{2,0},{4,2},{6,4},{8,6},{10,8},{12,10},{14,12},{16,14},{18,16},{20... | collective-permute-start | bytes 787208 | tf_op jit(solution)/shard_map/ppermute | solution.py:11
  43.1 12.7 %collective-permute-start.2 = (bf16[1025,128]{1,0:T(8,128)(2,1)}, bf16[1025,128]{1,0:T(8,128)(2,1)}, u32[]{:S(2)}, u32[]{:S(2)}) collective-permute-start(bf16[1025,128]{1,0:T(8,128)(2,1)} %fusion.11), channel_id=1, source_target_pairs={{0,2},{2,4},{4,6},{6,8},{8,10},{10,12},{12,14},{14,16},{16,18},{18... | collective-permute-start | bytes 787208 | tf_op jit(solution)/shard_map/ppermute | solution.py:11
  47.8 5.7 %copy-start.5 = (f32[2,4,2,4,2,4,2]{5,6,4,3,2,1,0:T(2,128)S(1)}, f32[2,4,2,4,2,4,2]{5,6,4,3,2,1,0:T(2,128)}, u32[]{:S(2)}) copy-start(f32[2,4,2,4,2,4,2]{5,6,4,3,2,1,0:T(2,128)} %copy.72) | copy-start | bytes 12292
  54.7 7.9 %copy-start.4 = (f32[3,3,3,128,128]{4,3,2,1,0:T(8,128)S(1)}, f32[3,3,3,128,128]{4,3,2,1,0:T(8,128)}, u32[]{:S(2)}) copy-start(f32[3,3,3,128,128]{4,3,2,1,0:T(8,128)} %fusion.12) | copy-start | bytes 5308420
  62.7 1.6 copy-start.1
  64.4 5.8 %collective-permute-start.4 = (bf16[2752,128]{1,0:T(8,128)(2,1)S(1)}, bf16[2752,128]{1,0:T(8,128)(2,1)}, u32[]{:S(2)}, u32[]{:S(2)}) collective-permute-start(bf16[2752,128]{1,0:T(8,128)(2,1)S(1)} %fusion.3), channel_id=1, source_target_pairs={{0,1},{1,0},{2,3},{3,2},{4,5},{5,4},{6,7},{7,6},{8,9},{9,8},{10,11... | collective-permute-start | bytes 2113544 | tf_op jit(solution)/shard_map/ppermute | solution.py:47
  72.6 8.9 %collective-permute-start.5 = (bf16[1376,128]{1,0:T(8,128)(2,1)}, bf16[1376,128]{1,0:T(8,128)(2,1)}, u32[]{:S(2)}, u32[]{:S(2)}) collective-permute-start(bf16[1376,128]{1,0:T(8,128)(2,1)} %fusion.9), channel_id=1, source_target_pairs={{0,2},{1,9},{2,0},{3,11},{4,6},{5,13},{6,4},{7,15},{8,10},{9,1},{1... | collective-permute-start | bytes 1056776 | tf_op jit(solution)/shard_map/ppermute | solution.py:47
  84.3 51.0 %copy-start.3 = (bf16[8,128,256]{2,1,0:T(8,128)(2,1)S(1)}, bf16[8,128,256]{2,1,0:T(8,128)(2,1)}, u32[]{:S(2)}) copy-start(bf16[8,128,256]{2,1,0:T(8,128)(2,1)} %param.20) | copy-start | bytes 1572868
  84.4 10.5 %collective-permute-start.6 = (bf16[688,128]{1,0:T(8,128)(2,1)S(1)}, bf16[688,128]{1,0:T(8,128)(2,1)S(1)}, u32[]{:S(2)}, u32[]{:S(2)}) collective-permute-start(bf16[688,128]{1,0:T(8,128)(2,1)S(1)} %fusion.15), channel_id=1, source_target_pairs={{0,8},{1,33},{2,10},{3,35},{4,12},{5,37},{6,14},{7,39},{8,0},{9,41... | collective-permute-start | bytes 528392 | tf_op jit(solution)/shard_map/ppermute | solution.py:47
  95.9 3.4 %collective-permute-start.7 = (bf16[344,128]{1,0:T(8,128)(2,1)S(1)}, bf16[344,128]{1,0:T(8,128)(2,1)S(1)}, u32[]{:S(2)}, u32[]{:S(2)}) collective-permute-start(bf16[344,128]{1,0:T(8,128)(2,1)S(1)} %fusion.20), channel_id=1, source_target_pairs={{0,32},{1,3},{2,34},{3,1},{4,36},{5,7},{6,38},{7,5},{8,40},{9,11},... | collective-permute-start | bytes 264200 | tf_op jit(solution)/shard_map/ppermute | solution.py:47
  99.3 4.9 %collective-permute-start.8 = (bf16[344,128]{1,0:T(8,128)(2,1)S(1)}, bf16[344,128]{1,0:T(8,128)(2,1)S(1)}, u32[]{:S(2)}, u32[]{:S(2)}) collective-permute-start(bf16[344,128]{1,0:T(8,128)(2,1)S(1)} %fusion.16), channel_id=1, source_target_pairs={{0,4},{1,17},{2,6},{3,19},{4,0},{5,21},{6,2},{7,23},{8,12},{9,25},... | collective-permute-start | bytes 264200 | tf_op jit(solution)/shard_map/ppermute | solution.py:50
  104.3 5.5 %collective-permute-start.9 = (bf16[344,128]{1,0:T(8,128)(2,1)S(1)}, bf16[344,128]{1,0:T(8,128)(2,1)S(1)}, u32[]{:S(2)}, u32[]{:S(2)}) collective-permute-start(bf16[344,128]{1,0:T(8,128)(2,1)S(1)} %add_convert_fusion.3), channel_id=1, source_target_pairs={{0,16},{1,65},{2,18},{3,67},{4,20},{5,69},{6,22},{7,71},{8,24},{9,... | collective-permute-start | bytes 264200 | tf_op jit(solution)/shard_map/ppermute | solution.py:50
  109.8 11.3 %collective-permute-start.10 = (bf16[344,128]{1,0:T(8,128)(2,1)S(1)}, bf16[344,128]{1,0:T(8,128)(2,1)S(1)}, u32[]{:S(2)}, u32[]{:S(2)}) collective-permute-start(bf16[344,128]{1,0:T(8,128)(2,1)S(1)} %add_convert_fusion.2), channel_id=1, source_target_pairs={{0,64},{1,129},{2,66},{3,131},{4,68},{5,133},{6,70},{7,135},{8,72}... | collective-permute-start | bytes 264200 | tf_op jit(solution)/shard_map/ppermute | solution.py:50
  121.1 4.9 %collective-permute-start.11 = (bf16[344,128]{1,0:T(8,128)(2,1)S(1)}, bf16[344,128]{1,0:T(8,128)(2,1)S(1)}, u32[]{:S(2)}, u32[]{:S(2)}) collective-permute-start(bf16[344,128]{1,0:T(8,128)(2,1)S(1)} %add_convert_fusion.1), channel_id=1, source_target_pairs={{0,128},{1,5},{2,130},{3,7},{4,132},{5,1},{6,134},{7,3},{8,136},{9... | collective-permute-start | bytes 264200 | tf_op jit(solution)/shard_map/ppermute | solution.py:50
  126.1 3.4 %collective-permute-start.12 = (bf16[344,128]{1,0:T(8,128)(2,1)S(1)}, bf16[344,128]{1,0:T(8,128)(2,1)S(1)}, u32[]{:S(2)}, u32[]{:S(2)}) collective-permute-start(bf16[344,128]{1,0:T(8,128)(2,1)S(1)} %add_convert_fusion), channel_id=1, source_target_pairs={{0,32},{1,3},{2,34},{3,1},{4,36},{5,7},{6,38},{7,5},{8,40},{9,11},... | collective-permute-start | bytes 264200 | tf_op jit(solution)/shard_map/ppermute | solution.py:55
  129.6 5.4 %collective-permute-start.13 = (bf16[688,128]{1,0:T(8,128)(2,1)S(1)}, bf16[688,128]{1,0:T(8,128)(2,1)S(1)}, u32[]{:S(2)}, u32[]{:S(2)}) collective-permute-start(bf16[688,128]{1,0:T(8,128)(2,1)S(1)} %maximum_select_fusion.3), channel_id=1, source_target_pairs={{0,8},{1,33},{2,10},{3,35},{4,12},{5,37},{6,14},{7,39},{8,0},{9,41... | collective-permute-start | bytes 528392 | tf_op jit(solution)/shard_map/ppermute | solution.py:55
  135.2 7.6 %collective-permute-start.14 = (bf16[1376,128]{1,0:T(8,128)(2,1)S(1)}, bf16[1376,128]{1,0:T(8,128)(2,1)S(1)}, u32[]{:S(2)}, u32[]{:S(2)}) collective-permute-start(bf16[1376,128]{1,0:T(8,128)(2,1)S(1)} %maximum_select_fusion.2), channel_id=1, source_target_pairs={{0,2},{1,9},{2,0},{3,11},{4,6},{5,13},{6,4},{7,15},{8,10},{9,1},{1... | collective-permute-start | bytes 1056776 | tf_op jit(solution)/shard_map/ppermute | solution.py:55
  143.0 13.3 %collective-permute-start.15 = (bf16[2752,128]{1,0:T(8,128)(2,1)S(1)}, bf16[2752,128]{1,0:T(8,128)(2,1)S(1)}, u32[]{:S(2)}, u32[]{:S(2)}) collective-permute-start(bf16[2752,128]{1,0:T(8,128)(2,1)S(1)} %maximum_select_fusion.1), channel_id=1, source_target_pairs={{0,1},{1,0},{2,3},{3,2},{4,5},{5,4},{6,7},{7,6},{8,9},{9,8},{10,11... | collective-permute-start | bytes 2113544 | tf_op jit(solution)/shard_map/ppermute | solution.py:55

commit v2 on v1

--- a/solution.py
+++ b/solution.py
@@ -65,13 +65,17 @@
     return column, voxel
 
 
-def halo_table(values, send_list):
+def halo_exchange(values, send_list):
     bricks, voxels, channels = values.shape
     cells = send_list.shape[0]
     slot_row = jnp.zeros((1, channels), values.dtype).at[0, :cells].set(send_list.astype(values.dtype))
     payload = jnp.concatenate([values.reshape(bricks * voxels, channels), slot_row], axis=0)
-    from_lower = from_behind(payload, "space", 1)
-    from_upper = from_behind(payload, "space", -1)
+    return from_behind(payload, "space", 1), from_behind(payload, "space", -1)
+
+
+def halo_table(values, received, cells):
+    bricks, voxels, channels = values.shape
+    from_lower, from_upper = received
     table = jnp.concatenate(
         [
             values.reshape(bricks * voxels, channels),
@@ -168,7 +172,8 @@
     send_list = send_slots[0]
     occupancy = voxel_mask[0].reshape(-1).astype(jnp.float32)
     masked = values * voxel_mask[0][..., None].astype(jnp.bfloat16)
-    table_x, lower_slots, upper_slots = halo_table(masked, send_list)
+    cells = send_list.shape[0]
+    table_x, lower_slots, upper_slots = halo_table(masked, halo_exchange(masked, send_list), cells)
     rows = brick_rows(link_rows, lower_slots, upper_slots, bricks)
     padded_x = pad_bricks(table_x, rows, voxels)
     pre_act = conv_forward(padded_x, w_sub) * occupancy[:, None]
@@ -190,8 +195,10 @@
     grad_pre = (grad_hidden.astype(jnp.float32) * silu_slope(pre_act) * occupancy[:, None]).astype(
         jnp.bfloat16
     )
-    table_g, _, _ = halo_table(grad_pre.reshape(bricks, voxels, channels), send_list)
-    sub_grad, table_g = lax.optimization_barrier((weight_grad(padded_x, grad_pre), table_g))
+    grad_pre_bricks = grad_pre.reshape(bricks, voxels, channels)
+    received_g = halo_exchange(grad_pre_bricks, send_list)
+    sub_grad, received_g = lax.optimization_barrier((weight_grad(padded_x, grad_pre), received_g))
+    table_g, _, _ = halo_table(grad_pre_bricks, received_g, cells)
     padded_g = pad_bricks(table_g, rows, voxels)
     grad_in = (conv_transpose(padded_g, w_sub) * occupancy[:, None]).astype(jnp.bfloat16)
     inverse_count = 1.0 / (lax.axis_size("space") * lax.axis_size("rep"))

time: 160 us -> 158 us (0.988)
  starting transfers between devices: 50.4 us -> 53.5 us
  waiting for transfers between devices: 35.4 us -> 32.3 us
    ppermute x4, starting transfers between devices: 15.4 us -> 19.3 us  [joint_psum(): lax.ppermute(send, axes, joint_pairs(*counts, masks)).astype(wide)]
    ppermute x4, waiting for transfers between devices: 8.69 us -> 5.63 us  [joint_psum(): other = lax.ppermute(buf, axes, joint_pairs(*counts, masks))]
    add x3, other arithmetic: 4.6 us -> 2.54 us  [joint_psum(): keep + lax.ppermute(send, axes, joint_pairs(*counts, masks)).astype(wide)]
    convert_element_type x4, local copies, waits for them, and re-layouts: 1.87 us -> 0.17 us  [joint_psum(): lax.dynamic_index_in_dim(halves, 1 - me, 0, keepdims=False)]
  transfers between devices with their start and end apart: 16 -> 16, of which waited for: 10 -> 10; matrix products, arithmetic and copies ran while one was open for 16% -> 21% of each run, Pallas kernels for 0% -> 0%
where the time goes in v2:
time: 158 us
  starting transfers between devices  53.5 us (34%)
  waiting for transfers between devices  32.3 us (20%)
  local copies, waits for them, and re-layouts  28.9 us (18%)
  other arithmetic  28.2 us (18%)
  matrix products  13.5 us (9%)
    ppermute x4, starting transfers between devices, joint_psum(): lax.ppermute(send, axes, joint_pairs(*counts, masks)).astype(wide)  19.3 us
    ppermute x4, waiting for transfers between devices, joint_psum(): other = lax.ppermute(narrow, axes, joint_pairs(*counts, masks))  13.8 us
    ppermute x4, starting transfers between devices, joint_psum(): other = lax.ppermute(narrow, axes, joint_pairs(*counts, masks))  13 us
    ppermute x4, waiting for transfers between devices, joint_psum(): lax.ppermute(send, axes, joint_pairs(*counts, masks)).astype(wide)  12.8 us
    gather x2, local copies, waits for them, and re-layouts, pad_bricks(): padded = jnp.take(table, index.reshape(-1), axis=0, mode='clip')  12.7 us
    concatenate x2, other arithmetic, halo_table(): jnp.concatenate([values.reshape(bricks * voxels, channels), from_lower[:b...  11.5 us
    ppermute x4, starting transfers between devices, from_behind(): lax.ppermute(value, axis, [(source, source + steps) for source in range(l...  11.4 us
    ppermute x4, starting transfers between devices, joint_psum(): other = lax.ppermute(buf, axes, joint_pairs(*counts, masks))  9.81 us
  transfers between devices with their start and end apart: 16, of which 10 were waited for; matrix products, arithmetic and copies ran while one was open for 21% of the time, Pallas kernels for 0%

profile of v2, /device:TPU:1, one launch (start us, length us, event | category | flops | bytes accessed | tf_op | source)
XLA Modules:
  0.0 157.5 jit_solution(13385496179231241313)
XLA Ops:
  1.3 1.4 convert_bitcast_fusion.1
  6.5 5.3 %collective-permute-start = (bf16[1025,128]{1,0:T(8,128)(2,1)S(1)}, bf16[1025,128]{1,0:T(8,128)(2,1)}, u32[]{:S(2)}, u32[]{:S(2)}) collective-permute-start(bf16[1025,128]{1,0:T(8,128)(2,1)S(1)} %fusion.10), channel_id=1, source_target_pairs={{0,2},{2,4},{4,6},{6,8},{8,10},{10,12},{12,14},{14,16},{16,18},{18... | collective-permute-start | bytes 787208 | tf_op jit(solution)/shard_map/ppermute | solution.py:11
  20.5 2.9 %gather_fusion.2 = s32[1000,2]{1,0:T(8,128)S(1)} fusion(s32[2,27]{0,1:T(8,128)S(1)} %compare_select_fusion, s32[1024]{0:T(1024)S(1)} %pad_clamp_fusion.1), kind=kCustom, calls=%fused_computation.2 | custom fusion | bytes 20000 | tf_op jit(solution)/shard_map/jit(_take)/gather | solution.py:107
  25.9 5.7 %maximum_maximum_fusion = bf16[3584,128]{1,0:T(8,128)(2,1)S(1)} fusion(bf16[1024,128]{1,0:T(8,128)(2,1)S(1)} %slice.69, bf16[1024,128]{1,0:T(8,128)(2,1)S(1)} %slice.68, bf16[1024,128]{1,0:T(8,128)(2,1)S(1)} %bitcast_multiply_fusion.1, bf16[3584]{0:T(1024)(128)(2,1)S(1)} %pad.34.clone), kind=kLoop, calls=%fused_computation.16 | loop fusion | flops 3670016 | bytes 1711104 | tf_op jit(solution)/shard_map/concatenate | solution.py:79
  31.6 6.3 %gather_fusion.3 = bf16[2000,128]{1,0:T(8,128)(2,1)S(1)} fusion(bf16[3584,128]{1,0:T(8,128)(2,1)S(1)} %maximum_maximum_fusion, s32[2048]{0:T(1024)S(1)} %pad_clamp_fusion), kind=kCustom, calls=%fused_computation.3 | custom fusion | bytes 1032000 | tf_op jit(solution)/shard_map/jit(_take)/gather | solution.py:109
  38.1 3.1 %fusion.18 = f32[2,8,8,8,128]{4,0,3,2,1:T(2,128)S(1)} fusion(bf16[3,3,3,128,128]{4,3,2,1,0:T(8,128)(2,1)S(1)} %bitcast.73, bf16[2,10,10,10,128]{4,3,2,1,0:T(8,128)(2,1)S(1)} %reshape.316), kind=kOutput, calls=%fused_computation.55 | convolution fusion | flops 905969664 | bytes 1921024 | tf_op jit(solution)/shard_map/conv_general_dilated | solution.py:119
  42.7 3.4 %collective-permute-start.2 = (bf16[1025,128]{1,0:T(8,128)(2,1)}, bf16[1025,128]{1,0:T(8,128)(2,1)}, u32[]{:S(2)}, u32[]{:S(2)}) collective-permute-start(bf16[1025,128]{1,0:T(8,128)(2,1)} %fusion.11), channel_id=1, source_target_pairs={{0,2},{2,4},{4,6},{6,8},{8,10},{10,12},{12,14},{14,16},{16,18},{18... | collective-permute-start | bytes 787208 | tf_op jit(solution)/shard_map/ppermute | solution.py:11
  46.0 1.5 collective-permute-start.3
  47.5 5.7 %fusion.12 = f32[3,3,3,128,128]{4,3,2,1,0:T(8,128)} fusion(bf16[2,8,8,8,128]{4,3,2,1,0:T(8,128)(2,1)S(1)} %get-tuple-element.31, bf16[2,10,10,10,128]{4,3,2,1,0:T(8,128)(2,1)S(1)} %reshape.316), kind=kOutput, calls=%fused_computation.42 | convolution fusion | flops 905969664 | bytes 2543616 | tf_op jit(solution)/shard_map/conv_general_dilated | solution.py:143
  54.5 1.7 %pad_maximum_fusion = f32[5504,128]{1,0:T(8,128)S(1)} fusion(f32[2048,128]{1,0:T(8,128)S(1)} %reshape.327, f32[3456,128]{1,0:T(8,128)} %bitcast.86), kind=kLoop, calls=%fused_computation.5 | loop fusion | flops 704512 | bytes 5636096 | tf_op jit(solution)/shard_map/concatenate | solution.py:206
  56.1 1.5 copy-done.1
  57.7 3.0 %collective-permute-start.4 = (bf16[2752,128]{1,0:T(8,128)(2,1)S(1)}, bf16[2752,128]{1,0:T(8,128)(2,1)S(1)}, u32[]{:S(2)}, u32[]{:S(2)}) collective-permute-start(bf16[2752,128]{1,0:T(8,128)(2,1)S(1)} %fusion.3), channel_id=1, source_target_pairs={{0,1},{1,0},{2,3},{3,2},{4,5},{5,4},{6,7},{7,6},{8,9},{9,8},{10,11... | collective-permute-start | bytes 2113544 | tf_op jit(solution)/shard_map/ppermute | solution.py:47
  60.7 1.8 %collective-permute-done.4 = bf16[2752,128]{1,0:T(8,128)(2,1)S(1)} collective-permute-done((bf16[2752,128]{1,0:T(8,128)(2,1)S(1)}, bf16[2752,128]{1,0:T(8,128)(2,1)S(1)}, u32[]{:S(2)}, u32[]{:S(2)}) %collective-permute-start.4) | collective-permute-done | bytes 704544 | tf_op jit(solution)/shard_map/ppermute | solution.py:47
  62.5 1.5 bitcast_add_fusion
  64.1 7.7 %collective-permute-start.5 = (bf16[1376,128]{1,0:T(8,128)(2,1)S(1)}, bf16[1376,128]{1,0:T(8,128)(2,1)}, u32[]{:S(2)}, u32[]{:S(2)}) collective-permute-start(bf16[1376,128]{1,0:T(8,128)(2,1)S(1)} %fusion.9), channel_id=1, source_target_pairs={{0,2},{1,9},{2,0},{3,11},{4,6},{5,13},{6,4},{7,15},{8,10},{9,1},{1... | collective-permute-start | bytes 1056776 | tf_op jit(solution)/shard_map/ppermute | solution.py:47
  71.8 4.8 %collective-permute-done.5 = bf16[1376,128]{1,0:T(8,128)(2,1)} collective-permute-done((bf16[1376,128]{1,0:T(8,128)(2,1)S(1)}, bf16[1376,128]{1,0:T(8,128)(2,1)}, u32[]{:S(2)}, u32[]{:S(2)}) %collective-permute-start.5) | collective-permute-done | bytes 352288 | tf_op jit(solution)/shard_map/ppermute | solution.py:47
  77.7 8.5 %collective-permute-start.6 = (bf16[688,128]{1,0:T(8,128)(2,1)S(1)}, bf16[688,128]{1,0:T(8,128)(2,1)S(1)}, u32[]{:S(2)}, u32[]{:S(2)}) collective-permute-start(bf16[688,128]{1,0:T(8,128)(2,1)S(1)} %fusion.15), channel_id=1, source_target_pairs={{0,8},{1,33},{2,10},{3,35},{4,12},{5,37},{6,14},{7,39},{8,0},{9,41... | collective-permute-start | bytes 528392 | tf_op jit(solution)/shard_map/ppermute | solution.py:47
  86.2 2.8 %collective-permute-done.6 = bf16[688,128]{1,0:T(8,128)(2,1)S(1)} collective-permute-done((bf16[688,128]{1,0:T(8,128)(2,1)S(1)}, bf16[688,128]{1,0:T(8,128)(2,1)S(1)}, u32[]{:S(2)}, u32[]{:S(2)}) %collective-permute-start.6) | collective-permute-done | bytes 176160 | tf_op jit(solution)/shard_map/ppermute | solution.py:47
  89.2 3.3 %collective-permute-done.7 = bf16[344,128]{1,0:T(8,128)(2,1)S(1)} collective-permute-done((bf16[344,128]{1,0:T(8,128)(2,1)S(1)}, bf16[344,128]{1,0:T(8,128)(2,1)S(1)}, u32[]{:S(2)}, u32[]{:S(2)}) %collective-permute-start.7) | collective-permute-done | bytes 88096 | tf_op jit(solution)/shard_map/ppermute | solution.py:47
  92.7 4.8 %collective-permute-done.8 = bf16[344,128]{1,0:T(8,128)(2,1)S(1)} collective-permute-done((bf16[344,128]{1,0:T(8,128)(2,1)S(1)}, bf16[344,128]{1,0:T(8,128)(2,1)S(1)}, u32[]{:S(2)}, u32[]{:S(2)}) %collective-permute-start.8) | collective-permute-done | bytes 88096 | tf_op jit(solution)/shard_map/ppermute | solution.py:50
  97.6 3.4 %collective-permute-start.9 = (bf16[344,128]{1,0:T(8,128)(2,1)S(1)}, bf16[344,128]{1,0:T(8,128)(2,1)S(1)}, u32[]{:S(2)}, u32[]{:S(2)}) collective-permute-start(bf16[344,128]{1,0:T(8,128)(2,1)S(1)} %add_convert_fusion.3), channel_id=1, source_target_pairs={{0,16},{1,65},{2,18},{3,67},{4,20},{5,69},{6,22},{7,71},{8,24},{9,... | collective-permute-start | bytes 264200 | tf_op jit(solution)/shard_map/ppermute | solution.py:50
  100.9 1.9 %collective-permute-done.9 = bf16[344,128]{1,0:T(8,128)(2,1)S(1)} collective-permute-done((bf16[344,128]{1,0:T(8,128)(2,1)S(1)}, bf16[344,128]{1,0:T(8,128)(2,1)S(1)}, u32[]{:S(2)}, u32[]{:S(2)}) %collective-permute-start.9) | collective-permute-done | bytes 88096 | tf_op jit(solution)/shard_map/ppermute | solution.py:50
  102.9 9.3 %collective-permute-start.10 = (bf16[344,128]{1,0:T(8,128)(2,1)S(1)}, bf16[344,128]{1,0:T(8,128)(2,1)S(1)}, u32[]{:S(2)}, u32[]{:S(2)}) collective-permute-start(bf16[344,128]{1,0:T(8,128)(2,1)S(1)} %add_convert_fusion.2), channel_id=1, source_target_pairs={{0,64},{1,129},{2,66},{3,131},{4,68},{5,133},{6,70},{7,135},{8,72}... | collective-permute-start | bytes 264200 | tf_op jit(solution)/shard_map/ppermute | solution.py:50
  112.1 2.4 %collective-permute-done.10 = bf16[344,128]{1,0:T(8,128)(2,1)S(1)} collective-permute-done((bf16[344,128]{1,0:T(8,128)(2,1)S(1)}, bf16[344,128]{1,0:T(8,128)(2,1)S(1)}, u32[]{:S(2)}, u32[]{:S(2)}) %collective-permute-start.10) | collective-permute-done | bytes 88096 | tf_op jit(solution)/shard_map/ppermute | solution.py:50
  114.8 4.7 %collective-permute-done.11 = bf16[344,128]{1,0:T(8,128)(2,1)S(1)} collective-permute-done((bf16[344,128]{1,0:T(8,128)(2,1)S(1)}, bf16[344,128]{1,0:T(8,128)(2,1)S(1)}, u32[]{:S(2)}, u32[]{:S(2)}) %collective-permute-start.11) | collective-permute-done | bytes 88096 | tf_op jit(solution)/shard_map/ppermute | solution.py:50
  119.7 3.2 %collective-permute-done.12 = bf16[344,128]{1,0:T(8,128)(2,1)S(1)} collective-permute-done((bf16[344,128]{1,0:T(8,128)(2,1)S(1)}, bf16[344,128]{1,0:T(8,128)(2,1)S(1)}, u32[]{:S(2)}, u32[]{:S(2)}) %collective-permute-start.12) | collective-permute-done | bytes 88096 | tf_op jit(solution)/shard_map/ppermute | solution.py:55
  125.9 2.4 %collective-permute-done.13 = bf16[688,128]{1,0:T(8,128)(2,1)S(1)} collective-permute-done((bf16[688,128]{1,0:T(8,128)(2,1)S(1)}, bf16[688,128]{1,0:T(8,128)(2,1)S(1)}, u32[]{:S(2)}, u32[]{:S(2)}) %collective-permute-start.13) | collective-permute-done | bytes 176160 | tf_op jit(solution)/shard_map/ppermute | solution.py:55
  128.8 5.7 %maximum_maximum_fusion.1 = bf16[3584,128]{1,0:T(8,128)(2,1)S(1)} fusion(bf16[1024,128]{1,0:T(8,128)(2,1)S(1)} %slice.55, bf16[1024,128]{1,0:T(8,128)(2,1)S(1)} %slice.54, bf16[1024,128]{1,0:T(8,128)(2,1)S(1)} %multiply_convert_fusion.1, bf16[3584]{0:T(1024)(128)(2,1)S(1)} %pad.34.clone), kind=kLoop, calls=%fused_computation.17 | loop fusion | flops 3670016 | bytes 1711104 | tf_op jit(solution)/shard_map/concatenate | solution.py:79
  134.5 6.3 %gather_fusion.4 = bf16[2000,128]{1,0:T(8,128)(2,1)S(1)} fusion(bf16[3584,128]{1,0:T(8,128)(2,1)S(1)} %maximum_maximum_fusion.1, s32[2048]{0:T(1024)S(1)} %pad_clamp_fusion), kind=kCustom, calls=%fused_computation.4 | custom fusion | bytes 1032000 | tf_op jit(solution)/shard_map/jit(_take)/gather | solution.py:109
  141.2 9.3 %collective-permute-start.15 = (bf16[2752,128]{1,0:T(8,128)(2,1)S(1)}, bf16[2752,128]{1,0:T(8,128)(2,1)S(1)}, u32[]{:S(2)}, u32[]{:S(2)}) collective-permute-start(bf16[2752,128]{1,0:T(8,128)(2,1)S(1)} %maximum_select_fusion.1), channel_id=1, source_target_pairs={{0,1},{1,0},{2,3},{3,2},{4,5},{5,4},{6,7},{7,6},{8,9},{9,8},{10,11... | collective-permute-start | bytes 2113544 | tf_op jit(solution)/shard_map/ppermute | solution.py:55
  150.5 3.1 %fusion.7 = f32[2,8,8,8,128]{4,0,3,2,1:T(2,128)S(1)} fusion(bf16[3,3,3,128,128]{4,3,2,1,0:T(8,128)(2,1)S(1)} %bitcast.74, bf16[2,10,10,10,128]{4,3,2,1,0:T(8,128)(2,1)S(1)} %reshape.324), kind=kOutput, calls=%fused_computation.33 | convolution fusion | flops 905969664 | bytes 1921024 | tf_op jit(solution)/shard_map/conv_general_dilated | solution.py:129
  154.9 1.3 slice_multiply_fusion
  (112 shorter events, 26.4 us)
Async XLA Ops:
  0.6 37.5 %copy-start = (bf16[27,128,128]{2,1,0:T(8,128)(2,1)S(1)}, bf16[27,128,128]{2,1,0:T(8,128)(2,1)}, u32[]{:S(2)}) copy-start(bf16[27,128,128]{2,1,0:T(8,128)(2,1)} %param.19) | copy-start | bytes 2654212
  0.6 15.6 %copy-start.9 = (s32[1,2,27]{2,1,0:T(2,128)S(1)}, s32[1,2,27]{2,1,0:T(2,128)}, u32[]{:S(2)}) copy-start(s32[1,2,27]{2,1,0:T(2,128)} %param.17) | copy-start | bytes 652
  0.7 13.4 %copy-start.2 = (bf16[8,128,256]{2,1,0:T(8,128)(2,1)S(1)}, bf16[8,128,256]{2,1,0:T(8,128)(2,1)}, u32[]{:S(2)}) copy-start(bf16[8,128,256]{2,1,0:T(8,128)(2,1)} %param.20) | copy-start | bytes 1572868
  4.0 8.8 %copy-start.11 = (bf16[1,16]{1,0:T(2,128)(2,1)}, bf16[1,16]{1,0:T(2,128)(2,1)S(1)}, u32[]{:S(2)}) copy-start(bf16[1,16]{1,0:T(2,128)(2,1)S(1)} %broadcast_select_fusion) | copy-start | bytes 100
  5.2 13.7 %collective-permute-start.1 = (bf16[1025,128]{1,0:T(8,128)(2,1)S(1)}, bf16[1025,128]{1,0:T(8,128)(2,1)}, u32[]{:S(2)}, u32[]{:S(2)}) collective-permute-start(bf16[1025,128]{1,0:T(8,128)(2,1)S(1)} %fusion.10), channel_id=1, source_target_pairs={{2,0},{4,2},{6,4},{8,6},{10,8},{12,10},{14,12},{16,14},{18,16},{20... | collective-permute-start | bytes 787208 | tf_op jit(solution)/shard_map/ppermute | solution.py:11
  6.5 10.7 %collective-permute-start = (bf16[1025,128]{1,0:T(8,128)(2,1)S(1)}, bf16[1025,128]{1,0:T(8,128)(2,1)}, u32[]{:S(2)}, u32[]{:S(2)}) collective-permute-start(bf16[1025,128]{1,0:T(8,128)(2,1)S(1)} %fusion.10), channel_id=1, source_target_pairs={{0,2},{2,4},{4,6},{6,8},{8,10},{10,12},{12,14},{14,16},{16,18},{18... | collective-permute-start | bytes 787208 | tf_op jit(solution)/shard_map/ppermute | solution.py:11
  14.0 0.6 copy-start.4
  14.0 3.2 %copy-start.10 = (s32[1000]{0:T(1024)S(1)}, s32[1000]{0:T(1024)}, u32[]{:S(2)}) copy-start(s32[1000]{0:T(1024)} %constant.133) | copy-start | bytes 12004
  16.9 6.5 %copy-start.8 = (s32[1000]{0:T(1024)S(1)}, s32[1000]{0:T(1024)}, u32[]{:S(2)}) copy-start(s32[1000]{0:T(1024)} %constant.132) | copy-start | bytes 12004
  38.1 3.2 %copy-start.6 = (f32[2,8,8,8]{3,2,1,0:T(8,128)S(1)}, f32[2,8,8,8]{3,2,1,0:T(8,128)}, u32[]{:S(2)}) copy-start(f32[2,8,8,8]{3,2,1,0:T(8,128)} %convert_element_type.230) | copy-start | bytes 12292
  41.3 0.7 copy-start.12
  42.7 11.8 %collective-permute-start.2 = (bf16[1025,128]{1,0:T(8,128)(2,1)}, bf16[1025,128]{1,0:T(8,128)(2,1)}, u32[]{:S(2)}, u32[]{:S(2)}) collective-permute-start(bf16[1025,128]{1,0:T(8,128)(2,1)} %fusion.11), channel_id=1, source_target_pairs={{0,2},{2,4},{4,6},{6,8},{8,10},{10,12},{12,14},{14,16},{16,18},{18... | collective-permute-start | bytes 787208 | tf_op jit(solution)/shard_map/ppermute | solution.py:11
  46.0 8.4 %collective-permute-start.3 = (bf16[1025,128]{1,0:T(8,128)(2,1)}, bf16[1025,128]{1,0:T(8,128)(2,1)}, u32[]{:S(2)}, u32[]{:S(2)}) collective-permute-start(bf16[1025,128]{1,0:T(8,128)(2,1)} %fusion.11), channel_id=1, source_target_pairs={{2,0},{4,2},{6,4},{8,6},{10,8},{12,10},{14,12},{16,14},{18,16},{20... | collective-permute-start | bytes 787208 | tf_op jit(solution)/shard_map/ppermute | solution.py:11
  53.2 0.8 copy-start.5
  56.1 1.6 copy-start.1
  57.7 4.8 %collective-permute-start.4 = (bf16[2752,128]{1,0:T(8,128)(2,1)S(1)}, bf16[2752,128]{1,0:T(8,128)(2,1)S(1)}, u32[]{:S(2)}, u32[]{:S(2)}) collective-permute-start(bf16[2752,128]{1,0:T(8,128)(2,1)S(1)} %fusion.3), channel_id=1, source_target_pairs={{0,1},{1,0},{2,3},{3,2},{4,5},{5,4},{6,7},{7,6},{8,9},{9,8},{10,11... | collective-permute-start | bytes 2113544 | tf_op jit(solution)/shard_map/ppermute | solution.py:47
  64.1 12.5 %collective-permute-start.5 = (bf16[1376,128]{1,0:T(8,128)(2,1)S(1)}, bf16[1376,128]{1,0:T(8,128)(2,1)}, u32[]{:S(2)}, u32[]{:S(2)}) collective-permute-start(bf16[1376,128]{1,0:T(8,128)(2,1)S(1)} %fusion.9), channel_id=1, source_target_pairs={{0,2},{1,9},{2,0},{3,11},{4,6},{5,13},{6,4},{7,15},{8,10},{9,1},{1... | collective-permute-start | bytes 1056776 | tf_op jit(solution)/shard_map/ppermute | solution.py:47
  77.6 45.5 %copy-start.3 = (bf16[8,128,256]{2,1,0:T(8,128)(2,1)S(1)}, bf16[8,128,256]{2,1,0:T(8,128)(2,1)}, u32[]{:S(2)}) copy-start(bf16[8,128,256]{2,1,0:T(8,128)(2,1)} %param.20) | copy-start | bytes 1572868
  77.7 11.4 %collective-permute-start.6 = (bf16[688,128]{1,0:T(8,128)(2,1)S(1)}, bf16[688,128]{1,0:T(8,128)(2,1)S(1)}, u32[]{:S(2)}, u32[]{:S(2)}) collective-permute-start(bf16[688,128]{1,0:T(8,128)(2,1)S(1)} %fusion.15), channel_id=1, source_target_pairs={{0,8},{1,33},{2,10},{3,35},{4,12},{5,37},{6,14},{7,39},{8,0},{9,41... | collective-permute-start | bytes 528392 | tf_op jit(solution)/shard_map/ppermute | solution.py:47
  89.1 3.4 %collective-permute-start.7 = (bf16[344,128]{1,0:T(8,128)(2,1)S(1)}, bf16[344,128]{1,0:T(8,128)(2,1)S(1)}, u32[]{:S(2)}, u32[]{:S(2)}) collective-permute-start(bf16[344,128]{1,0:T(8,128)(2,1)S(1)} %fusion.20), channel_id=1, source_target_pairs={{0,32},{1,3},{2,34},{3,1},{4,36},{5,7},{6,38},{7,5},{8,40},{9,11},... | collective-permute-start | bytes 264200 | tf_op jit(solution)/shard_map/ppermute | solution.py:47
  92.6 4.9 %collective-permute-start.8 = (bf16[344,128]{1,0:T(8,128)(2,1)S(1)}, bf16[344,128]{1,0:T(8,128)(2,1)S(1)}, u32[]{:S(2)}, u32[]{:S(2)}) collective-permute-start(bf16[344,128]{1,0:T(8,128)(2,1)S(1)} %fusion.16), channel_id=1, source_target_pairs={{0,4},{1,17},{2,6},{3,19},{4,0},{5,21},{6,2},{7,23},{8,12},{9,25},... | collective-permute-start | bytes 264200 | tf_op jit(solution)/shard_map/ppermute | solution.py:50
  97.6 5.3 %collective-permute-start.9 = (bf16[344,128]{1,0:T(8,128)(2,1)S(1)}, bf16[344,128]{1,0:T(8,128)(2,1)S(1)}, u32[]{:S(2)}, u32[]{:S(2)}) collective-permute-start(bf16[344,128]{1,0:T(8,128)(2,1)S(1)} %add_convert_fusion.3), channel_id=1, source_target_pairs={{0,16},{1,65},{2,18},{3,67},{4,20},{5,69},{6,22},{7,71},{8,24},{9,... | collective-permute-start | bytes 264200 | tf_op jit(solution)/shard_map/ppermute | solution.py:50
  102.9 11.6 %collective-permute-start.10 = (bf16[344,128]{1,0:T(8,128)(2,1)S(1)}, bf16[344,128]{1,0:T(8,128)(2,1)S(1)}, u32[]{:S(2)}, u32[]{:S(2)}) collective-permute-start(bf16[344,128]{1,0:T(8,128)(2,1)S(1)} %add_convert_fusion.2), channel_id=1, source_target_pairs={{0,64},{1,129},{2,66},{3,131},{4,68},{5,133},{6,70},{7,135},{8,72}... | collective-permute-start | bytes 264200 | tf_op jit(solution)/shard_map/ppermute | solution.py:50
  114.5 4.9 %collective-permute-start.11 = (bf16[344,128]{1,0:T(8,128)(2,1)S(1)}, bf16[344,128]{1,0:T(8,128)(2,1)S(1)}, u32[]{:S(2)}, u32[]{:S(2)}) collective-permute-start(bf16[344,128]{1,0:T(8,128)(2,1)S(1)} %add_convert_fusion.1), channel_id=1, source_target_pairs={{0,128},{1,5},{2,130},{3,7},{4,132},{5,1},{6,134},{7,3},{8,136},{9... | collective-permute-start | bytes 264200 | tf_op jit(solution)/shard_map/ppermute | solution.py:50
  119.5 3.4 %collective-permute-start.12 = (bf16[344,128]{1,0:T(8,128)(2,1)S(1)}, bf16[344,128]{1,0:T(8,128)(2,1)S(1)}, u32[]{:S(2)}, u32[]{:S(2)}) collective-permute-start(bf16[344,128]{1,0:T(8,128)(2,1)S(1)} %add_convert_fusion), channel_id=1, source_target_pairs={{0,32},{1,3},{2,34},{3,1},{4,36},{5,7},{6,38},{7,5},{8,40},{9,11},... | collective-permute-start | bytes 264200 | tf_op jit(solution)/shard_map/ppermute | solution.py:55
  123.0 5.3 %collective-permute-start.13 = (bf16[688,128]{1,0:T(8,128)(2,1)S(1)}, bf16[688,128]{1,0:T(8,128)(2,1)S(1)}, u32[]{:S(2)}, u32[]{:S(2)}) collective-permute-start(bf16[688,128]{1,0:T(8,128)(2,1)S(1)} %maximum_select_fusion.3), channel_id=1, source_target_pairs={{0,8},{1,33},{2,10},{3,35},{4,12},{5,37},{6,14},{7,39},{8,0},{9,41... | collective-permute-start | bytes 528392 | tf_op jit(solution)/shard_map/ppermute | solution.py:55
  128.4 12.6 %collective-permute-start.14 = (bf16[1376,128]{1,0:T(8,128)(2,1)S(1)}, bf16[1376,128]{1,0:T(8,128)(2,1)S(1)}, u32[]{:S(2)}, u32[]{:S(2)}) collective-permute-start(bf16[1376,128]{1,0:T(8,128)(2,1)S(1)} %maximum_select_fusion.2), channel_id=1, source_target_pairs={{0,2},{1,9},{2,0},{3,11},{4,6},{5,13},{6,4},{7,15},{8,10},{9,1},{1... | collective-permute-start | bytes 1056776 | tf_op jit(solution)/shard_map/ppermute | solution.py:55
  141.2 12.5 %copy-start.7 = (f32[2,512]{1,0:T(2,128)S(1)}, f32[2,512]{1,0:T(2,128)}, u32[]{:S(2)}) copy-start(f32[2,512]{1,0:T(2,128)} %get-tuple-element.32) | copy-start | bytes 12292
  141.2 13.4 %collective-permute-start.15 = (bf16[2752,128]{1,0:T(8,128)(2,1)S(1)}, bf16[2752,128]{1,0:T(8,128)(2,1)S(1)}, u32[]{:S(2)}, u32[]{:S(2)}) collective-permute-start(bf16[2752,128]{1,0:T(8,128)(2,1)S(1)} %maximum_select_fusion.1), channel_id=1, source_target_pairs={{0,1},{1,0},{2,3},{3,2},{4,5},{5,4},{6,7},{7,6},{8,9},{9,8},{10,11... | collective-permute-start | bytes 2113544 | tf_op jit(solution)/shard_map/ppermute | solution.py:55

commit v3 on v2

--- a/solution.py
+++ b/solution.py
@@ -11,8 +11,8 @@
     return lax.ppermute(value, axis, [(source, source + steps) for source in range(leading, last)])
 
 
-HALVE = (None, (1, 4), (4, 16), (16, 1))
-SPREAD = ((2, 8), (8, 32), (32, 64), (64, 2))
+HALVE = (None, (1, 4), (4, 16))
+SPREAD = ((16, 1), (2, 8), (8, 32), (32, 64), (64, 2))
 
 
 def joint_pairs(space_count, rep_count, masks):

time: 158 us -> 163 us (1.032)
  starting transfers between devices: 53.5 us -> 56.3 us
    ppermute x4 -> x5, waiting for transfers between devices: 13.8 us -> 20.9 us  [joint_psum(): other = lax.ppermute(narrow, axes, joint_pairs(*counts, masks))]
    ppermute x4 -> x3, waiting for transfers between devices: 12.8 us -> 9.47 us  [joint_psum(): lax.ppermute(send, axes, joint_pairs(*counts, masks)).astype(wide)]
    ppermute x4 -> x3, waiting for transfers between devices: 5.63 us -> 3.02 us  [joint_psum(): other = lax.ppermute(buf, axes, joint_pairs(*counts, masks))]
    ppermute x4 -> x5, starting transfers between devices: 13 us -> 15 us  [joint_psum(): other = lax.ppermute(narrow, axes, joint_pairs(*counts, masks))]
    ppermute x4 -> x3, starting transfers between devices: 9.81 us -> 10.7 us  [joint_psum(): other = lax.ppermute(buf, axes, joint_pairs(*counts, masks))]
    ppermute x4 -> x3, starting transfers between devices: 19.3 us -> 19.2 us  [joint_psum(): lax.ppermute(send, axes, joint_pairs(*counts, masks)).astype(wide)]
  transfers between devices with their start and end apart: 16 -> 15, of which waited for: 10 -> 9; matrix products, arithmetic and copies ran while one was open for 21% -> 20% of each run, Pallas kernels for 0% -> 0%
where the time goes in v3:
time: 163 us; the launch traced here: 161 us
  starting transfers between devices  56.3 us (35%)
  waiting for transfers between devices  33.4 us (20%)
  local copies, waits for them, and re-layouts  28.9 us (18%)
  other arithmetic  28.3 us (17%)
  matrix products  13.5 us (8%)
    ppermute x5, waiting for transfers between devices, joint_psum(): other = lax.ppermute(narrow, axes, joint_pairs(*counts, masks))  20.9 us
    ppermute x3, starting transfers between devices, joint_psum(): lax.ppermute(send, axes, joint_pairs(*counts, masks)).astype(wide)  19.2 us
    ppermute x5, starting transfers between devices, joint_psum(): other = lax.ppermute(narrow, axes, joint_pairs(*counts, masks))  15 us
    gather x2, local copies, waits for them, and re-layouts, pad_bricks(): padded = jnp.take(table, index.reshape(-1), axis=0, mode='clip')  12.7 us
    concatenate x2, other arithmetic, halo_table(): jnp.concatenate([values.reshape(bricks * voxels, channels), from_lower[:b...  11.5 us
    ppermute x4, starting transfers between devices, from_behind(): lax.ppermute(value, axis, [(source, source + steps) for source in range(l...  11.4 us
    ppermute x3, starting transfers between devices, joint_psum(): other = lax.ppermute(buf, axes, joint_pairs(*counts, masks))  10.7 us
    ppermute x3, waiting for transfers between devices, joint_psum(): lax.ppermute(send, axes, joint_pairs(*counts, masks)).astype(wide)  9.47 us
  transfers between devices with their start and end apart: 15, of which 9 were waited for; matrix products, arithmetic and copies ran while one was open for 20% of the time, Pallas kernels for 0%

profile of v3, /device:TPU:1, one launch (start us, length us, event | category | flops | bytes accessed | tf_op | source)
XLA Modules:
  0.0 161.4 jit_solution(2808854712270691415)
XLA Ops:
  1.3 1.4 convert_bitcast_fusion.1
  6.5 5.3 %collective-permute-start = (bf16[1025,128]{1,0:T(8,128)(2,1)S(1)}, bf16[1025,128]{1,0:T(8,128)(2,1)}, u32[]{:S(2)}, u32[]{:S(2)}) collective-permute-start(bf16[1025,128]{1,0:T(8,128)(2,1)S(1)} %fusion.11), channel_id=1, source_target_pairs={{0,2},{2,4},{4,6},{6,8},{8,10},{10,12},{12,14},{14,16},{16,18},{18... | collective-permute-start | bytes 787208 | tf_op jit(solution)/shard_map/ppermute | solution.py:11
  20.5 2.9 %gather_fusion.2 = s32[1000,2]{1,0:T(8,128)S(1)} fusion(s32[2,27]{0,1:T(8,128)S(1)} %compare_select_fusion, s32[1024]{0:T(1024)S(1)} %pad_clamp_fusion.1), kind=kCustom, calls=%fused_computation.2 | custom fusion | bytes 20000 | tf_op jit(solution)/shard_map/jit(_take)/gather | solution.py:107
  25.8 5.7 %maximum_maximum_fusion = bf16[3584,128]{1,0:T(8,128)(2,1)S(1)} fusion(bf16[1024,128]{1,0:T(8,128)(2,1)S(1)} %slice.69, bf16[1024,128]{1,0:T(8,128)(2,1)S(1)} %slice.68, bf16[1024,128]{1,0:T(8,128)(2,1)S(1)} %bitcast_multiply_fusion.1, bf16[3584]{0:T(1024)(128)(2,1)S(1)} %pad.30.clone), kind=kLoop, calls=%fused_computation.16 | loop fusion | flops 3670016 | bytes 1711104 | tf_op jit(solution)/shard_map/concatenate | solution.py:79
  31.6 6.3 %gather_fusion.3 = bf16[2000,128]{1,0:T(8,128)(2,1)S(1)} fusion(bf16[3584,128]{1,0:T(8,128)(2,1)S(1)} %maximum_maximum_fusion, s32[2048]{0:T(1024)S(1)} %pad_clamp_fusion), kind=kCustom, calls=%fused_computation.3 | custom fusion | bytes 1032000 | tf_op jit(solution)/shard_map/jit(_take)/gather | solution.py:109
  38.1 3.1 %fusion.18 = f32[2,8,8,8,128]{4,0,3,2,1:T(2,128)S(1)} fusion(bf16[3,3,3,128,128]{4,3,2,1,0:T(8,128)(2,1)S(1)} %bitcast.68, bf16[2,10,10,10,128]{4,3,2,1,0:T(8,128)(2,1)S(1)} %reshape.312), kind=kOutput, calls=%fused_computation.53 | convolution fusion | flops 905969664 | bytes 1921024 | tf_op jit(solution)/shard_map/conv_general_dilated | solution.py:119
  42.7 3.4 %collective-permute-start.2 = (bf16[1025,128]{1,0:T(8,128)(2,1)}, bf16[1025,128]{1,0:T(8,128)(2,1)}, u32[]{:S(2)}, u32[]{:S(2)}) collective-permute-start(bf16[1025,128]{1,0:T(8,128)(2,1)} %fusion.12), channel_id=1, source_target_pairs={{0,2},{2,4},{4,6},{6,8},{8,10},{10,12},{12,14},{14,16},{16,18},{18... | collective-permute-start | bytes 787208 | tf_op jit(solution)/shard_map/ppermute | solution.py:11
  46.0 1.5 collective-permute-start.3
  47.5 5.7 %fusion.13 = f32[3,3,3,128,128]{4,3,2,1,0:T(8,128)} fusion(bf16[2,8,8,8,128]{4,3,2,1,0:T(8,128)(2,1)S(1)} %get-tuple-element.31, bf16[2,10,10,10,128]{4,3,2,1,0:T(8,128)(2,1)S(1)} %reshape.312), kind=kOutput, calls=%fused_computation.48 | convolution fusion | flops 905969664 | bytes 2543616 | tf_op jit(solution)/shard_map/conv_general_dilated | solution.py:143
  54.4 1.7 %pad_maximum_fusion = f32[5504,128]{1,0:T(8,128)S(1)} fusion(f32[2048,128]{1,0:T(8,128)S(1)} %reshape.323, f32[3456,128]{1,0:T(8,128)} %bitcast.81), kind=kLoop, calls=%fused_computation.5 | loop fusion | flops 704512 | bytes 5636096 | tf_op jit(solution)/shard_map/concatenate | solution.py:206
  56.1 1.5 copy-done.1
  57.7 3.0 %collective-permute-start.4 = (bf16[2752,128]{1,0:T(8,128)(2,1)S(1)}, bf16[2752,128]{1,0:T(8,128)(2,1)S(1)}, u32[]{:S(2)}, u32[]{:S(2)}) collective-permute-start(bf16[2752,128]{1,0:T(8,128)(2,1)S(1)} %fusion.3), channel_id=1, source_target_pairs={{0,1},{1,0},{2,3},{3,2},{4,5},{5,4},{6,7},{7,6},{8,9},{9,8},{10,11... | collective-permute-start | bytes 2113544 | tf_op jit(solution)/shard_map/ppermute | solution.py:47
  60.7 1.8 %collective-permute-done.4 = bf16[2752,128]{1,0:T(8,128)(2,1)S(1)} collective-permute-done((bf16[2752,128]{1,0:T(8,128)(2,1)S(1)}, bf16[2752,128]{1,0:T(8,128)(2,1)S(1)}, u32[]{:S(2)}, u32[]{:S(2)}) %collective-permute-start.4) | collective-permute-done | bytes 704544 | tf_op jit(solution)/shard_map/ppermute | solution.py:47
  62.5 1.5 bitcast_add_fusion
  64.0 7.7 %collective-permute-start.5 = (bf16[1376,128]{1,0:T(8,128)(2,1)S(1)}, bf16[1376,128]{1,0:T(8,128)(2,1)}, u32[]{:S(2)}, u32[]{:S(2)}) collective-permute-start(bf16[1376,128]{1,0:T(8,128)(2,1)S(1)} %fusion.9), channel_id=1, source_target_pairs={{0,2},{1,9},{2,0},{3,11},{4,6},{5,13},{6,4},{7,15},{8,10},{9,1},{1... | collective-permute-start | bytes 1056776 | tf_op jit(solution)/shard_map/ppermute | solution.py:47
  71.8 4.8 %collective-permute-done.5 = bf16[1376,128]{1,0:T(8,128)(2,1)} collective-permute-done((bf16[1376,128]{1,0:T(8,128)(2,1)S(1)}, bf16[1376,128]{1,0:T(8,128)(2,1)}, u32[]{:S(2)}, u32[]{:S(2)}) %collective-permute-start.5) | collective-permute-done | bytes 352288 | tf_op jit(solution)/shard_map/ppermute | solution.py:47
  77.7 8.5 %collective-permute-start.6 = (bf16[688,128]{1,0:T(8,128)(2,1)S(1)}, bf16[688,128]{1,0:T(8,128)(2,1)S(1)}, u32[]{:S(2)}, u32[]{:S(2)}) collective-permute-start(bf16[688,128]{1,0:T(8,128)(2,1)S(1)} %fusion.16), channel_id=1, source_target_pairs={{0,8},{1,33},{2,10},{3,35},{4,12},{5,37},{6,14},{7,39},{8,0},{9,41... | collective-permute-start | bytes 528392 | tf_op jit(solution)/shard_map/ppermute | solution.py:47
  86.2 2.8 %collective-permute-done.6 = bf16[688,128]{1,0:T(8,128)(2,1)S(1)} collective-permute-done((bf16[688,128]{1,0:T(8,128)(2,1)S(1)}, bf16[688,128]{1,0:T(8,128)(2,1)S(1)}, u32[]{:S(2)}, u32[]{:S(2)}) %collective-permute-start.6) | collective-permute-done | bytes 176160 | tf_op jit(solution)/shard_map/ppermute | solution.py:47
  89.2 4.3 %collective-permute-done.7 = bf16[688,128]{1,0:T(8,128)(2,1)S(1)} collective-permute-done((bf16[688,128]{1,0:T(8,128)(2,1)S(1)}, bf16[688,128]{1,0:T(8,128)(2,1)S(1)}, u32[]{:S(2)}, u32[]{:S(2)}) %collective-permute-start.7) | collective-permute-done | bytes 176160 | tf_op jit(solution)/shard_map/ppermute | solution.py:50
  93.6 5.8 %collective-permute-done.8 = bf16[688,128]{1,0:T(8,128)(2,1)S(1)} collective-permute-done((bf16[688,128]{1,0:T(8,128)(2,1)S(1)}, bf16[688,128]{1,0:T(8,128)(2,1)S(1)}, u32[]{:S(2)}, u32[]{:S(2)}) %collective-permute-start.8) | collective-permute-done | bytes 176160 | tf_op jit(solution)/shard_map/ppermute | solution.py:50
  99.5 3.4 %collective-permute-start.9 = (bf16[688,128]{1,0:T(8,128)(2,1)S(1)}, bf16[688,128]{1,0:T(8,128)(2,1)S(1)}, u32[]{:S(2)}, u32[]{:S(2)}) collective-permute-start(bf16[688,128]{1,0:T(8,128)(2,1)S(1)} %add_convert_fusion.3), channel_id=1, source_target_pairs={{0,16},{1,65},{2,18},{3,67},{4,20},{5,69},{6,22},{7,71},{8,24},{9,... | collective-permute-start | bytes 528392 | tf_op jit(solution)/shard_map/ppermute | solution.py:50
  102.8 4.7 %collective-permute-done.9 = bf16[688,128]{1,0:T(8,128)(2,1)S(1)} collective-permute-done((bf16[688,128]{1,0:T(8,128)(2,1)S(1)}, bf16[688,128]{1,0:T(8,128)(2,1)S(1)}, u32[]{:S(2)}, u32[]{:S(2)}) %collective-permute-start.9) | collective-permute-done | bytes 176160 | tf_op jit(solution)/shard_map/ppermute | solution.py:50
  107.6 8.4 %collective-permute-start.10 = (bf16[688,128]{1,0:T(8,128)(2,1)S(1)}, bf16[688,128]{1,0:T(8,128)(2,1)S(1)}, u32[]{:S(2)}, u32[]{:S(2)}) collective-permute-start(bf16[688,128]{1,0:T(8,128)(2,1)S(1)} %add_convert_fusion.2), channel_id=1, source_target_pairs={{0,64},{1,129},{2,66},{3,131},{4,68},{5,133},{6,70},{7,135},{8,72}... | collective-permute-start | bytes 528392 | tf_op jit(solution)/shard_map/ppermute | solution.py:50
  116.0 3.4 %collective-permute-done.10 = bf16[688,128]{1,0:T(8,128)(2,1)S(1)} collective-permute-done((bf16[688,128]{1,0:T(8,128)(2,1)S(1)}, bf16[688,128]{1,0:T(8,128)(2,1)S(1)}, u32[]{:S(2)}, u32[]{:S(2)}) %collective-permute-start.10) | collective-permute-done | bytes 176160 | tf_op jit(solution)/shard_map/ppermute | solution.py:50
  119.4 3.1 %collective-permute-start.11 = (bf16[688,128]{1,0:T(8,128)(2,1)S(1)}, bf16[688,128]{1,0:T(8,128)(2,1)S(1)}, u32[]{:S(2)}, u32[]{:S(2)}) collective-permute-start(bf16[688,128]{1,0:T(8,128)(2,1)S(1)} %add_convert_fusion.1), channel_id=1, source_target_pairs={{0,128},{1,5},{2,130},{3,7},{4,132},{5,1},{6,134},{7,3},{8,136},{9... | collective-permute-start | bytes 528392 | tf_op jit(solution)/shard_map/ppermute | solution.py:50
  122.6 2.7 %collective-permute-done.11 = bf16[688,128]{1,0:T(8,128)(2,1)S(1)} collective-permute-done((bf16[688,128]{1,0:T(8,128)(2,1)S(1)}, bf16[688,128]{1,0:T(8,128)(2,1)S(1)}, u32[]{:S(2)}, u32[]{:S(2)}) %collective-permute-start.11) | collective-permute-done | bytes 176160 | tf_op jit(solution)/shard_map/ppermute | solution.py:50
  128.6 3.0 %collective-permute-done.12 = bf16[688,128]{1,0:T(8,128)(2,1)S(1)} collective-permute-done((bf16[688,128]{1,0:T(8,128)(2,1)S(1)}, bf16[688,128]{1,0:T(8,128)(2,1)S(1)}, u32[]{:S(2)}, u32[]{:S(2)}) %collective-permute-start.12) | collective-permute-done | bytes 176160 | tf_op jit(solution)/shard_map/ppermute | solution.py:55
  131.8 1.9 %collective-permute-start.13 = (bf16[1376,128]{1,0:T(8,128)(2,1)S(1)}, bf16[1376,128]{1,0:T(8,128)(2,1)S(1)}, u32[]{:S(2)}, u32[]{:S(2)}) collective-permute-start(bf16[1376,128]{1,0:T(8,128)(2,1)S(1)} %maximum_select_fusion.2), channel_id=1, source_target_pairs={{0,2},{1,9},{2,0},{3,11},{4,6},{5,13},{6,4},{7,15},{8,10},{9,1},{1... | collective-permute-start | bytes 1056776 | tf_op jit(solution)/shard_map/ppermute | solution.py:55
  133.7 5.7 %maximum_maximum_fusion.1 = bf16[3584,128]{1,0:T(8,128)(2,1)S(1)} fusion(bf16[1024,128]{1,0:T(8,128)(2,1)S(1)} %slice.55, bf16[1024,128]{1,0:T(8,128)(2,1)S(1)} %slice.54, bf16[1024,128]{1,0:T(8,128)(2,1)S(1)} %multiply_convert_fusion.1, bf16[3584]{0:T(1024)(128)(2,1)S(1)} %pad.30.clone), kind=kLoop, calls=%fused_computation.17 | loop fusion | flops 3670016 | bytes 1711104 | tf_op jit(solution)/shard_map/concatenate | solution.py:79
  139.4 6.3 %gather_fusion.4 = bf16[2000,128]{1,0:T(8,128)(2,1)S(1)} fusion(bf16[3584,128]{1,0:T(8,128)(2,1)S(1)} %maximum_maximum_fusion.1, s32[2048]{0:T(1024)S(1)} %pad_clamp_fusion), kind=kCustom, calls=%fused_computation.4 | custom fusion | bytes 1032000 | tf_op jit(solution)/shard_map/jit(_take)/gather | solution.py:109
  146.1 8.4 %collective-permute-start.14 = (bf16[2752,128]{1,0:T(8,128)(2,1)S(1)}, bf16[2752,128]{1,0:T(8,128)(2,1)S(1)}, u32[]{:S(2)}, u32[]{:S(2)}) collective-permute-start(bf16[2752,128]{1,0:T(8,128)(2,1)S(1)} %maximum_select_fusion.1), channel_id=1, source_target_pairs={{0,1},{1,0},{2,3},{3,2},{4,5},{5,4},{6,7},{7,6},{8,9},{9,8},{10,11... | collective-permute-start | bytes 2113544 | tf_op jit(solution)/shard_map/ppermute | solution.py:55
  154.4 3.1 %fusion.7 = f32[2,8,8,8,128]{4,0,3,2,1:T(2,128)S(1)} fusion(bf16[3,3,3,128,128]{4,3,2,1,0:T(8,128)(2,1)S(1)} %bitcast.69, bf16[2,10,10,10,128]{4,3,2,1,0:T(8,128)(2,1)S(1)} %reshape.320), kind=kOutput, calls=%fused_computation.33 | convolution fusion | flops 905969664 | bytes 1921024 | tf_op jit(solution)/shard_map/conv_general_dilated | solution.py:129
  (108 shorter events, 27.5 us)
Async XLA Ops:
  0.6 37.5 %copy-start = (bf16[27,128,128]{2,1,0:T(8,128)(2,1)S(1)}, bf16[27,128,128]{2,1,0:T(8,128)(2,1)}, u32[]{:S(2)}) copy-start(bf16[27,128,128]{2,1,0:T(8,128)(2,1)} %param.19) | copy-start | bytes 2654212
  0.6 15.6 %copy-start.9 = (s32[1,2,27]{2,1,0:T(2,128)S(1)}, s32[1,2,27]{2,1,0:T(2,128)}, u32[]{:S(2)}) copy-start(s32[1,2,27]{2,1,0:T(2,128)} %param.17) | copy-start | bytes 652
  0.7 13.4 %copy-start.2 = (bf16[8,128,256]{2,1,0:T(8,128)(2,1)S(1)}, bf16[8,128,256]{2,1,0:T(8,128)(2,1)}, u32[]{:S(2)}) copy-start(bf16[8,128,256]{2,1,0:T(8,128)(2,1)} %param.20) | copy-start | bytes 1572868
  4.0 8.8 %copy-start.11 = (bf16[1,16]{1,0:T(2,128)(2,1)}, bf16[1,16]{1,0:T(2,128)(2,1)S(1)}, u32[]{:S(2)}) copy-start(bf16[1,16]{1,0:T(2,128)(2,1)S(1)} %broadcast_select_fusion) | copy-start | bytes 100
  5.2 13.7 %collective-permute-start.1 = (bf16[1025,128]{1,0:T(8,128)(2,1)S(1)}, bf16[1025,128]{1,0:T(8,128)(2,1)}, u32[]{:S(2)}, u32[]{:S(2)}) collective-permute-start(bf16[1025,128]{1,0:T(8,128)(2,1)S(1)} %fusion.11), channel_id=1, source_target_pairs={{2,0},{4,2},{6,4},{8,6},{10,8},{12,10},{14,12},{16,14},{18,16},{20... | collective-permute-start | bytes 787208 | tf_op jit(solution)/shard_map/ppermute | solution.py:11
  6.5 10.7 %collective-permute-start = (bf16[1025,128]{1,0:T(8,128)(2,1)S(1)}, bf16[1025,128]{1,0:T(8,128)(2,1)}, u32[]{:S(2)}, u32[]{:S(2)}) collective-permute-start(bf16[1025,128]{1,0:T(8,128)(2,1)S(1)} %fusion.11), channel_id=1, source_target_pairs={{0,2},{2,4},{4,6},{6,8},{8,10},{10,12},{12,14},{14,16},{16,18},{18... | collective-permute-start | bytes 787208 | tf_op jit(solution)/shard_map/ppermute | solution.py:11
  14.0 0.6 copy-start.4
  14.0 3.2 %copy-start.10 = (s32[1000]{0:T(1024)S(1)}, s32[1000]{0:T(1024)}, u32[]{:S(2)}) copy-start(s32[1000]{0:T(1024)} %constant.126) | copy-start | bytes 12004
  16.9 6.5 %copy-start.8 = (s32[1000]{0:T(1024)S(1)}, s32[1000]{0:T(1024)}, u32[]{:S(2)}) copy-start(s32[1000]{0:T(1024)} %constant.125) | copy-start | bytes 12004
  38.1 3.2 %copy-start.6 = (f32[2,8,8,8]{3,2,1,0:T(8,128)S(1)}, f32[2,8,8,8]{3,2,1,0:T(8,128)}, u32[]{:S(2)}) copy-start(f32[2,8,8,8]{3,2,1,0:T(8,128)} %convert_element_type.226) | copy-start | bytes 12292
  41.3 0.7 copy-start.12
  42.7 11.8 %collective-permute-start.2 = (bf16[1025,128]{1,0:T(8,128)(2,1)}, bf16[1025,128]{1,0:T(8,128)(2,1)}, u32[]{:S(2)}, u32[]{:S(2)}) collective-permute-start(bf16[1025,128]{1,0:T(8,128)(2,1)} %fusion.12), channel_id=1, source_target_pairs={{0,2},{2,4},{4,6},{6,8},{8,10},{10,12},{12,14},{14,16},{16,18},{18... | collective-permute-start | bytes 787208 | tf_op jit(solution)/shard_map/ppermute | solution.py:11
  46.0 8.4 %collective-permute-start.3 = (bf16[1025,128]{1,0:T(8,128)(2,1)}, bf16[1025,128]{1,0:T(8,128)(2,1)}, u32[]{:S(2)}, u32[]{:S(2)}) collective-permute-start(bf16[1025,128]{1,0:T(8,128)(2,1)} %fusion.12), channel_id=1, source_target_pairs={{2,0},{4,2},{6,4},{8,6},{10,8},{12,10},{14,12},{16,14},{18,16},{20... | collective-permute-start | bytes 787208 | tf_op jit(solution)/shard_map/ppermute | solution.py:11
  53.2 0.8 copy-start.5
  56.1 1.6 copy-start.1
  57.7 4.8 %collective-permute-start.4 = (bf16[2752,128]{1,0:T(8,128)(2,1)S(1)}, bf16[2752,128]{1,0:T(8,128)(2,1)S(1)}, u32[]{:S(2)}, u32[]{:S(2)}) collective-permute-start(bf16[2752,128]{1,0:T(8,128)(2,1)S(1)} %fusion.3), channel_id=1, source_target_pairs={{0,1},{1,0},{2,3},{3,2},{4,5},{5,4},{6,7},{7,6},{8,9},{9,8},{10,11... | collective-permute-start | bytes 2113544 | tf_op jit(solution)/shard_map/ppermute | solution.py:47
  64.0 12.6 %collective-permute-start.5 = (bf16[1376,128]{1,0:T(8,128)(2,1)S(1)}, bf16[1376,128]{1,0:T(8,128)(2,1)}, u32[]{:S(2)}, u32[]{:S(2)}) collective-permute-start(bf16[1376,128]{1,0:T(8,128)(2,1)S(1)} %fusion.9), channel_id=1, source_target_pairs={{0,2},{1,9},{2,0},{3,11},{4,6},{5,13},{6,4},{7,15},{8,10},{9,1},{1... | collective-permute-start | bytes 1056776 | tf_op jit(solution)/shard_map/ppermute | solution.py:47
  77.6 48.2 %copy-start.3 = (bf16[8,128,256]{2,1,0:T(8,128)(2,1)S(1)}, bf16[8,128,256]{2,1,0:T(8,128)(2,1)}, u32[]{:S(2)}) copy-start(bf16[8,128,256]{2,1,0:T(8,128)(2,1)} %param.20) | copy-start | bytes 1572868
  77.7 11.4 %collective-permute-start.6 = (bf16[688,128]{1,0:T(8,128)(2,1)S(1)}, bf16[688,128]{1,0:T(8,128)(2,1)S(1)}, u32[]{:S(2)}, u32[]{:S(2)}) collective-permute-start(bf16[688,128]{1,0:T(8,128)(2,1)S(1)} %fusion.16), channel_id=1, source_target_pairs={{0,8},{1,33},{2,10},{3,35},{4,12},{5,37},{6,14},{7,39},{8,0},{9,41... | collective-permute-start | bytes 528392 | tf_op jit(solution)/shard_map/ppermute | solution.py:47
  89.1 4.4 %collective-permute-start.7 = (bf16[688,128]{1,0:T(8,128)(2,1)S(1)}, bf16[688,128]{1,0:T(8,128)(2,1)S(1)}, u32[]{:S(2)}, u32[]{:S(2)}) collective-permute-start(bf16[688,128]{1,0:T(8,128)(2,1)S(1)} %fusion.10), channel_id=1, source_target_pairs={{0,32},{1,3},{2,34},{3,1},{4,36},{5,7},{6,38},{7,5},{8,40},{9,11},... | collective-permute-start | bytes 528392 | tf_op jit(solution)/shard_map/ppermute | solution.py:50
  93.5 5.9 %collective-permute-start.8 = (bf16[688,128]{1,0:T(8,128)(2,1)S(1)}, bf16[688,128]{1,0:T(8,128)(2,1)S(1)}, u32[]{:S(2)}, u32[]{:S(2)}) collective-permute-start(bf16[688,128]{1,0:T(8,128)(2,1)S(1)} %add_convert_fusion.4), channel_id=1, source_target_pairs={{0,4},{1,17},{2,6},{3,19},{4,0},{5,21},{6,2},{7,23},{8,12},{9,25},... | collective-permute-start | bytes 528392 | tf_op jit(solution)/shard_map/ppermute | solution.py:50
  99.5 8.1 %collective-permute-start.9 = (bf16[688,128]{1,0:T(8,128)(2,1)S(1)}, bf16[688,128]{1,0:T(8,128)(2,1)S(1)}, u32[]{:S(2)}, u32[]{:S(2)}) collective-permute-start(bf16[688,128]{1,0:T(8,128)(2,1)S(1)} %add_convert_fusion.3), channel_id=1, source_target_pairs={{0,16},{1,65},{2,18},{3,67},{4,20},{5,69},{6,22},{7,71},{8,24},{9,... | collective-permute-start | bytes 528392 | tf_op jit(solution)/shard_map/ppermute | solution.py:50
  107.6 11.7 %collective-permute-start.10 = (bf16[688,128]{1,0:T(8,128)(2,1)S(1)}, bf16[688,128]{1,0:T(8,128)(2,1)S(1)}, u32[]{:S(2)}, u32[]{:S(2)}) collective-permute-start(bf16[688,128]{1,0:T(8,128)(2,1)S(1)} %add_convert_fusion.2), channel_id=1, source_target_pairs={{0,64},{1,129},{2,66},{3,131},{4,68},{5,133},{6,70},{7,135},{8,72}... | collective-permute-start | bytes 528392 | tf_op jit(solution)/shard_map/ppermute | solution.py:50
  119.4 5.9 %collective-permute-start.11 = (bf16[688,128]{1,0:T(8,128)(2,1)S(1)}, bf16[688,128]{1,0:T(8,128)(2,1)S(1)}, u32[]{:S(2)}, u32[]{:S(2)}) collective-permute-start(bf16[688,128]{1,0:T(8,128)(2,1)S(1)} %add_convert_fusion.1), channel_id=1, source_target_pairs={{0,128},{1,5},{2,130},{3,7},{4,132},{5,1},{6,134},{7,3},{8,136},{9... | collective-permute-start | bytes 528392 | tf_op jit(solution)/shard_map/ppermute | solution.py:50
  125.4 6.3 %collective-permute-start.12 = (bf16[688,128]{1,0:T(8,128)(2,1)S(1)}, bf16[688,128]{1,0:T(8,128)(2,1)S(1)}, u32[]{:S(2)}, u32[]{:S(2)}) collective-permute-start(bf16[688,128]{1,0:T(8,128)(2,1)S(1)} %add_convert_fusion), channel_id=1, source_target_pairs={{0,8},{1,33},{2,10},{3,35},{4,12},{5,37},{6,14},{7,39},{8,0},{9,41... | collective-permute-start | bytes 528392 | tf_op jit(solution)/shard_map/ppermute | solution.py:55
  131.8 14.1 %collective-permute-start.13 = (bf16[1376,128]{1,0:T(8,128)(2,1)S(1)}, bf16[1376,128]{1,0:T(8,128)(2,1)S(1)}, u32[]{:S(2)}, u32[]{:S(2)}) collective-permute-start(bf16[1376,128]{1,0:T(8,128)(2,1)S(1)} %maximum_select_fusion.2), channel_id=1, source_target_pairs={{0,2},{1,9},{2,0},{3,11},{4,6},{5,13},{6,4},{7,15},{8,10},{9,1},{1... | collective-permute-start | bytes 1056776 | tf_op jit(solution)/shard_map/ppermute | solution.py:55
  146.1 11.5 %copy-start.7 = (f32[2,512]{1,0:T(2,128)S(1)}, f32[2,512]{1,0:T(2,128)}, u32[]{:S(2)}) copy-start(f32[2,512]{1,0:T(2,128)} %get-tuple-element.32) | copy-start | bytes 12292
  146.1 12.4 %collective-permute-start.14 = (bf16[2752,128]{1,0:T(8,128)(2,1)S(1)}, bf16[2752,128]{1,0:T(8,128)(2,1)S(1)}, u32[]{:S(2)}, u32[]{:S(2)}) collective-permute-start(bf16[2752,128]{1,0:T(8,128)(2,1)S(1)} %maximum_select_fusion.1), channel_id=1, source_target_pairs={{0,1},{1,0},{2,3},{3,2},{4,5},{5,4},{6,7},{7,6},{8,9},{9,8},{10,11... | collective-permute-start | bytes 2113544 | tf_op jit(solution)/shard_map/ppermute | solution.py:55

commit v4 on v2

--- a/solution.py
+++ b/solution.py
@@ -35,7 +35,7 @@
     return ((lax.axis_index("space") & mask) > 0).astype(jnp.int32)
 
 
-def joint_psum(buf):
+def joint_psum(buf, scale):
     axes = ("space", "rep")
     counts = (lax.axis_size("space"), lax.axis_size("rep"))
     wide = buf.dtype
@@ -49,7 +49,7 @@
         narrow = buf.astype(jnp.bfloat16)
         other = lax.ppermute(narrow, axes, joint_pairs(*counts, masks))
         buf = narrow.astype(wide) + other.astype(wide)
-    buf = buf.astype(jnp.bfloat16)
+    buf = (buf * scale).astype(jnp.bfloat16)
     for masks in reversed(HALVE):
         me = step_bit(masks)
         other = lax.ppermute(buf, axes, joint_pairs(*counts, masks))
@@ -104,7 +104,8 @@
 
 def pad_bricks(table, rows, voxels):
     column, voxel = padding_maps()
-    index = jnp.take(rows, jnp.asarray(column.reshape(-1)), axis=1, mode="clip") * voxels
+    picks = jnp.asarray(column.reshape(1, -1, 1) == np.arange(rows.shape[1]).reshape(1, 1, -1))
+    index = jnp.sum(jnp.where(picks, rows[:, None, :], 0), axis=-1) * voxels
     index = index + jnp.asarray(voxel.reshape(1, -1))
     padded = jnp.take(table, index.reshape(-1), axis=0, mode="clip")
     return padded.reshape(rows.shape[0], 10, 10, 10, table.shape[-1])
@@ -204,15 +205,15 @@
     inverse_count = 1.0 / (lax.axis_size("space") * lax.axis_size("rep"))
     lanes = 128
     flat = jnp.concatenate([sub_grad.reshape(-1, lanes), down_grad.reshape(-1, lanes)])
-    flat = joint_psum(flat)
+    flat = joint_psum(flat, inverse_count)
     split = sub_grad.size // lanes
     sub_total = flat[:split].reshape(sub_grad.shape)
     down_total = flat[split:].reshape(down_grad.shape)
     return (
         coarse.reshape(1, bricks, voxels // 8, out_channels),
         grad_in.reshape(1, bricks, voxels, channels),
-        sub_total * inverse_count,
-        (down_total * inverse_count).reshape(w_down.shape),
+        sub_total,
+        down_total.reshape(w_down.shape),
     )
 
 

time: 158 us -> 155 us (0.981)
  local copies, waits for them, and re-layouts: 28.9 us -> 26.3 us
  other arithmetic: 28.2 us -> 26.2 us
    gather x1 -> x0, local copies, waits for them, and re-layouts: 2.9 us -> none  [pad_bricks(): jnp.take(rows, jnp.asarray(column.reshape(-1)), axis=1, mode='clip')]
  transfers between devices with their start and end apart: 16 -> 16, of which waited for: 10 -> 10; matrix products, arithmetic and copies ran while one was open for 21% -> 20% of each run, Pallas kernels for 0% -> 0%
where the time goes in v4:
time: 155 us; the launch traced here: 154 us
  starting transfers between devices  54.9 us (35%)
  waiting for transfers between devices  32.3 us (21%)
  local copies, waits for them, and re-layouts  26.3 us (17%)
  other arithmetic  26.2 us (17%)
  matrix products  13.5 us (9%)
    ppermute x4, starting transfers between devices, joint_psum(): lax.ppermute(send, axes, joint_pairs(*counts, masks)).astype(wide)  20.3 us
    ppermute x4, waiting for transfers between devices, joint_psum(): other = lax.ppermute(narrow, axes, joint_pairs(*counts, masks))  13.8 us
    ppermute x4, starting transfers between devices, joint_psum(): other = lax.ppermute(narrow, axes, joint_pairs(*counts, masks))  13 us
    ppermute x4, waiting for transfers between devices, joint_psum(): lax.ppermute(send, axes, joint_pairs(*counts, masks)).astype(wide)  12.8 us
    gather x2, local copies, waits for them, and re-layouts, pad_bricks(): padded = jnp.take(table, index.reshape(-1), axis=0, mode='clip')  12.7 us
    ppermute x4, starting transfers between devices, from_behind(): lax.ppermute(value, axis, [(source, source + steps) for source in range(l...  11.8 us
    concatenate x2, other arithmetic, halo_table(): jnp.concatenate([values.reshape(bricks * voxels, channels), from_lower[:b...  11.5 us
    ppermute x4, starting transfers between devices, joint_psum(): other = lax.ppermute(buf, axes, joint_pairs(*counts, masks))  9.8 us
  transfers between devices with their start and end apart: 16, of which 10 were waited for; matrix products, arithmetic and copies ran while one was open for 20% of the time, Pallas kernels for 0%

profile of v4, /device:TPU:1, one launch (start us, length us, event | category | flops | bytes accessed | tf_op | source)
XLA Modules:
  0.0 154.4 jit_solution(8040835685646318266)
XLA Ops:
  1.3 1.4 convert_bitcast_fusion.1
  2.7 1.3 broadcast_select_fusion
  6.5 5.3 %collective-permute-start = (bf16[1025,128]{1,0:T(8,128)(2,1)S(1)}, bf16[1025,128]{1,0:T(8,128)(2,1)}, u32[]{:S(2)}, u32[]{:S(2)}) collective-permute-start(bf16[1025,128]{1,0:T(8,128)(2,1)S(1)} %fusion.10), channel_id=1, source_target_pairs={{0,2},{2,4},{4,6},{6,8},{8,10},{10,12},{12,14},{14,16},{16,18},{18... | collective-permute-start | bytes 787208 | tf_op jit(solution)/shard_map/ppermute | solution.py:11
  21.3 5.7 %maximum_maximum_fusion = bf16[3584,128]{1,0:T(8,128)(2,1)S(1)} fusion(bf16[1024,128]{1,0:T(8,128)(2,1)S(1)} %slice.67, bf16[1024,128]{1,0:T(8,128)(2,1)S(1)} %slice.66, bf16[1024,128]{1,0:T(8,128)(2,1)S(1)} %bitcast_multiply_fusion.1, bf16[3584]{0:T(1024)(128)(2,1)S(1)} %pad.34.clone), kind=kLoop, calls=%fused_computation.13 | loop fusion | flops 3670016 | bytes 1711104 | tf_op jit(solution)/shard_map/concatenate | solution.py:79
  27.1 6.3 %gather_fusion.2 = bf16[2000,128]{1,0:T(8,128)(2,1)S(1)} fusion(bf16[3584,128]{1,0:T(8,128)(2,1)S(1)} %maximum_maximum_fusion, s32[2048]{0:T(1024)S(1)} %pad_clamp_fusion), kind=kCustom, calls=%fused_computation.2 | custom fusion | bytes 1032000 | tf_op jit(solution)/shard_map/jit(_take)/gather | solution.py:110
  33.6 3.1 %fusion.18 = f32[2,8,8,8,128]{4,0,3,2,1:T(2,128)S(1)} fusion(bf16[3,3,3,128,128]{4,3,2,1,0:T(8,128)(2,1)S(1)} %bitcast.72, bf16[2,10,10,10,128]{4,3,2,1,0:T(8,128)(2,1)S(1)} %reshape.340), kind=kOutput, calls=%fused_computation.52 | convolution fusion | flops 905969664 | bytes 1921024 | tf_op jit(solution)/shard_map/conv_general_dilated | solution.py:120
  38.1 3.8 %collective-permute-start.2 = (bf16[1025,128]{1,0:T(8,128)(2,1)}, bf16[1025,128]{1,0:T(8,128)(2,1)}, u32[]{:S(2)}, u32[]{:S(2)}) collective-permute-start(bf16[1025,128]{1,0:T(8,128)(2,1)} %fusion.11), channel_id=1, source_target_pairs={{0,2},{2,4},{4,6},{6,8},{8,10},{10,12},{12,14},{14,16},{16,18},{18... | collective-permute-start | bytes 787208 | tf_op jit(solution)/shard_map/ppermute | solution.py:11
  41.9 1.5 collective-permute-start.3
  43.4 5.7 %fusion.12 = f32[3,3,3,128,128]{4,3,2,1,0:T(8,128)} fusion(bf16[2,8,8,8,128]{4,3,2,1,0:T(8,128)(2,1)S(1)} %get-tuple-element.31, bf16[2,10,10,10,128]{4,3,2,1,0:T(8,128)(2,1)S(1)} %reshape.340), kind=kOutput, calls=%fused_computation.38 | convolution fusion | flops 905969664 | bytes 2543616 | tf_op jit(solution)/shard_map/conv_general_dilated | solution.py:144
  50.3 1.7 %pad_maximum_fusion = f32[5504,128]{1,0:T(8,128)S(1)} fusion(f32[2048,128]{1,0:T(8,128)S(1)} %reshape.351, f32[3456,128]{1,0:T(8,128)} %bitcast.85), kind=kLoop, calls=%fused_computation.4 | loop fusion | flops 704512 | bytes 5636096 | tf_op jit(solution)/shard_map/concatenate | solution.py:207
  52.0 1.6 %copy-done.1 = f32[5504,128]{1,0:T(8,128)} copy-done((f32[5504,128]{1,0:T(8,128)}, f32[5504,128]{1,0:T(8,128)S(1)}, u32[]{:S(2)}) %copy-start.1) | copy-done | bytes 2818072
  53.6 4.0 %collective-permute-start.4 = (bf16[2752,128]{1,0:T(8,128)(2,1)S(1)}, bf16[2752,128]{1,0:T(8,128)(2,1)S(1)}, u32[]{:S(2)}, u32[]{:S(2)}) collective-permute-start(bf16[2752,128]{1,0:T(8,128)(2,1)S(1)} %fusion.3), channel_id=1, source_target_pairs={{0,1},{1,0},{2,3},{3,2},{4,5},{5,4},{6,7},{7,6},{8,9},{9,8},{10,11... | collective-permute-start | bytes 2113544 | tf_op jit(solution)/shard_map/ppermute | solution.py:47
  57.6 1.8 %collective-permute-done.4 = bf16[2752,128]{1,0:T(8,128)(2,1)S(1)} collective-permute-done((bf16[2752,128]{1,0:T(8,128)(2,1)S(1)}, bf16[2752,128]{1,0:T(8,128)(2,1)S(1)}, u32[]{:S(2)}, u32[]{:S(2)}) %collective-permute-start.4) | collective-permute-done | bytes 704544 | tf_op jit(solution)/shard_map/ppermute | solution.py:47
  59.4 1.5 bitcast_add_fusion
  60.9 7.7 %collective-permute-start.5 = (bf16[1376,128]{1,0:T(8,128)(2,1)S(1)}, bf16[1376,128]{1,0:T(8,128)(2,1)}, u32[]{:S(2)}, u32[]{:S(2)}) collective-permute-start(bf16[1376,128]{1,0:T(8,128)(2,1)S(1)} %fusion.9), channel_id=1, source_target_pairs={{0,2},{1,9},{2,0},{3,11},{4,6},{5,13},{6,4},{7,15},{8,10},{9,1},{1... | collective-permute-start | bytes 1056776 | tf_op jit(solution)/shard_map/ppermute | solution.py:47
  68.6 4.8 %collective-permute-done.5 = bf16[1376,128]{1,0:T(8,128)(2,1)} collective-permute-done((bf16[1376,128]{1,0:T(8,128)(2,1)S(1)}, bf16[1376,128]{1,0:T(8,128)(2,1)}, u32[]{:S(2)}, u32[]{:S(2)}) %collective-permute-start.5) | collective-permute-done | bytes 352288 | tf_op jit(solution)/shard_map/ppermute | solution.py:47
  74.5 8.5 %collective-permute-start.6 = (bf16[688,128]{1,0:T(8,128)(2,1)S(1)}, bf16[688,128]{1,0:T(8,128)(2,1)S(1)}, u32[]{:S(2)}, u32[]{:S(2)}) collective-permute-start(bf16[688,128]{1,0:T(8,128)(2,1)S(1)} %fusion.15), channel_id=1, source_target_pairs={{0,8},{1,33},{2,10},{3,35},{4,12},{5,37},{6,14},{7,39},{8,0},{9,41... | collective-permute-start | bytes 528392 | tf_op jit(solution)/shard_map/ppermute | solution.py:47
  83.0 2.8 %collective-permute-done.6 = bf16[688,128]{1,0:T(8,128)(2,1)S(1)} collective-permute-done((bf16[688,128]{1,0:T(8,128)(2,1)S(1)}, bf16[688,128]{1,0:T(8,128)(2,1)S(1)}, u32[]{:S(2)}, u32[]{:S(2)}) %collective-permute-start.6) | collective-permute-done | bytes 176160 | tf_op jit(solution)/shard_map/ppermute | solution.py:47
  86.0 3.3 %collective-permute-done.7 = bf16[344,128]{1,0:T(8,128)(2,1)S(1)} collective-permute-done((bf16[344,128]{1,0:T(8,128)(2,1)S(1)}, bf16[344,128]{1,0:T(8,128)(2,1)S(1)}, u32[]{:S(2)}, u32[]{:S(2)}) %collective-permute-start.7) | collective-permute-done | bytes 88096 | tf_op jit(solution)/shard_map/ppermute | solution.py:47
  89.5 4.8 %collective-permute-done.8 = bf16[344,128]{1,0:T(8,128)(2,1)S(1)} collective-permute-done((bf16[344,128]{1,0:T(8,128)(2,1)S(1)}, bf16[344,128]{1,0:T(8,128)(2,1)S(1)}, u32[]{:S(2)}, u32[]{:S(2)}) %collective-permute-start.8) | collective-permute-done | bytes 88096 | tf_op jit(solution)/shard_map/ppermute | solution.py:50
  94.4 3.4 %collective-permute-start.9 = (bf16[344,128]{1,0:T(8,128)(2,1)S(1)}, bf16[344,128]{1,0:T(8,128)(2,1)S(1)}, u32[]{:S(2)}, u32[]{:S(2)}) collective-permute-start(bf16[344,128]{1,0:T(8,128)(2,1)S(1)} %add_convert_fusion.2), channel_id=1, source_target_pairs={{0,16},{1,65},{2,18},{3,67},{4,20},{5,69},{6,22},{7,71},{8,24},{9,... | collective-permute-start | bytes 264200 | tf_op jit(solution)/shard_map/ppermute | solution.py:50
  97.8 1.9 %collective-permute-done.9 = bf16[344,128]{1,0:T(8,128)(2,1)S(1)} collective-permute-done((bf16[344,128]{1,0:T(8,128)(2,1)S(1)}, bf16[344,128]{1,0:T(8,128)(2,1)S(1)}, u32[]{:S(2)}, u32[]{:S(2)}) %collective-permute-start.9) | collective-permute-done | bytes 88096 | tf_op jit(solution)/shard_map/ppermute | solution.py:50
  99.7 9.3 %collective-permute-start.10 = (bf16[344,128]{1,0:T(8,128)(2,1)S(1)}, bf16[344,128]{1,0:T(8,128)(2,1)S(1)}, u32[]{:S(2)}, u32[]{:S(2)}) collective-permute-start(bf16[344,128]{1,0:T(8,128)(2,1)S(1)} %add_convert_fusion.1), channel_id=1, source_target_pairs={{0,64},{1,129},{2,66},{3,131},{4,68},{5,133},{6,70},{7,135},{8,72}... | collective-permute-start | bytes 264200 | tf_op jit(solution)/shard_map/ppermute | solution.py:50
  109.0 2.4 %collective-permute-done.10 = bf16[344,128]{1,0:T(8,128)(2,1)S(1)} collective-permute-done((bf16[344,128]{1,0:T(8,128)(2,1)S(1)}, bf16[344,128]{1,0:T(8,128)(2,1)S(1)}, u32[]{:S(2)}, u32[]{:S(2)}) %collective-permute-start.10) | collective-permute-done | bytes 88096 | tf_op jit(solution)/shard_map/ppermute | solution.py:50
  111.6 4.7 %collective-permute-done.11 = bf16[344,128]{1,0:T(8,128)(2,1)S(1)} collective-permute-done((bf16[344,128]{1,0:T(8,128)(2,1)S(1)}, bf16[344,128]{1,0:T(8,128)(2,1)S(1)}, u32[]{:S(2)}, u32[]{:S(2)}) %collective-permute-start.11) | collective-permute-done | bytes 88096 | tf_op jit(solution)/shard_map/ppermute | solution.py:50
  116.6 3.2 %collective-permute-done.12 = bf16[344,128]{1,0:T(8,128)(2,1)S(1)} collective-permute-done((bf16[344,128]{1,0:T(8,128)(2,1)S(1)}, bf16[344,128]{1,0:T(8,128)(2,1)S(1)}, u32[]{:S(2)}, u32[]{:S(2)}) %collective-permute-start.12) | collective-permute-done | bytes 88096 | tf_op jit(solution)/shard_map/ppermute | solution.py:55
  122.8 2.4 %collective-permute-done.13 = bf16[688,128]{1,0:T(8,128)(2,1)S(1)} collective-permute-done((bf16[688,128]{1,0:T(8,128)(2,1)S(1)}, bf16[688,128]{1,0:T(8,128)(2,1)S(1)}, u32[]{:S(2)}, u32[]{:S(2)}) %collective-permute-start.13) | collective-permute-done | bytes 176160 | tf_op jit(solution)/shard_map/ppermute | solution.py:55
  125.6 5.7 %maximum_maximum_fusion.1 = bf16[3584,128]{1,0:T(8,128)(2,1)S(1)} fusion(bf16[1024,128]{1,0:T(8,128)(2,1)S(1)} %slice.55, bf16[1024,128]{1,0:T(8,128)(2,1)S(1)} %slice.54, bf16[1024,128]{1,0:T(8,128)(2,1)S(1)} %multiply_convert_fusion.1, bf16[3584]{0:T(1024)(128)(2,1)S(1)} %pad.34.clone), kind=kLoop, calls=%fused_computation.14 | loop fusion | flops 3670016 | bytes 1711104 | tf_op jit(solution)/shard_map/concatenate | solution.py:79
  131.3 6.3 %gather_fusion.3 = bf16[2000,128]{1,0:T(8,128)(2,1)S(1)} fusion(bf16[3584,128]{1,0:T(8,128)(2,1)S(1)} %maximum_maximum_fusion.1, s32[2048]{0:T(1024)S(1)} %pad_clamp_fusion), kind=kCustom, calls=%fused_computation.3 | custom fusion | bytes 1032000 | tf_op jit(solution)/shard_map/jit(_take)/gather | solution.py:110
  138.1 9.3 %collective-permute-start.15 = (bf16[2752,128]{1,0:T(8,128)(2,1)S(1)}, bf16[2752,128]{1,0:T(8,128)(2,1)S(1)}, u32[]{:S(2)}, u32[]{:S(2)}) collective-permute-start(bf16[2752,128]{1,0:T(8,128)(2,1)S(1)} %maximum_select_fusion.1), channel_id=1, source_target_pairs={{0,1},{1,0},{2,3},{3,2},{4,5},{5,4},{6,7},{7,6},{8,9},{9,8},{10,11... | collective-permute-start | bytes 2113544 | tf_op jit(solution)/shard_map/ppermute | solution.py:55
  147.4 3.1 %fusion.7 = f32[2,8,8,8,128]{4,0,3,2,1:T(2,128)S(1)} fusion(bf16[3,3,3,128,128]{4,3,2,1,0:T(8,128)(2,1)S(1)} %bitcast.73, bf16[2,10,10,10,128]{4,3,2,1,0:T(8,128)(2,1)S(1)} %reshape.348), kind=kOutput, calls=%fused_computation.29 | convolution fusion | flops 905969664 | bytes 1921024 | tf_op jit(solution)/shard_map/conv_general_dilated | solution.py:130
  151.7 1.3 slice.70
  (102 shorter events, 23.5 us)
Async XLA Ops:
  0.6 32.9 %copy-start = (bf16[27,128,128]{2,1,0:T(8,128)(2,1)S(1)}, bf16[27,128,128]{2,1,0:T(8,128)(2,1)}, u32[]{:S(2)}) copy-start(bf16[27,128,128]{2,1,0:T(8,128)(2,1)} %param.19) | copy-start | bytes 2654212
  0.6 12.6 %copy-start.2 = (bf16[8,128,256]{2,1,0:T(8,128)(2,1)S(1)}, bf16[8,128,256]{2,1,0:T(8,128)(2,1)}, u32[]{:S(2)}) copy-start(bf16[8,128,256]{2,1,0:T(8,128)(2,1)} %param.20) | copy-start | bytes 1572868
  0.7 13.2 %copy-start.9 = (s32[1,2,27]{2,1,0:T(2,128)S(1)}, s32[1,2,27]{2,1,0:T(2,128)}, u32[]{:S(2)}) copy-start(s32[1,2,27]{2,1,0:T(2,128)} %param.17) | copy-start | bytes 652
  5.2 12.2 %collective-permute-start.1 = (bf16[1025,128]{1,0:T(8,128)(2,1)S(1)}, bf16[1025,128]{1,0:T(8,128)(2,1)}, u32[]{:S(2)}, u32[]{:S(2)}) collective-permute-start(bf16[1025,128]{1,0:T(8,128)(2,1)S(1)} %fusion.10), channel_id=1, source_target_pairs={{2,0},{4,2},{6,4},{8,6},{10,8},{12,10},{14,12},{16,14},{18,16},{20... | collective-permute-start | bytes 787208 | tf_op jit(solution)/shard_map/ppermute | solution.py:11
  6.5 9.3 %collective-permute-start = (bf16[1025,128]{1,0:T(8,128)(2,1)S(1)}, bf16[1025,128]{1,0:T(8,128)(2,1)}, u32[]{:S(2)}, u32[]{:S(2)}) collective-permute-start(bf16[1025,128]{1,0:T(8,128)(2,1)S(1)} %fusion.10), channel_id=1, source_target_pairs={{0,2},{2,4},{4,6},{6,8},{8,10},{10,12},{12,14},{14,16},{16,18},{18... | collective-permute-start | bytes 787208 | tf_op jit(solution)/shard_map/ppermute | solution.py:11
  13.2 0.6 copy-start.4
  15.5 3.5 %copy-start.6 = (pred[1000,27]{0,1:T(8,128)(4,1)S(1)}, pred[1000,27]{0,1:T(8,128)(4,1)}, u32[]{:S(2)}) copy-start(pred[1000,27]{0,1:T(8,128)(4,1)} %constant.130) | copy-start | bytes 81004
  15.5 3.8 %copy-start.8 = (s32[1000]{0:T(1024)S(1)}, s32[1000]{0:T(1024)}, u32[]{:S(2)}) copy-start(s32[1000]{0:T(1024)} %constant.131) | copy-start | bytes 12004
  38.1 12.2 %collective-permute-start.2 = (bf16[1025,128]{1,0:T(8,128)(2,1)}, bf16[1025,128]{1,0:T(8,128)(2,1)}, u32[]{:S(2)}, u32[]{:S(2)}) collective-permute-start(bf16[1025,128]{1,0:T(8,128)(2,1)} %fusion.11), channel_id=1, source_target_pairs={{0,2},{2,4},{4,6},{6,8},{8,10},{10,12},{12,14},{14,16},{16,18},{18... | collective-permute-start | bytes 787208 | tf_op jit(solution)/shard_map/ppermute | solution.py:11
  41.9 8.4 %collective-permute-start.3 = (bf16[1025,128]{1,0:T(8,128)(2,1)}, bf16[1025,128]{1,0:T(8,128)(2,1)}, u32[]{:S(2)}, u32[]{:S(2)}) collective-permute-start(bf16[1025,128]{1,0:T(8,128)(2,1)} %fusion.11), channel_id=1, source_target_pairs={{2,0},{4,2},{6,4},{8,6},{10,8},{12,10},{14,12},{16,14},{18,16},{20... | collective-permute-start | bytes 787208 | tf_op jit(solution)/shard_map/ppermute | solution.py:11
  49.0 0.8 copy-start.5
  52.0 1.6 %copy-start.1 = (f32[5504,128]{1,0:T(8,128)}, f32[5504,128]{1,0:T(8,128)S(1)}, u32[]{:S(2)}) copy-start(f32[5504,128]{1,0:T(8,128)S(1)} %pad_maximum_fusion) | copy-start | bytes 8454148
  53.6 5.8 %collective-permute-start.4 = (bf16[2752,128]{1,0:T(8,128)(2,1)S(1)}, bf16[2752,128]{1,0:T(8,128)(2,1)S(1)}, u32[]{:S(2)}, u32[]{:S(2)}) collective-permute-start(bf16[2752,128]{1,0:T(8,128)(2,1)S(1)} %fusion.3), channel_id=1, source_target_pairs={{0,1},{1,0},{2,3},{3,2},{4,5},{5,4},{6,7},{7,6},{8,9},{9,8},{10,11... | collective-permute-start | bytes 2113544 | tf_op jit(solution)/shard_map/ppermute | solution.py:47
  60.9 12.5 %collective-permute-start.5 = (bf16[1376,128]{1,0:T(8,128)(2,1)S(1)}, bf16[1376,128]{1,0:T(8,128)(2,1)}, u32[]{:S(2)}, u32[]{:S(2)}) collective-permute-start(bf16[1376,128]{1,0:T(8,128)(2,1)S(1)} %fusion.9), channel_id=1, source_target_pairs={{0,2},{1,9},{2,0},{3,11},{4,6},{5,13},{6,4},{7,15},{8,10},{9,1},{1... | collective-permute-start | bytes 1056776 | tf_op jit(solution)/shard_map/ppermute | solution.py:47
  74.5 45.5 %copy-start.3 = (bf16[8,128,256]{2,1,0:T(8,128)(2,1)S(1)}, bf16[8,128,256]{2,1,0:T(8,128)(2,1)}, u32[]{:S(2)}) copy-start(bf16[8,128,256]{2,1,0:T(8,128)(2,1)} %param.20) | copy-start | bytes 1572868
  74.5 11.4 %collective-permute-start.6 = (bf16[688,128]{1,0:T(8,128)(2,1)S(1)}, bf16[688,128]{1,0:T(8,128)(2,1)S(1)}, u32[]{:S(2)}, u32[]{:S(2)}) collective-permute-start(bf16[688,128]{1,0:T(8,128)(2,1)S(1)} %fusion.15), channel_id=1, source_target_pairs={{0,8},{1,33},{2,10},{3,35},{4,12},{5,37},{6,14},{7,39},{8,0},{9,41... | collective-permute-start | bytes 528392 | tf_op jit(solution)/shard_map/ppermute | solution.py:47
  85.9 3.4 %collective-permute-start.7 = (bf16[344,128]{1,0:T(8,128)(2,1)S(1)}, bf16[344,128]{1,0:T(8,128)(2,1)S(1)}, u32[]{:S(2)}, u32[]{:S(2)}) collective-permute-start(bf16[344,128]{1,0:T(8,128)(2,1)S(1)} %fusion.20), channel_id=1, source_target_pairs={{0,32},{1,3},{2,34},{3,1},{4,36},{5,7},{6,38},{7,5},{8,40},{9,11},... | collective-permute-start | bytes 264200 | tf_op jit(solution)/shard_map/ppermute | solution.py:47
  89.4 4.9 %collective-permute-start.8 = (bf16[344,128]{1,0:T(8,128)(2,1)S(1)}, bf16[344,128]{1,0:T(8,128)(2,1)S(1)}, u32[]{:S(2)}, u32[]{:S(2)}) collective-permute-start(bf16[344,128]{1,0:T(8,128)(2,1)S(1)} %fusion.16), channel_id=1, source_target_pairs={{0,4},{1,17},{2,6},{3,19},{4,0},{5,21},{6,2},{7,23},{8,12},{9,25},... | collective-permute-start | bytes 264200 | tf_op jit(solution)/shard_map/ppermute | solution.py:50
  94.4 5.3 %collective-permute-start.9 = (bf16[344,128]{1,0:T(8,128)(2,1)S(1)}, bf16[344,128]{1,0:T(8,128)(2,1)S(1)}, u32[]{:S(2)}, u32[]{:S(2)}) collective-permute-start(bf16[344,128]{1,0:T(8,128)(2,1)S(1)} %add_convert_fusion.2), channel_id=1, source_target_pairs={{0,16},{1,65},{2,18},{3,67},{4,20},{5,69},{6,22},{7,71},{8,24},{9,... | collective-permute-start | bytes 264200 | tf_op jit(solution)/shard_map/ppermute | solution.py:50
  99.7 11.6 %collective-permute-start.10 = (bf16[344,128]{1,0:T(8,128)(2,1)S(1)}, bf16[344,128]{1,0:T(8,128)(2,1)S(1)}, u32[]{:S(2)}, u32[]{:S(2)}) collective-permute-start(bf16[344,128]{1,0:T(8,128)(2,1)S(1)} %add_convert_fusion.1), channel_id=1, source_target_pairs={{0,64},{1,129},{2,66},{3,131},{4,68},{5,133},{6,70},{7,135},{8,72}... | collective-permute-start | bytes 264200 | tf_op jit(solution)/shard_map/ppermute | solution.py:50
  111.4 4.9 %collective-permute-start.11 = (bf16[344,128]{1,0:T(8,128)(2,1)S(1)}, bf16[344,128]{1,0:T(8,128)(2,1)S(1)}, u32[]{:S(2)}, u32[]{:S(2)}) collective-permute-start(bf16[344,128]{1,0:T(8,128)(2,1)S(1)} %add_convert_fusion), channel_id=1, source_target_pairs={{0,128},{1,5},{2,130},{3,7},{4,132},{5,1},{6,134},{7,3},{8,136},{9... | collective-permute-start | bytes 264200 | tf_op jit(solution)/shard_map/ppermute | solution.py:50
  116.3 3.4 %collective-permute-start.12 = (bf16[344,128]{1,0:T(8,128)(2,1)S(1)}, bf16[344,128]{1,0:T(8,128)(2,1)S(1)}, u32[]{:S(2)}, u32[]{:S(2)}) collective-permute-start(bf16[344,128]{1,0:T(8,128)(2,1)S(1)} %multiply_convert_fusion.2), channel_id=1, source_target_pairs={{0,32},{1,3},{2,34},{3,1},{4,36},{5,7},{6,38},{7,5},{8,40},{9,11},... | collective-permute-start | bytes 264200 | tf_op jit(solution)/shard_map/ppermute | solution.py:55
  119.8 5.3 %collective-permute-start.13 = (bf16[688,128]{1,0:T(8,128)(2,1)S(1)}, bf16[688,128]{1,0:T(8,128)(2,1)S(1)}, u32[]{:S(2)}, u32[]{:S(2)}) collective-permute-start(bf16[688,128]{1,0:T(8,128)(2,1)S(1)} %maximum_select_fusion.3), channel_id=1, source_target_pairs={{0,8},{1,33},{2,10},{3,35},{4,12},{5,37},{6,14},{7,39},{8,0},{9,41... | collective-permute-start | bytes 528392 | tf_op jit(solution)/shard_map/ppermute | solution.py:55
  125.3 12.6 %collective-permute-start.14 = (bf16[1376,128]{1,0:T(8,128)(2,1)S(1)}, bf16[1376,128]{1,0:T(8,128)(2,1)S(1)}, u32[]{:S(2)}, u32[]{:S(2)}) collective-permute-start(bf16[1376,128]{1,0:T(8,128)(2,1)S(1)} %maximum_select_fusion.2), channel_id=1, source_target_pairs={{0,2},{1,9},{2,0},{3,11},{4,6},{5,13},{6,4},{7,15},{8,10},{9,1},{1... | collective-permute-start | bytes 1056776 | tf_op jit(solution)/shard_map/ppermute | solution.py:55
  138.1 12.5 %copy-start.7 = (f32[2,512]{1,0:T(2,128)S(1)}, f32[2,512]{1,0:T(2,128)}, u32[]{:S(2)}) copy-start(f32[2,512]{1,0:T(2,128)} %get-tuple-element.32) | copy-start | bytes 12292
  138.1 13.4 %collective-permute-start.15 = (bf16[2752,128]{1,0:T(8,128)(2,1)S(1)}, bf16[2752,128]{1,0:T(8,128)(2,1)S(1)}, u32[]{:S(2)}, u32[]{:S(2)}) collective-permute-start(bf16[2752,128]{1,0:T(8,128)(2,1)S(1)} %maximum_select_fusion.1), channel_id=1, source_target_pairs={{0,1},{1,0},{2,3},{3,2},{4,5},{5,4},{6,7},{7,6},{8,9},{9,8},{10,11... | collective-permute-start | bytes 2113544 | tf_op jit(solution)/shard_map/ppermute | solution.py:55

commit v5 on v4

--- a/solution.py
+++ b/solution.py
@@ -76,15 +76,11 @@
 def halo_table(values, received, cells):
     bricks, voxels, channels = values.shape
     from_lower, from_upper = received
-    table = jnp.concatenate(
-        [
-            values.reshape(bricks * voxels, channels),
-            from_lower[: bricks * voxels],
-            from_upper[: bricks * voxels],
-            jnp.zeros((voxels, channels), values.dtype),
-        ],
-        axis=0,
-    )
+    block = bricks * voxels
+    table = jnp.zeros(((3 * bricks + 1) * voxels, channels), values.dtype)
+    table = lax.dynamic_update_slice(table, values.reshape(block, channels), (0, 0))
+    table = lax.dynamic_update_slice(table, from_lower[:block], (block, 0))
+    table = lax.dynamic_update_slice(table, from_upper[:block], (2 * block, 0))
     lower_slots = from_lower[bricks * voxels, :cells].astype(jnp.int32)
     upper_slots = from_upper[bricks * voxels, :cells].astype(jnp.int32)
     return table, lower_slots, upper_slots

time: 155 us -> 139 us (0.90)
  other arithmetic: 26.2 us -> 13.3 us
  starting transfers between devices: 54.9 us -> 49 us
  local copies, waits for them, and re-layouts: 26.3 us -> 28.2 us
    concatenate x2 -> x0, other arithmetic: 11.5 us -> none  [halo_table(): jnp.concatenate([values.reshape(bricks * voxels, channels), from_lower[:b...]
    ppermute x4, starting transfers between devices: 20.3 us -> 13.5 us  [joint_psum(): lax.ppermute(send, axes, joint_pairs(*counts, masks)).astype(wide)]
    dynamic_update_slice x0 -> x6, local copies, waits for them, and re-layouts: none -> 4.15 us  [the longest x2 1.97 us: halo_table(): table = lax.dynamic_update_slice(table, from_upper[:block], (2 * block, 0))]
    slice x4 -> x0, local copies, waits for them, and re-layouts: 3.87 us -> none  [the longest x2 1.94 us: halo_table(): from_lower[:bricks * voxels]]
    ppermute x4, waiting for transfers between devices: 13.8 us -> 11.5 us  [joint_psum(): other = lax.ppermute(narrow, axes, joint_pairs(*counts, masks))]
    ppermute x4, waiting for transfers between devices: 5.63 us -> 7.61 us  [joint_psum(): other = lax.ppermute(buf, axes, joint_pairs(*counts, masks))]
    ppermute x4, starting transfers between devices: 13 us -> 14.9 us  [joint_psum(): other = lax.ppermute(narrow, axes, joint_pairs(*counts, masks))]
    convert_element_type x2, local copies, waits for them, and re-layouts: 0.66 us -> 2.5 us  [body(): grad_hidden.astype(jnp.float32) * silu_slope(pre_act) * occupancy[:, None]]
  transfers between devices with their start and end apart: 16 -> 16, of which waited for: 10 -> 11; matrix products, arithmetic and copies ran while one was open for 20% -> 19% of each run, Pallas kernels for 0% -> 0%
where the time goes in v5:
time: 139 us; the launch traced here: 138 us
  starting transfers between devices  49 us (35%)
  waiting for transfers between devices  33.1 us (24%)
  local copies, waits for them, and re-layouts  28.2 us (20%)
  matrix products  13.6 us (10%)
  other arithmetic  13.3 us (10%)
    ppermute x4, starting transfers between devices, joint_psum(): other = lax.ppermute(narrow, axes, joint_pairs(*counts, masks))  14.9 us
    ppermute x4, starting transfers between devices, joint_psum(): lax.ppermute(send, axes, joint_pairs(*counts, masks)).astype(wide)  13.5 us
    ppermute x4, waiting for transfers between devices, joint_psum(): lax.ppermute(send, axes, joint_pairs(*counts, masks)).astype(wide)  12.8 us
    gather x2, local copies, waits for them, and re-layouts, pad_bricks(): padded = jnp.take(table, index.reshape(-1), axis=0, mode='clip')  12.7 us
    ppermute x4, waiting for transfers between devices, joint_psum(): other = lax.ppermute(narrow, axes, joint_pairs(*counts, masks))  11.5 us
    ppermute x4, starting transfers between devices, from_behind(): lax.ppermute(value, axis, [(source, source + steps) for source in range(l...  10.8 us
    ppermute x4, starting transfers between devices, joint_psum(): other = lax.ppermute(buf, axes, joint_pairs(*counts, masks))  9.77 us
    ppermute x4, waiting for transfers between devices, joint_psum(): other = lax.ppermute(buf, axes, joint_pairs(*counts, masks))  7.61 us
  transfers between devices with their start and end apart: 16, of which 11 were waited for; matrix products, arithmetic and copies ran while one was open for 19% of the time, Pallas kernels for 0%

profile of v5, /device:TPU:1, one launch (start us, length us, event | category | flops | bytes accessed | tf_op | source)
XLA Modules:
  0.0 138.3 jit_solution(9176334623023528045)
XLA Ops:
  3.3 1.3 broadcast_select_fusion
  4.6 4.6 %collective-permute-start = (bf16[1025,128]{1,0:T(8,128)(2,1)S(1)}, bf16[1025,128]{1,0:T(8,128)(2,1)}, u32[]{:S(2)}, u32[]{:S(2)}) collective-permute-start(bf16[1025,128]{1,0:T(8,128)(2,1)S(1)} %fusion.10), channel_id=1, source_target_pairs={{0,2},{2,4},{4,6},{6,8},{8,10},{10,12},{12,14},{14,16},{16,18},{18... | collective-permute-start | bytes 787208 | tf_op jit(solution)/shard_map/ppermute | solution.py:11
  9.2 1.3 collective-permute-start.1
  14.1 1.3 copy.61
  22.1 6.3 %gather_fusion.2 = bf16[2000,128]{1,0:T(8,128)(2,1)S(1)} fusion(bf16[3584,128]{1,0:T(8,128)(2,1)S(1)} %slice_dynamic-update-slice_fusion, s32[2048]{0:T(1024)S(1)} %pad_clamp_fusion), kind=kCustom, calls=%fused_computation.2 | custom fusion | bytes 1032000 | tf_op jit(solution)/shard_map/jit(_take)/gather | solution.py:106
  28.7 3.1 %fusion.18 = f32[2,8,8,8,128]{4,0,3,2,1:T(2,128)S(1)} fusion(bf16[3,3,3,128,128]{4,3,2,1,0:T(8,128)(2,1)S(1)} %bitcast.72, bf16[2,10,10,10,128]{4,3,2,1,0:T(8,128)(2,1)S(1)} %reshape.340), kind=kOutput, calls=%fused_computation.54 | convolution fusion | flops 905969664 | bytes 1921024 | tf_op jit(solution)/shard_map/conv_general_dilated | solution.py:116
  33.2 3.5 %collective-permute-start.2 = (bf16[1025,128]{1,0:T(8,128)(2,1)}, bf16[1025,128]{1,0:T(8,128)(2,1)}, u32[]{:S(2)}, u32[]{:S(2)}) collective-permute-start(bf16[1025,128]{1,0:T(8,128)(2,1)} %fusion.11), channel_id=1, source_target_pairs={{0,2},{2,4},{4,6},{6,8},{8,10},{10,12},{12,14},{14,16},{16,18},{18... | collective-permute-start | bytes 787208 | tf_op jit(solution)/shard_map/ppermute | solution.py:11
  36.7 1.5 %collective-permute-start.3 = (bf16[1025,128]{1,0:T(8,128)(2,1)}, bf16[1025,128]{1,0:T(8,128)(2,1)}, u32[]{:S(2)}, u32[]{:S(2)}) collective-permute-start(bf16[1025,128]{1,0:T(8,128)(2,1)} %fusion.11), channel_id=1, source_target_pairs={{2,0},{4,2},{6,4},{8,6},{10,8},{12,10},{14,12},{16,14},{18,16},{20... | collective-permute-start | bytes 787208 | tf_op jit(solution)/shard_map/ppermute | solution.py:11
  38.1 5.7 %fusion.12 = f32[3,3,3,128,128]{4,3,2,1,0:T(8,128)} fusion(bf16[2,8,8,8,128]{4,3,2,1,0:T(8,128)(2,1)S(1)} %get-tuple-element.30, bf16[2,10,10,10,128]{4,3,2,1,0:T(8,128)(2,1)S(1)} %reshape.340), kind=kOutput, calls=%fused_computation.38 | convolution fusion | flops 905969664 | bytes 2543616 | tf_op jit(solution)/shard_map/conv_general_dilated | solution.py:140
  45.1 1.7 %pad_maximum_fusion = f32[5504,128]{1,0:T(8,128)S(1)} fusion(f32[2048,128]{1,0:T(8,128)S(1)} %reshape.351, f32[3456,128]{1,0:T(8,128)} %bitcast.85), kind=kLoop, calls=%fused_computation.4 | loop fusion | flops 704512 | bytes 5636096 | tf_op jit(solution)/shard_map/concatenate | solution.py:203
  46.7 1.5 %copy-done.1 = f32[5504,128]{1,0:T(8,128)} copy-done((f32[5504,128]{1,0:T(8,128)}, f32[5504,128]{1,0:T(8,128)S(1)}, u32[]{:S(2)}) %copy-start.1) | copy-done | bytes 2818072
  48.4 2.6 %collective-permute-start.4 = (bf16[2752,128]{1,0:T(8,128)(2,1)S(1)}, bf16[2752,128]{1,0:T(8,128)(2,1)S(1)}, u32[]{:S(2)}, u32[]{:S(2)}) collective-permute-start(bf16[2752,128]{1,0:T(8,128)(2,1)S(1)} %fusion.3), channel_id=1, source_target_pairs={{0,1},{1,0},{2,3},{3,2},{4,5},{5,4},{6,7},{7,6},{8,9},{9,8},{10,11... | collective-permute-start | bytes 2113544 | tf_op jit(solution)/shard_map/ppermute | solution.py:47
  51.0 1.8 %collective-permute-done.4 = bf16[2752,128]{1,0:T(8,128)(2,1)S(1)} collective-permute-done((bf16[2752,128]{1,0:T(8,128)(2,1)S(1)}, bf16[2752,128]{1,0:T(8,128)(2,1)S(1)}, u32[]{:S(2)}, u32[]{:S(2)}) %collective-permute-start.4) | collective-permute-done | bytes 704544 | tf_op jit(solution)/shard_map/ppermute | solution.py:47
  52.8 1.5 %bitcast_add_fusion = f32[2752,128]{1,0:T(8,128)S(1)} fusion(bf16[2752,128]{1,0:T(8,128)(2,1)S(1)} %collective-permute-done.4, f32[2,2752,128]{2,1,0:T(8,128)} %bitcast.75, s32[]{:T(128)S(6)} %select_n.131), kind=kLoop, calls=%fused_computation.7 | loop fusion | flops 704512 | bytes 3522564 | tf_op jit(solution)/shard_map/add | solution.py:47
  54.3 4.4 %collective-permute-start.5 = (bf16[1376,128]{1,0:T(8,128)(2,1)S(1)}, bf16[1376,128]{1,0:T(8,128)(2,1)}, u32[]{:S(2)}, u32[]{:S(2)}) collective-permute-start(bf16[1376,128]{1,0:T(8,128)(2,1)S(1)} %fusion.9), channel_id=1, source_target_pairs={{0,2},{1,9},{2,0},{3,11},{4,6},{5,13},{6,4},{7,15},{8,10},{9,1},{1... | collective-permute-start | bytes 1056776 | tf_op jit(solution)/shard_map/ppermute | solution.py:47
  58.7 4.8 %collective-permute-done.5 = bf16[1376,128]{1,0:T(8,128)(2,1)} collective-permute-done((bf16[1376,128]{1,0:T(8,128)(2,1)S(1)}, bf16[1376,128]{1,0:T(8,128)(2,1)}, u32[]{:S(2)}, u32[]{:S(2)}) %collective-permute-start.5) | collective-permute-done | bytes 352288 | tf_op jit(solution)/shard_map/ppermute | solution.py:47
  64.6 6.4 %collective-permute-start.6 = (bf16[688,128]{1,0:T(8,128)(2,1)S(1)}, bf16[688,128]{1,0:T(8,128)(2,1)S(1)}, u32[]{:S(2)}, u32[]{:S(2)}) collective-permute-start(bf16[688,128]{1,0:T(8,128)(2,1)S(1)} %fusion.15), channel_id=1, source_target_pairs={{0,8},{1,33},{2,10},{3,35},{4,12},{5,37},{6,14},{7,39},{8,0},{9,41... | collective-permute-start | bytes 528392 | tf_op jit(solution)/shard_map/ppermute | solution.py:47
  71.0 2.8 %collective-permute-done.6 = bf16[688,128]{1,0:T(8,128)(2,1)S(1)} collective-permute-done((bf16[688,128]{1,0:T(8,128)(2,1)S(1)}, bf16[688,128]{1,0:T(8,128)(2,1)S(1)}, u32[]{:S(2)}, u32[]{:S(2)}) %collective-permute-start.6) | collective-permute-done | bytes 176160 | tf_op jit(solution)/shard_map/ppermute | solution.py:47
  74.0 3.3 %collective-permute-done.7 = bf16[344,128]{1,0:T(8,128)(2,1)S(1)} collective-permute-done((bf16[344,128]{1,0:T(8,128)(2,1)S(1)}, bf16[344,128]{1,0:T(8,128)(2,1)S(1)}, u32[]{:S(2)}, u32[]{:S(2)}) %collective-permute-start.7) | collective-permute-done | bytes 88096 | tf_op jit(solution)/shard_map/ppermute | solution.py:47
  77.5 4.8 %collective-permute-done.8 = bf16[344,128]{1,0:T(8,128)(2,1)S(1)} collective-permute-done((bf16[344,128]{1,0:T(8,128)(2,1)S(1)}, bf16[344,128]{1,0:T(8,128)(2,1)S(1)}, u32[]{:S(2)}, u32[]{:S(2)}) %collective-permute-start.8) | collective-permute-done | bytes 88096 | tf_op jit(solution)/shard_map/ppermute | solution.py:50
  82.3 3.4 %collective-permute-start.9 = (bf16[344,128]{1,0:T(8,128)(2,1)S(1)}, bf16[344,128]{1,0:T(8,128)(2,1)S(1)}, u32[]{:S(2)}, u32[]{:S(2)}) collective-permute-start(bf16[344,128]{1,0:T(8,128)(2,1)S(1)} %add_convert_fusion.2), channel_id=1, source_target_pairs={{0,16},{1,65},{2,18},{3,67},{4,20},{5,69},{6,22},{7,71},{8,24},{9,... | collective-permute-start | bytes 264200 | tf_op jit(solution)/shard_map/ppermute | solution.py:50
  85.7 1.9 %collective-permute-done.9 = bf16[344,128]{1,0:T(8,128)(2,1)S(1)} collective-permute-done((bf16[344,128]{1,0:T(8,128)(2,1)S(1)}, bf16[344,128]{1,0:T(8,128)(2,1)S(1)}, u32[]{:S(2)}, u32[]{:S(2)}) %collective-permute-start.9) | collective-permute-done | bytes 88096 | tf_op jit(solution)/shard_map/ppermute | solution.py:50
  87.6 9.3 %collective-permute-start.10 = (bf16[344,128]{1,0:T(8,128)(2,1)S(1)}, bf16[344,128]{1,0:T(8,128)(2,1)S(1)}, u32[]{:S(2)}, u32[]{:S(2)}) collective-permute-start(bf16[344,128]{1,0:T(8,128)(2,1)S(1)} %add_convert_fusion.1), channel_id=1, source_target_pairs={{0,64},{1,129},{2,66},{3,131},{4,68},{5,133},{6,70},{7,135},{8,72}... | collective-permute-start | bytes 264200 | tf_op jit(solution)/shard_map/ppermute | solution.py:50
  96.9 1.9 %collective-permute-done.10 = bf16[344,128]{1,0:T(8,128)(2,1)S(1)} collective-permute-done((bf16[344,128]{1,0:T(8,128)(2,1)S(1)}, bf16[344,128]{1,0:T(8,128)(2,1)S(1)}, u32[]{:S(2)}, u32[]{:S(2)}) %collective-permute-start.10) | collective-permute-done | bytes 88096 | tf_op jit(solution)/shard_map/ppermute | solution.py:50
  98.8 2.1 %collective-permute-start.11 = (bf16[344,128]{1,0:T(8,128)(2,1)S(1)}, bf16[344,128]{1,0:T(8,128)(2,1)S(1)}, u32[]{:S(2)}, u32[]{:S(2)}) collective-permute-start(bf16[344,128]{1,0:T(8,128)(2,1)S(1)} %add_convert_fusion), channel_id=1, source_target_pairs={{0,128},{1,5},{2,130},{3,7},{4,132},{5,1},{6,134},{7,3},{8,136},{9... | collective-permute-start | bytes 264200 | tf_op jit(solution)/shard_map/ppermute | solution.py:50
  101.0 2.8 %collective-permute-done.11 = bf16[344,128]{1,0:T(8,128)(2,1)S(1)} collective-permute-done((bf16[344,128]{1,0:T(8,128)(2,1)S(1)}, bf16[344,128]{1,0:T(8,128)(2,1)S(1)}, u32[]{:S(2)}, u32[]{:S(2)}) %collective-permute-start.11) | collective-permute-done | bytes 88096 | tf_op jit(solution)/shard_map/ppermute | solution.py:50
  104.2 3.1 %collective-permute-done.12 = bf16[344,128]{1,0:T(8,128)(2,1)S(1)} collective-permute-done((bf16[344,128]{1,0:T(8,128)(2,1)S(1)}, bf16[344,128]{1,0:T(8,128)(2,1)S(1)}, u32[]{:S(2)}, u32[]{:S(2)}) %collective-permute-start.12) | collective-permute-done | bytes 88096 | tf_op jit(solution)/shard_map/ppermute | solution.py:55
  108.3 4.5 %collective-permute-done.13 = bf16[688,128]{1,0:T(8,128)(2,1)S(1)} collective-permute-done((bf16[688,128]{1,0:T(8,128)(2,1)S(1)}, bf16[688,128]{1,0:T(8,128)(2,1)S(1)}, u32[]{:S(2)}, u32[]{:S(2)}) %collective-permute-start.13) | collective-permute-done | bytes 176160 | tf_op jit(solution)/shard_map/ppermute | solution.py:55
  115.2 6.3 %gather_fusion.3 = bf16[2000,128]{1,0:T(8,128)(2,1)S(1)} fusion(bf16[3584,128]{1,0:T(8,128)(2,1)S(1)} %slice_dynamic-update-slice_fusion.2, s32[2048]{0:T(1024)S(1)} %pad_clamp_fusion), kind=kCustom, calls=%fused_computation.3 | custom fusion | bytes 1032000 | tf_op jit(solution)/shard_map/jit(_take)/gather | solution.py:106
  121.9 9.3 %collective-permute-start.15 = (bf16[2752,128]{1,0:T(8,128)(2,1)S(1)}, bf16[2752,128]{1,0:T(8,128)(2,1)S(1)}, u32[]{:S(2)}, u32[]{:S(2)}) collective-permute-start(bf16[2752,128]{1,0:T(8,128)(2,1)S(1)} %maximum_select_fusion.1), channel_id=1, source_target_pairs={{0,1},{1,0},{2,3},{3,2},{4,5},{5,4},{6,7},{7,6},{8,9},{9,8},{10,11... | collective-permute-start | bytes 2113544 | tf_op jit(solution)/shard_map/ppermute | solution.py:55
  131.2 3.2 %fusion.7 = f32[2,8,8,8,128]{4,0,3,2,1:T(2,128)S(1)} fusion(bf16[3,3,3,128,128]{4,3,2,1,0:T(8,128)(2,1)S(1)} %bitcast.73, bf16[2,10,10,10,128]{4,3,2,1,0:T(8,128)(2,1)S(1)} %reshape.348), kind=kOutput, calls=%fused_computation.27 | convolution fusion | flops 905969664 | bytes 1921024 | tf_op jit(solution)/shard_map/conv_general_dilated | solution.py:126
  135.6 1.3 slice.70
  (104 shorter events, 23.7 us)
Async XLA Ops:
  0.6 28.0 %copy-start = (bf16[27,128,128]{2,1,0:T(8,128)(2,1)S(1)}, bf16[27,128,128]{2,1,0:T(8,128)(2,1)}, u32[]{:S(2)}) copy-start(bf16[27,128,128]{2,1,0:T(8,128)(2,1)} %param.19) | copy-start | bytes 2654212
  0.6 10.4 %copy-start.6 = (bf16[1,2,64,256]{3,2,1,0:T(8,128)(2,1)S(1)}, bf16[1,2,64,256]{3,2,1,0:T(8,128)(2,1)}, u32[]{:S(2)}) copy-start(bf16[1,2,64,256]{3,2,1,0:T(8,128)(2,1)} %param.21) | copy-start | bytes 196612
  0.7 10.5 %copy-start.2 = (bf16[8,128,256]{2,1,0:T(8,128)(2,1)S(1)}, bf16[8,128,256]{2,1,0:T(8,128)(2,1)}, u32[]{:S(2)}) copy-start(bf16[8,128,256]{2,1,0:T(8,128)(2,1)} %param.20) | copy-start | bytes 1572868
  2.1 9.4 %copy-start.9 = (s32[1,2,27]{2,1,0:T(2,128)S(1)}, s32[1,2,27]{2,1,0:T(2,128)}, u32[]{:S(2)}) copy-start(s32[1,2,27]{2,1,0:T(2,128)} %param.17) | copy-start | bytes 652
  4.6 8.0 %copy-start.10 = (bf16[1,16]{1,0:T(2,128)(2,1)}, bf16[1,16]{1,0:T(2,128)(2,1)S(1)}, u32[]{:S(2)}) copy-start(bf16[1,16]{1,0:T(2,128)(2,1)S(1)} %broadcast_select_fusion) | copy-start | bytes 100
  4.6 10.8 %collective-permute-start = (bf16[1025,128]{1,0:T(8,128)(2,1)S(1)}, bf16[1025,128]{1,0:T(8,128)(2,1)}, u32[]{:S(2)}, u32[]{:S(2)}) collective-permute-start(bf16[1025,128]{1,0:T(8,128)(2,1)S(1)} %fusion.10), channel_id=1, source_target_pairs={{0,2},{2,4},{4,6},{6,8},{8,10},{10,12},{12,14},{14,16},{16,18},{18... | collective-permute-start | bytes 787208 | tf_op jit(solution)/shard_map/ppermute | solution.py:11
  9.2 8.9 %collective-permute-start.1 = (bf16[1025,128]{1,0:T(8,128)(2,1)S(1)}, bf16[1025,128]{1,0:T(8,128)(2,1)}, u32[]{:S(2)}, u32[]{:S(2)}) collective-permute-start(bf16[1025,128]{1,0:T(8,128)(2,1)S(1)} %fusion.10), channel_id=1, source_target_pairs={{2,0},{4,2},{6,4},{8,6},{10,8},{12,10},{14,12},{16,14},{18,16},{20... | collective-permute-start | bytes 787208 | tf_op jit(solution)/shard_map/ppermute | solution.py:11
  11.2 1.4 copy-start.4
  14.1 5.8 %copy-start.7 = (pred[1000,27]{0,1:T(8,128)(4,1)S(1)}, pred[1000,27]{0,1:T(8,128)(4,1)}, u32[]{:S(2)}) copy-start(pred[1000,27]{0,1:T(8,128)(4,1)} %constant.138) | copy-start | bytes 81004
  14.1 6.0 %copy-start.8 = (s32[1000]{0:T(1024)S(1)}, s32[1000]{0:T(1024)}, u32[]{:S(2)}) copy-start(s32[1000]{0:T(1024)} %constant.139) | copy-start | bytes 12004
  31.8 0.7 copy-start.11
  33.2 11.9 %collective-permute-start.2 = (bf16[1025,128]{1,0:T(8,128)(2,1)}, bf16[1025,128]{1,0:T(8,128)(2,1)}, u32[]{:S(2)}, u32[]{:S(2)}) collective-permute-start(bf16[1025,128]{1,0:T(8,128)(2,1)} %fusion.11), channel_id=1, source_target_pairs={{0,2},{2,4},{4,6},{6,8},{8,10},{10,12},{12,14},{14,16},{16,18},{18... | collective-permute-start | bytes 787208 | tf_op jit(solution)/shard_map/ppermute | solution.py:11
  36.7 8.4 %collective-permute-start.3 = (bf16[1025,128]{1,0:T(8,128)(2,1)}, bf16[1025,128]{1,0:T(8,128)(2,1)}, u32[]{:S(2)}, u32[]{:S(2)}) collective-permute-start(bf16[1025,128]{1,0:T(8,128)(2,1)} %fusion.11), channel_id=1, source_target_pairs={{2,0},{4,2},{6,4},{8,6},{10,8},{12,10},{14,12},{16,14},{18,16},{20... | collective-permute-start | bytes 787208 | tf_op jit(solution)/shard_map/ppermute | solution.py:11
  43.8 0.8 copy-start.5
  46.7 1.6 %copy-start.1 = (f32[5504,128]{1,0:T(8,128)}, f32[5504,128]{1,0:T(8,128)S(1)}, u32[]{:S(2)}) copy-start(f32[5504,128]{1,0:T(8,128)S(1)} %pad_maximum_fusion) | copy-start | bytes 8454148
  48.4 4.4 %collective-permute-start.4 = (bf16[2752,128]{1,0:T(8,128)(2,1)S(1)}, bf16[2752,128]{1,0:T(8,128)(2,1)S(1)}, u32[]{:S(2)}, u32[]{:S(2)}) collective-permute-start(bf16[2752,128]{1,0:T(8,128)(2,1)S(1)} %fusion.3), channel_id=1, source_target_pairs={{0,1},{1,0},{2,3},{3,2},{4,5},{5,4},{6,7},{7,6},{8,9},{9,8},{10,11... | collective-permute-start | bytes 2113544 | tf_op jit(solution)/shard_map/ppermute | solution.py:47
  54.3 9.2 %collective-permute-start.5 = (bf16[1376,128]{1,0:T(8,128)(2,1)S(1)}, bf16[1376,128]{1,0:T(8,128)(2,1)}, u32[]{:S(2)}, u32[]{:S(2)}) collective-permute-start(bf16[1376,128]{1,0:T(8,128)(2,1)S(1)} %fusion.9), channel_id=1, source_target_pairs={{0,2},{1,9},{2,0},{3,11},{4,6},{5,13},{6,4},{7,15},{8,10},{9,1},{1... | collective-permute-start | bytes 1056776 | tf_op jit(solution)/shard_map/ppermute | solution.py:47
  64.6 9.2 %collective-permute-start.6 = (bf16[688,128]{1,0:T(8,128)(2,1)S(1)}, bf16[688,128]{1,0:T(8,128)(2,1)S(1)}, u32[]{:S(2)}, u32[]{:S(2)}) collective-permute-start(bf16[688,128]{1,0:T(8,128)(2,1)S(1)} %fusion.15), channel_id=1, source_target_pairs={{0,8},{1,33},{2,10},{3,35},{4,12},{5,37},{6,14},{7,39},{8,0},{9,41... | collective-permute-start | bytes 528392 | tf_op jit(solution)/shard_map/ppermute | solution.py:47
  73.9 3.4 %collective-permute-start.7 = (bf16[344,128]{1,0:T(8,128)(2,1)S(1)}, bf16[344,128]{1,0:T(8,128)(2,1)S(1)}, u32[]{:S(2)}, u32[]{:S(2)}) collective-permute-start(bf16[344,128]{1,0:T(8,128)(2,1)S(1)} %fusion.20), channel_id=1, source_target_pairs={{0,32},{1,3},{2,34},{3,1},{4,36},{5,7},{6,38},{7,5},{8,40},{9,11},... | collective-permute-start | bytes 264200 | tf_op jit(solution)/shard_map/ppermute | solution.py:47
  74.0 33.4 %copy-start.3 = (bf16[8,128,256]{2,1,0:T(8,128)(2,1)S(1)}, bf16[8,128,256]{2,1,0:T(8,128)(2,1)}, u32[]{:S(2)}) copy-start(bf16[8,128,256]{2,1,0:T(8,128)(2,1)} %param.20) | copy-start | bytes 1572868
  77.4 4.9 %collective-permute-start.8 = (bf16[344,128]{1,0:T(8,128)(2,1)S(1)}, bf16[344,128]{1,0:T(8,128)(2,1)S(1)}, u32[]{:S(2)}, u32[]{:S(2)}) collective-permute-start(bf16[344,128]{1,0:T(8,128)(2,1)S(1)} %fusion.16), channel_id=1, source_target_pairs={{0,4},{1,17},{2,6},{3,19},{4,0},{5,21},{6,2},{7,23},{8,12},{9,25},... | collective-permute-start | bytes 264200 | tf_op jit(solution)/shard_map/ppermute | solution.py:50
  82.3 5.3 %collective-permute-start.9 = (bf16[344,128]{1,0:T(8,128)(2,1)S(1)}, bf16[344,128]{1,0:T(8,128)(2,1)S(1)}, u32[]{:S(2)}, u32[]{:S(2)}) collective-permute-start(bf16[344,128]{1,0:T(8,128)(2,1)S(1)} %add_convert_fusion.2), channel_id=1, source_target_pairs={{0,16},{1,65},{2,18},{3,67},{4,20},{5,69},{6,22},{7,71},{8,24},{9,... | collective-permute-start | bytes 264200 | tf_op jit(solution)/shard_map/ppermute | solution.py:50
  87.6 11.2 %collective-permute-start.10 = (bf16[344,128]{1,0:T(8,128)(2,1)S(1)}, bf16[344,128]{1,0:T(8,128)(2,1)S(1)}, u32[]{:S(2)}, u32[]{:S(2)}) collective-permute-start(bf16[344,128]{1,0:T(8,128)(2,1)S(1)} %add_convert_fusion.1), channel_id=1, source_target_pairs={{0,64},{1,129},{2,66},{3,131},{4,68},{5,133},{6,70},{7,135},{8,72}... | collective-permute-start | bytes 264200 | tf_op jit(solution)/shard_map/ppermute | solution.py:50
  98.8 4.9 %collective-permute-start.11 = (bf16[344,128]{1,0:T(8,128)(2,1)S(1)}, bf16[344,128]{1,0:T(8,128)(2,1)S(1)}, u32[]{:S(2)}, u32[]{:S(2)}) collective-permute-start(bf16[344,128]{1,0:T(8,128)(2,1)S(1)} %add_convert_fusion), channel_id=1, source_target_pairs={{0,128},{1,5},{2,130},{3,7},{4,132},{5,1},{6,134},{7,3},{8,136},{9... | collective-permute-start | bytes 264200 | tf_op jit(solution)/shard_map/ppermute | solution.py:50
  103.8 3.4 %collective-permute-start.12 = (bf16[344,128]{1,0:T(8,128)(2,1)S(1)}, bf16[344,128]{1,0:T(8,128)(2,1)S(1)}, u32[]{:S(2)}, u32[]{:S(2)}) collective-permute-start(bf16[344,128]{1,0:T(8,128)(2,1)S(1)} %multiply_convert_fusion.2), channel_id=1, source_target_pairs={{0,32},{1,3},{2,34},{3,1},{4,36},{5,7},{6,38},{7,5},{8,40},{9,11},... | collective-permute-start | bytes 264200 | tf_op jit(solution)/shard_map/ppermute | solution.py:55
  107.3 5.5 %collective-permute-start.13 = (bf16[688,128]{1,0:T(8,128)(2,1)S(1)}, bf16[688,128]{1,0:T(8,128)(2,1)S(1)}, u32[]{:S(2)}, u32[]{:S(2)}) collective-permute-start(bf16[688,128]{1,0:T(8,128)(2,1)S(1)} %maximum_select_fusion.3), channel_id=1, source_target_pairs={{0,8},{1,33},{2,10},{3,35},{4,12},{5,37},{6,14},{7,39},{8,0},{9,41... | collective-permute-start | bytes 528392 | tf_op jit(solution)/shard_map/ppermute | solution.py:55
  112.9 8.8 %collective-permute-start.14 = (bf16[1376,128]{1,0:T(8,128)(2,1)S(1)}, bf16[1376,128]{1,0:T(8,128)(2,1)S(1)}, u32[]{:S(2)}, u32[]{:S(2)}) collective-permute-start(bf16[1376,128]{1,0:T(8,128)(2,1)S(1)} %maximum_select_fusion.2), channel_id=1, source_target_pairs={{0,2},{1,9},{2,0},{3,11},{4,6},{5,13},{6,4},{7,15},{8,10},{9,1},{1... | collective-permute-start | bytes 1056776 | tf_op jit(solution)/shard_map/ppermute | solution.py:55
  121.9 13.4 %collective-permute-start.15 = (bf16[2752,128]{1,0:T(8,128)(2,1)S(1)}, bf16[2752,128]{1,0:T(8,128)(2,1)S(1)}, u32[]{:S(2)}, u32[]{:S(2)}) collective-permute-start(bf16[2752,128]{1,0:T(8,128)(2,1)S(1)} %maximum_select_fusion.1), channel_id=1, source_target_pairs={{0,1},{1,0},{2,3},{3,2},{4,5},{5,4},{6,7},{7,6},{8,9},{9,8},{10,11... | collective-permute-start | bytes 2113544 | tf_op jit(solution)/shard_map/ppermute | solution.py:55

commit v6 on v5

--- a/solution.py
+++ b/solution.py
@@ -89,8 +89,11 @@
 def brick_rows(link_rows, lower_slots, upper_slots, bricks):
     cells = lower_slots.shape[0]
     empty = 3 * bricks
-    lower = jnp.take(lower_slots, jnp.clip(link_rows - bricks, 0, cells - 1), mode="clip")
-    upper = jnp.take(upper_slots, jnp.clip(link_rows - bricks - cells, 0, cells - 1), mode="clip")
+    positions = jnp.arange(cells, dtype=jnp.int32)
+    lower_hit = (link_rows - bricks)[..., None] == positions
+    upper_hit = (link_rows - bricks - cells)[..., None] == positions
+    lower = jnp.sum(jnp.where(lower_hit, lower_slots, 0), axis=-1)
+    upper = jnp.sum(jnp.where(upper_hit, upper_slots, 0), axis=-1)
     lower = jnp.where(lower < bricks, bricks + lower, empty)
     upper = jnp.where(upper < bricks, 2 * bricks + upper, empty)
     from_upper = jnp.where(link_rows < bricks + 2 * cells, upper, empty)

time: 139 us -> 138 us (level)
  local copies, waits for them, and re-layouts: 28.2 us -> 26.3 us
  waiting for transfers between devices: 33.1 us -> 34.6 us
    gather x2 -> x0, local copies, waits for them, and re-layouts: 1.55 us -> none  [the longest x1 0.77 us: brick_rows(): jnp.take(lower_slots, jnp.clip(link_rows - bricks, 0, cells - 1), mode='c...]
where the time goes in v6:
time: 138 us; the launch traced here: 137 us
  starting transfers between devices  47.9 us (35%)
  waiting for transfers between devices  34.6 us (25%)
  local copies, waits for them, and re-layouts  26.3 us (19%)
  matrix products  13.6 us (10%)
  other arithmetic  13.5 us (10%)
    ppermute x4, starting transfers between devices, joint_psum(): other = lax.ppermute(narrow, axes, joint_pairs(*counts, masks))  14.4 us
    ppermute x4, starting transfers between devices, joint_psum(): lax.ppermute(send, axes, joint_pairs(*counts, masks)).astype(wide)  13.3 us
    ppermute x4, waiting for transfers between devices, joint_psum(): lax.ppermute(send, axes, joint_pairs(*counts, masks)).astype(wide)  12.8 us
    gather x2, local copies, waits for them, and re-layouts, pad_bricks(): padded = jnp.take(table, index.reshape(-1), axis=0, mode='clip')  12.7 us
    ppermute x4, waiting for transfers between devices, joint_psum(): other = lax.ppermute(narrow, axes, joint_pairs(*counts, masks))  12.2 us
    ppermute x4, starting transfers between devices, from_behind(): lax.ppermute(value, axis, [(source, source + steps) for source in range(l...  10.5 us
    ppermute x4, starting transfers between devices, joint_psum(): other = lax.ppermute(buf, axes, joint_pairs(*counts, masks))  9.77 us
    ppermute x4, waiting for transfers between devices, joint_psum(): other = lax.ppermute(buf, axes, joint_pairs(*counts, masks))  7.42 us
  transfers between devices with their start and end apart: 16, of which 11 were waited for; matrix products, arithmetic and copies ran while one was open for 19% of the time, Pallas kernels for 0%

profile of v6, /device:TPU:1, one launch (start us, length us, event | category | flops | bytes accessed | tf_op | source)
XLA Modules:
  0.0 136.9 jit_solution(4643482236328878253)
XLA Ops:
  3.2 1.3 broadcast_select_fusion
  4.6 4.6 %collective-permute-start = (bf16[1025,128]{1,0:T(8,128)(2,1)S(1)}, bf16[1025,128]{1,0:T(8,128)(2,1)}, u32[]{:S(2)}, u32[]{:S(2)}) collective-permute-start(bf16[1025,128]{1,0:T(8,128)(2,1)S(1)} %fusion.10), channel_id=1, source_target_pairs={{0,2},{2,4},{4,6},{6,8},{8,10},{10,12},{12,14},{14,16},{16,18},{18... | collective-permute-start | bytes 787208 | tf_op jit(solution)/shard_map/ppermute | solution.py:11
  9.2 1.3 collective-permute-start.1
  16.0 2.2 %collective-permute-done.1 = bf16[1025,128]{1,0:T(8,128)(2,1)} collective-permute-done((bf16[1025,128]{1,0:T(8,128)(2,1)S(1)}, bf16[1025,128]{1,0:T(8,128)(2,1)}, u32[]{:S(2)}, u32[]{:S(2)}) %collective-permute-start.1) | collective-permute-done | bytes 262432 | tf_op jit(solution)/shard_map/ppermute | solution.py:11
  21.4 6.3 %gather_fusion = bf16[2000,128]{1,0:T(8,128)(2,1)S(1)} fusion(bf16[3584,128]{1,0:T(8,128)(2,1)S(1)} %slice_dynamic-update-slice_fusion, s32[2048]{0:T(1024)S(1)} %pad_clamp_fusion), kind=kCustom, calls=%fused_computation | custom fusion | bytes 1032000 | tf_op jit(solution)/shard_map/jit(_take)/gather | solution.py:109
  27.9 3.1 %fusion.18 = f32[2,8,8,8,128]{4,0,3,2,1:T(2,128)S(1)} fusion(bf16[3,3,3,128,128]{4,3,2,1,0:T(8,128)(2,1)S(1)} %bitcast.74, bf16[2,10,10,10,128]{4,3,2,1,0:T(8,128)(2,1)S(1)} %reshape.314), kind=kOutput, calls=%fused_computation.52 | convolution fusion | flops 905969664 | bytes 1921024 | tf_op jit(solution)/shard_map/conv_general_dilated | solution.py:119
  32.4 3.1 %collective-permute-start.2 = (bf16[1025,128]{1,0:T(8,128)(2,1)}, bf16[1025,128]{1,0:T(8,128)(2,1)}, u32[]{:S(2)}, u32[]{:S(2)}) collective-permute-start(bf16[1025,128]{1,0:T(8,128)(2,1)} %fusion.11), channel_id=1, source_target_pairs={{0,2},{2,4},{4,6},{6,8},{8,10},{10,12},{12,14},{14,16},{16,18},{18... | collective-permute-start | bytes 787208 | tf_op jit(solution)/shard_map/ppermute | solution.py:11
  35.5 1.5 %collective-permute-start.3 = (bf16[1025,128]{1,0:T(8,128)(2,1)}, bf16[1025,128]{1,0:T(8,128)(2,1)}, u32[]{:S(2)}, u32[]{:S(2)}) collective-permute-start(bf16[1025,128]{1,0:T(8,128)(2,1)} %fusion.11), channel_id=1, source_target_pairs={{2,0},{4,2},{6,4},{8,6},{10,8},{12,10},{14,12},{16,14},{18,16},{20... | collective-permute-start | bytes 787208 | tf_op jit(solution)/shard_map/ppermute | solution.py:11
  37.0 5.7 %fusion.12 = f32[3,3,3,128,128]{4,3,2,1,0:T(8,128)} fusion(bf16[2,8,8,8,128]{4,3,2,1,0:T(8,128)(2,1)S(1)} %get-tuple-element.30, bf16[2,10,10,10,128]{4,3,2,1,0:T(8,128)(2,1)S(1)} %reshape.314), kind=kOutput, calls=%fused_computation.36 | convolution fusion | flops 905969664 | bytes 2543616 | tf_op jit(solution)/shard_map/conv_general_dilated | solution.py:143
  43.9 1.7 %pad_maximum_fusion = f32[5504,128]{1,0:T(8,128)S(1)} fusion(f32[2048,128]{1,0:T(8,128)S(1)} %reshape.325, f32[3456,128]{1,0:T(8,128)} %bitcast.87), kind=kLoop, calls=%fused_computation.2 | loop fusion | flops 704512 | bytes 5636096 | tf_op jit(solution)/shard_map/concatenate | solution.py:206
  45.6 1.5 %copy-done.1 = f32[5504,128]{1,0:T(8,128)} copy-done((f32[5504,128]{1,0:T(8,128)}, f32[5504,128]{1,0:T(8,128)S(1)}, u32[]{:S(2)}) %copy-start.1) | copy-done | bytes 2818072
  47.2 2.6 %collective-permute-start.4 = (bf16[2752,128]{1,0:T(8,128)(2,1)S(1)}, bf16[2752,128]{1,0:T(8,128)(2,1)S(1)}, u32[]{:S(2)}, u32[]{:S(2)}) collective-permute-start(bf16[2752,128]{1,0:T(8,128)(2,1)S(1)} %fusion.3), channel_id=1, source_target_pairs={{0,1},{1,0},{2,3},{3,2},{4,5},{5,4},{6,7},{7,6},{8,9},{9,8},{10,11... | collective-permute-start | bytes 2113544 | tf_op jit(solution)/shard_map/ppermute | solution.py:47
  49.9 1.8 %collective-permute-done.4 = bf16[2752,128]{1,0:T(8,128)(2,1)S(1)} collective-permute-done((bf16[2752,128]{1,0:T(8,128)(2,1)S(1)}, bf16[2752,128]{1,0:T(8,128)(2,1)S(1)}, u32[]{:S(2)}, u32[]{:S(2)}) %collective-permute-start.4) | collective-permute-done | bytes 704544 | tf_op jit(solution)/shard_map/ppermute | solution.py:47
  51.6 1.5 %bitcast_add_fusion = f32[2752,128]{1,0:T(8,128)S(1)} fusion(bf16[2752,128]{1,0:T(8,128)(2,1)S(1)} %collective-permute-done.4, f32[2,2752,128]{2,1,0:T(8,128)} %bitcast.77, s32[]{:T(128)S(6)} %select_n.140), kind=kLoop, calls=%fused_computation.5 | loop fusion | flops 704512 | bytes 3522564 | tf_op jit(solution)/shard_map/add | solution.py:47
  53.2 4.1 %collective-permute-start.5 = (bf16[1376,128]{1,0:T(8,128)(2,1)S(1)}, bf16[1376,128]{1,0:T(8,128)(2,1)}, u32[]{:S(2)}, u32[]{:S(2)}) collective-permute-start(bf16[1376,128]{1,0:T(8,128)(2,1)S(1)} %fusion.9), channel_id=1, source_target_pairs={{0,2},{1,9},{2,0},{3,11},{4,6},{5,13},{6,4},{7,15},{8,10},{9,1},{1... | collective-permute-start | bytes 1056776 | tf_op jit(solution)/shard_map/ppermute | solution.py:47
  57.3 4.8 %collective-permute-done.5 = bf16[1376,128]{1,0:T(8,128)(2,1)} collective-permute-done((bf16[1376,128]{1,0:T(8,128)(2,1)S(1)}, bf16[1376,128]{1,0:T(8,128)(2,1)}, u32[]{:S(2)}, u32[]{:S(2)}) %collective-permute-start.5) | collective-permute-done | bytes 352288 | tf_op jit(solution)/shard_map/ppermute | solution.py:47
  63.2 6.4 %collective-permute-start.6 = (bf16[688,128]{1,0:T(8,128)(2,1)S(1)}, bf16[688,128]{1,0:T(8,128)(2,1)S(1)}, u32[]{:S(2)}, u32[]{:S(2)}) collective-permute-start(bf16[688,128]{1,0:T(8,128)(2,1)S(1)} %fusion.15), channel_id=1, source_target_pairs={{0,8},{1,33},{2,10},{3,35},{4,12},{5,37},{6,14},{7,39},{8,0},{9,41... | collective-permute-start | bytes 528392 | tf_op jit(solution)/shard_map/ppermute | solution.py:47
  69.6 2.8 %collective-permute-done.6 = bf16[688,128]{1,0:T(8,128)(2,1)S(1)} collective-permute-done((bf16[688,128]{1,0:T(8,128)(2,1)S(1)}, bf16[688,128]{1,0:T(8,128)(2,1)S(1)}, u32[]{:S(2)}, u32[]{:S(2)}) %collective-permute-start.6) | collective-permute-done | bytes 176160 | tf_op jit(solution)/shard_map/ppermute | solution.py:47
  72.6 3.3 %collective-permute-done.7 = bf16[344,128]{1,0:T(8,128)(2,1)S(1)} collective-permute-done((bf16[344,128]{1,0:T(8,128)(2,1)S(1)}, bf16[344,128]{1,0:T(8,128)(2,1)S(1)}, u32[]{:S(2)}, u32[]{:S(2)}) %collective-permute-start.7) | collective-permute-done | bytes 88096 | tf_op jit(solution)/shard_map/ppermute | solution.py:47
  76.1 4.8 %collective-permute-done.8 = bf16[344,128]{1,0:T(8,128)(2,1)S(1)} collective-permute-done((bf16[344,128]{1,0:T(8,128)(2,1)S(1)}, bf16[344,128]{1,0:T(8,128)(2,1)S(1)}, u32[]{:S(2)}, u32[]{:S(2)}) %collective-permute-start.8) | collective-permute-done | bytes 88096 | tf_op jit(solution)/shard_map/ppermute | solution.py:50
  81.0 3.4 %collective-permute-start.9 = (bf16[344,128]{1,0:T(8,128)(2,1)S(1)}, bf16[344,128]{1,0:T(8,128)(2,1)S(1)}, u32[]{:S(2)}, u32[]{:S(2)}) collective-permute-start(bf16[344,128]{1,0:T(8,128)(2,1)S(1)} %add_convert_fusion.2), channel_id=1, source_target_pairs={{0,16},{1,65},{2,18},{3,67},{4,20},{5,69},{6,22},{7,71},{8,24},{9,... | collective-permute-start | bytes 264200 | tf_op jit(solution)/shard_map/ppermute | solution.py:50
  84.3 1.9 %collective-permute-done.9 = bf16[344,128]{1,0:T(8,128)(2,1)S(1)} collective-permute-done((bf16[344,128]{1,0:T(8,128)(2,1)S(1)}, bf16[344,128]{1,0:T(8,128)(2,1)S(1)}, u32[]{:S(2)}, u32[]{:S(2)}) %collective-permute-start.9) | collective-permute-done | bytes 88096 | tf_op jit(solution)/shard_map/ppermute | solution.py:50
  86.3 9.3 %collective-permute-start.10 = (bf16[344,128]{1,0:T(8,128)(2,1)S(1)}, bf16[344,128]{1,0:T(8,128)(2,1)S(1)}, u32[]{:S(2)}, u32[]{:S(2)}) collective-permute-start(bf16[344,128]{1,0:T(8,128)(2,1)S(1)} %add_convert_fusion.1), channel_id=1, source_target_pairs={{0,64},{1,129},{2,66},{3,131},{4,68},{5,133},{6,70},{7,135},{8,72}... | collective-permute-start | bytes 264200 | tf_op jit(solution)/shard_map/ppermute | solution.py:50
  95.6 2.1 %collective-permute-done.10 = bf16[344,128]{1,0:T(8,128)(2,1)S(1)} collective-permute-done((bf16[344,128]{1,0:T(8,128)(2,1)S(1)}, bf16[344,128]{1,0:T(8,128)(2,1)S(1)}, u32[]{:S(2)}, u32[]{:S(2)}) %collective-permute-start.10) | collective-permute-done | bytes 88096 | tf_op jit(solution)/shard_map/ppermute | solution.py:50
  97.7 1.6 %collective-permute-start.11 = (bf16[344,128]{1,0:T(8,128)(2,1)S(1)}, bf16[344,128]{1,0:T(8,128)(2,1)S(1)}, u32[]{:S(2)}, u32[]{:S(2)}) collective-permute-start(bf16[344,128]{1,0:T(8,128)(2,1)S(1)} %add_convert_fusion), channel_id=1, source_target_pairs={{0,128},{1,5},{2,130},{3,7},{4,132},{5,1},{6,134},{7,3},{8,136},{9... | collective-permute-start | bytes 264200 | tf_op jit(solution)/shard_map/ppermute | solution.py:50
  99.3 3.3 %collective-permute-done.11 = bf16[344,128]{1,0:T(8,128)(2,1)S(1)} collective-permute-done((bf16[344,128]{1,0:T(8,128)(2,1)S(1)}, bf16[344,128]{1,0:T(8,128)(2,1)S(1)}, u32[]{:S(2)}, u32[]{:S(2)}) %collective-permute-start.11) | collective-permute-done | bytes 88096 | tf_op jit(solution)/shard_map/ppermute | solution.py:50
  103.0 3.1 %collective-permute-done.12 = bf16[344,128]{1,0:T(8,128)(2,1)S(1)} collective-permute-done((bf16[344,128]{1,0:T(8,128)(2,1)S(1)}, bf16[344,128]{1,0:T(8,128)(2,1)S(1)}, u32[]{:S(2)}, u32[]{:S(2)}) %collective-permute-start.12) | collective-permute-done | bytes 88096 | tf_op jit(solution)/shard_map/ppermute | solution.py:55
  107.1 4.3 %collective-permute-done.13 = bf16[688,128]{1,0:T(8,128)(2,1)S(1)} collective-permute-done((bf16[688,128]{1,0:T(8,128)(2,1)S(1)}, bf16[688,128]{1,0:T(8,128)(2,1)S(1)}, u32[]{:S(2)}, u32[]{:S(2)}) %collective-permute-start.13) | collective-permute-done | bytes 176160 | tf_op jit(solution)/shard_map/ppermute | solution.py:55
  113.8 6.3 %gather_fusion.1 = bf16[2000,128]{1,0:T(8,128)(2,1)S(1)} fusion(bf16[3584,128]{1,0:T(8,128)(2,1)S(1)} %slice_dynamic-update-slice_fusion.2, s32[2048]{0:T(1024)S(1)} %pad_clamp_fusion), kind=kCustom, calls=%fused_computation.1 | custom fusion | bytes 1032000 | tf_op jit(solution)/shard_map/jit(_take)/gather | solution.py:109
  120.6 9.3 %collective-permute-start.15 = (bf16[2752,128]{1,0:T(8,128)(2,1)S(1)}, bf16[2752,128]{1,0:T(8,128)(2,1)S(1)}, u32[]{:S(2)}, u32[]{:S(2)}) collective-permute-start(bf16[2752,128]{1,0:T(8,128)(2,1)S(1)} %maximum_select_fusion.1), channel_id=1, source_target_pairs={{0,1},{1,0},{2,3},{3,2},{4,5},{5,4},{6,7},{7,6},{8,9},{9,8},{10,11... | collective-permute-start | bytes 2113544 | tf_op jit(solution)/shard_map/ppermute | solution.py:55
  129.8 3.2 %fusion.7 = f32[2,8,8,8,128]{4,0,3,2,1:T(2,128)S(1)} fusion(bf16[3,3,3,128,128]{4,3,2,1,0:T(8,128)(2,1)S(1)} %bitcast.75, bf16[2,10,10,10,128]{4,3,2,1,0:T(8,128)(2,1)S(1)} %reshape.322), kind=kOutput, calls=%fused_computation.25 | convolution fusion | flops 905969664 | bytes 1921024 | tf_op jit(solution)/shard_map/conv_general_dilated | solution.py:129
  134.3 1.3 slice.66
  (92 shorter events, 22.0 us)
Async XLA Ops:
  0.6 27.2 %copy-start = (bf16[27,128,128]{2,1,0:T(8,128)(2,1)S(1)}, bf16[27,128,128]{2,1,0:T(8,128)(2,1)}, u32[]{:S(2)}) copy-start(bf16[27,128,128]{2,1,0:T(8,128)(2,1)} %param.19) | copy-start | bytes 2654212
  0.6 10.4 %copy-start.6 = (bf16[1,2,64,256]{3,2,1,0:T(8,128)(2,1)S(1)}, bf16[1,2,64,256]{3,2,1,0:T(8,128)(2,1)}, u32[]{:S(2)}) copy-start(bf16[1,2,64,256]{3,2,1,0:T(8,128)(2,1)} %param.21) | copy-start | bytes 196612
  0.7 10.5 %copy-start.2 = (bf16[8,128,256]{2,1,0:T(8,128)(2,1)S(1)}, bf16[8,128,256]{2,1,0:T(8,128)(2,1)}, u32[]{:S(2)}) copy-start(bf16[8,128,256]{2,1,0:T(8,128)(2,1)} %param.20) | copy-start | bytes 1572868
  4.6 10.6 %collective-permute-start = (bf16[1025,128]{1,0:T(8,128)(2,1)S(1)}, bf16[1025,128]{1,0:T(8,128)(2,1)}, u32[]{:S(2)}, u32[]{:S(2)}) collective-permute-start(bf16[1025,128]{1,0:T(8,128)(2,1)S(1)} %fusion.10), channel_id=1, source_target_pairs={{0,2},{2,4},{4,6},{6,8},{8,10},{10,12},{12,14},{14,16},{16,18},{18... | collective-permute-start | bytes 787208 | tf_op jit(solution)/shard_map/ppermute | solution.py:11
  9.2 8.9 %collective-permute-start.1 = (bf16[1025,128]{1,0:T(8,128)(2,1)S(1)}, bf16[1025,128]{1,0:T(8,128)(2,1)}, u32[]{:S(2)}, u32[]{:S(2)}) collective-permute-start(bf16[1025,128]{1,0:T(8,128)(2,1)S(1)} %fusion.10), channel_id=1, source_target_pairs={{2,0},{4,2},{6,4},{8,6},{10,8},{12,10},{14,12},{16,14},{18,16},{20... | collective-permute-start | bytes 787208 | tf_op jit(solution)/shard_map/ppermute | solution.py:11
  11.2 1.3 copy-start.4
  12.5 2.7 %copy-start.9 = (s32[1,2,27]{2,1,0:T(2,128)S(1)}, s32[1,2,27]{2,1,0:T(2,128)}, u32[]{:S(2)}) copy-start(s32[1,2,27]{2,1,0:T(2,128)} %param.17) | copy-start | bytes 652
  12.5 6.5 %copy-start.7 = (pred[1000,27]{0,1:T(8,128)(4,1)S(1)}, pred[1000,27]{0,1:T(8,128)(4,1)}, u32[]{:S(2)}) copy-start(pred[1000,27]{0,1:T(8,128)(4,1)} %constant.136) | copy-start | bytes 81004
  12.5 6.7 %copy-start.8 = (s32[1000]{0:T(1024)S(1)}, s32[1000]{0:T(1024)}, u32[]{:S(2)}) copy-start(s32[1000]{0:T(1024)} %constant.137) | copy-start | bytes 12004
  32.4 11.5 %collective-permute-start.2 = (bf16[1025,128]{1,0:T(8,128)(2,1)}, bf16[1025,128]{1,0:T(8,128)(2,1)}, u32[]{:S(2)}, u32[]{:S(2)}) collective-permute-start(bf16[1025,128]{1,0:T(8,128)(2,1)} %fusion.11), channel_id=1, source_target_pairs={{0,2},{2,4},{4,6},{6,8},{8,10},{10,12},{12,14},{14,16},{16,18},{18... | collective-permute-start | bytes 787208 | tf_op jit(solution)/shard_map/ppermute | solution.py:11
  35.5 8.4 %collective-permute-start.3 = (bf16[1025,128]{1,0:T(8,128)(2,1)}, bf16[1025,128]{1,0:T(8,128)(2,1)}, u32[]{:S(2)}, u32[]{:S(2)}) collective-permute-start(bf16[1025,128]{1,0:T(8,128)(2,1)} %fusion.11), channel_id=1, source_target_pairs={{2,0},{4,2},{6,4},{8,6},{10,8},{12,10},{14,12},{16,14},{18,16},{20... | collective-permute-start | bytes 787208 | tf_op jit(solution)/shard_map/ppermute | solution.py:11
  42.7 0.8 copy-start.5
  45.6 1.6 %copy-start.1 = (f32[5504,128]{1,0:T(8,128)}, f32[5504,128]{1,0:T(8,128)S(1)}, u32[]{:S(2)}) copy-start(f32[5504,128]{1,0:T(8,128)S(1)} %pad_maximum_fusion) | copy-start | bytes 8454148
  47.2 4.4 %collective-permute-start.4 = (bf16[2752,128]{1,0:T(8,128)(2,1)S(1)}, bf16[2752,128]{1,0:T(8,128)(2,1)S(1)}, u32[]{:S(2)}, u32[]{:S(2)}) collective-permute-start(bf16[2752,128]{1,0:T(8,128)(2,1)S(1)} %fusion.3), channel_id=1, source_target_pairs={{0,1},{1,0},{2,3},{3,2},{4,5},{5,4},{6,7},{7,6},{8,9},{9,8},{10,11... | collective-permute-start | bytes 2113544 | tf_op jit(solution)/shard_map/ppermute | solution.py:47
  53.2 9.0 %collective-permute-start.5 = (bf16[1376,128]{1,0:T(8,128)(2,1)S(1)}, bf16[1376,128]{1,0:T(8,128)(2,1)}, u32[]{:S(2)}, u32[]{:S(2)}) collective-permute-start(bf16[1376,128]{1,0:T(8,128)(2,1)S(1)} %fusion.9), channel_id=1, source_target_pairs={{0,2},{1,9},{2,0},{3,11},{4,6},{5,13},{6,4},{7,15},{8,10},{9,1},{1... | collective-permute-start | bytes 1056776 | tf_op jit(solution)/shard_map/ppermute | solution.py:47
  63.2 9.2 %collective-permute-start.6 = (bf16[688,128]{1,0:T(8,128)(2,1)S(1)}, bf16[688,128]{1,0:T(8,128)(2,1)S(1)}, u32[]{:S(2)}, u32[]{:S(2)}) collective-permute-start(bf16[688,128]{1,0:T(8,128)(2,1)S(1)} %fusion.15), channel_id=1, source_target_pairs={{0,8},{1,33},{2,10},{3,35},{4,12},{5,37},{6,14},{7,39},{8,0},{9,41... | collective-permute-start | bytes 528392 | tf_op jit(solution)/shard_map/ppermute | solution.py:47
  72.5 3.4 %collective-permute-start.7 = (bf16[344,128]{1,0:T(8,128)(2,1)S(1)}, bf16[344,128]{1,0:T(8,128)(2,1)S(1)}, u32[]{:S(2)}, u32[]{:S(2)}) collective-permute-start(bf16[344,128]{1,0:T(8,128)(2,1)S(1)} %fusion.20), channel_id=1, source_target_pairs={{0,32},{1,3},{2,34},{3,1},{4,36},{5,7},{6,38},{7,5},{8,40},{9,11},... | collective-permute-start | bytes 264200 | tf_op jit(solution)/shard_map/ppermute | solution.py:47
  72.6 33.6 %copy-start.3 = (bf16[8,128,256]{2,1,0:T(8,128)(2,1)S(1)}, bf16[8,128,256]{2,1,0:T(8,128)(2,1)}, u32[]{:S(2)}) copy-start(bf16[8,128,256]{2,1,0:T(8,128)(2,1)} %param.20) | copy-start | bytes 1572868
  76.0 4.9 %collective-permute-start.8 = (bf16[344,128]{1,0:T(8,128)(2,1)S(1)}, bf16[344,128]{1,0:T(8,128)(2,1)S(1)}, u32[]{:S(2)}, u32[]{:S(2)}) collective-permute-start(bf16[344,128]{1,0:T(8,128)(2,1)S(1)} %fusion.16), channel_id=1, source_target_pairs={{0,4},{1,17},{2,6},{3,19},{4,0},{5,21},{6,2},{7,23},{8,12},{9,25},... | collective-permute-start | bytes 264200 | tf_op jit(solution)/shard_map/ppermute | solution.py:50
  81.0 5.3 %collective-permute-start.9 = (bf16[344,128]{1,0:T(8,128)(2,1)S(1)}, bf16[344,128]{1,0:T(8,128)(2,1)S(1)}, u32[]{:S(2)}, u32[]{:S(2)}) collective-permute-start(bf16[344,128]{1,0:T(8,128)(2,1)S(1)} %add_convert_fusion.2), channel_id=1, source_target_pairs={{0,16},{1,65},{2,18},{3,67},{4,20},{5,69},{6,22},{7,71},{8,24},{9,... | collective-permute-start | bytes 264200 | tf_op jit(solution)/shard_map/ppermute | solution.py:50
  86.3 11.4 %collective-permute-start.10 = (bf16[344,128]{1,0:T(8,128)(2,1)S(1)}, bf16[344,128]{1,0:T(8,128)(2,1)S(1)}, u32[]{:S(2)}, u32[]{:S(2)}) collective-permute-start(bf16[344,128]{1,0:T(8,128)(2,1)S(1)} %add_convert_fusion.1), channel_id=1, source_target_pairs={{0,64},{1,129},{2,66},{3,131},{4,68},{5,133},{6,70},{7,135},{8,72}... | collective-permute-start | bytes 264200 | tf_op jit(solution)/shard_map/ppermute | solution.py:50
  97.7 4.9 %collective-permute-start.11 = (bf16[344,128]{1,0:T(8,128)(2,1)S(1)}, bf16[344,128]{1,0:T(8,128)(2,1)S(1)}, u32[]{:S(2)}, u32[]{:S(2)}) collective-permute-start(bf16[344,128]{1,0:T(8,128)(2,1)S(1)} %add_convert_fusion), channel_id=1, source_target_pairs={{0,128},{1,5},{2,130},{3,7},{4,132},{5,1},{6,134},{7,3},{8,136},{9... | collective-permute-start | bytes 264200 | tf_op jit(solution)/shard_map/ppermute | solution.py:50
  102.7 3.4 %collective-permute-start.12 = (bf16[344,128]{1,0:T(8,128)(2,1)S(1)}, bf16[344,128]{1,0:T(8,128)(2,1)S(1)}, u32[]{:S(2)}, u32[]{:S(2)}) collective-permute-start(bf16[344,128]{1,0:T(8,128)(2,1)S(1)} %multiply_convert_fusion.2), channel_id=1, source_target_pairs={{0,32},{1,3},{2,34},{3,1},{4,36},{5,7},{6,38},{7,5},{8,40},{9,11},... | collective-permute-start | bytes 264200 | tf_op jit(solution)/shard_map/ppermute | solution.py:55
  106.2 5.3 %collective-permute-start.13 = (bf16[688,128]{1,0:T(8,128)(2,1)S(1)}, bf16[688,128]{1,0:T(8,128)(2,1)S(1)}, u32[]{:S(2)}, u32[]{:S(2)}) collective-permute-start(bf16[688,128]{1,0:T(8,128)(2,1)S(1)} %maximum_select_fusion.3), channel_id=1, source_target_pairs={{0,8},{1,33},{2,10},{3,35},{4,12},{5,37},{6,14},{7,39},{8,0},{9,41... | collective-permute-start | bytes 528392 | tf_op jit(solution)/shard_map/ppermute | solution.py:55
  111.5 8.8 %collective-permute-start.14 = (bf16[1376,128]{1,0:T(8,128)(2,1)S(1)}, bf16[1376,128]{1,0:T(8,128)(2,1)S(1)}, u32[]{:S(2)}, u32[]{:S(2)}) collective-permute-start(bf16[1376,128]{1,0:T(8,128)(2,1)S(1)} %maximum_select_fusion.2), channel_id=1, source_target_pairs={{0,2},{1,9},{2,0},{3,11},{4,6},{5,13},{6,4},{7,15},{8,10},{9,1},{1... | collective-permute-start | bytes 1056776 | tf_op jit(solution)/shard_map/ppermute | solution.py:55
  120.6 13.4 %collective-permute-start.15 = (bf16[2752,128]{1,0:T(8,128)(2,1)S(1)}, bf16[2752,128]{1,0:T(8,128)(2,1)S(1)}, u32[]{:S(2)}, u32[]{:S(2)}) collective-permute-start(bf16[2752,128]{1,0:T(8,128)(2,1)S(1)} %maximum_select_fusion.1), channel_id=1, source_target_pairs={{0,1},{1,0},{2,3},{3,2},{4,5},{5,4},{6,7},{7,6},{8,9},{9,8},{10,11... | collective-permute-start | bytes 2113544 | tf_op jit(solution)/shard_map/ppermute | solution.py:55
